TPU v7x, 768 devices: a whole 4x8x12 slice. The times are simulated.
768 devices in a mesh: energy: 48 (over z_hi, y, core), layer: 16 (over z_lo, x).
Axes of the slice: x: 4, y: 8, z: 12 (z_hi: 3, z_lo: 4; z = z_hi * 4 + z_lo), core: 2. Of those that a mesh axis runs over, the one named last changes fastest.
Arguments:
- retarded: bfloat16 [48, 48, 3, 256, 256], P('energy', 'layer'), may hold values from -0.375 to 0.375
- scatter_in: bfloat16 [48, 48, 256, 256], P('energy', 'layer'), may hold values from -6 to 6
- screen: bfloat16 [48, 48, 256, 256], P('energy', 'layer'), may hold values from -0.875 to 0.875
Outputs:
- lesser: bfloat16 [48, 48, 256, 256], P('energy', 'layer')
- self_energy: bfloat16 [48, 48, 256, 256], P('energy', 'layer')
All inputs are finite; a program needn't handle non-finite values.
Results may differ from a plain program's by a relative error of at most 0.0095.
Values may be sent and summed in bfloat16 or wider, within the bound.
No kernel may reach another device: no remote copies, remote signals or barrier semaphores. Data moves between devices by JAX's collectives and lax.ppermute only.
A program may use at most 32 MiB of HBM per device.

v0:
```python
import jax
import jax.numpy as jnp
from jax import lax
from jax.sharding import PartitionSpec as P

ITERS = 2


def padded_2(cells, sides, width):
    for axis, dim in sides:
        count = lax.axis_size(axis)
        ends = count - 1
        head = lax.slice_in_dim(cells, 0, width, axis=dim)
        tail = lax.slice_in_dim(cells, cells.shape[dim] - width, cells.shape[dim], axis=dim)
        cells = jnp.concatenate(
            [
                lax.ppermute(tail, axis, [(i, (i + 1) % count) for i in range(ends)]),
                cells,
                lax.ppermute(head, axis, [((i + 1) % count, i) for i in range(ends)]),
            ],
            axis=dim,
        )
    return cells


def symmetric(matrix):
    matrix = matrix.astype(jnp.float32)
    return 0.5 * (matrix + jnp.swapaxes(matrix, -1, -2))


def energy_convolve(series, kernel):
    energies = series.shape[0]
    width = series.shape[1]
    padded_series = jnp.concatenate(
        [jnp.zeros((energies, width), jnp.float32), series.astype(jnp.float32)], axis=0
    )
    kernel_values = kernel.astype(jnp.float32)
    group_size = 8

    def add_group(group, total):
        for inner in range(group_size):
            lag = group * group_size + inner
            moved = lax.dynamic_slice_in_dim(padded_series, energies - lag, energies, 0)
            weight_row = lax.dynamic_slice_in_dim(kernel_values, lag, 1, 0)
            total = total + moved * weight_row
        return total

    start = jnp.zeros((energies, width), jnp.float32)
    total = lax.fori_loop(0, energies // group_size, add_group, start)
    return total.astype(jnp.bfloat16)


def lesser_blocks(retarded, padded, layers):
    running = None
    for offset in range(3):
        neighbour = padded[:, offset : offset + layers]
        factor = retarded[:, :, offset]
        left_part = jnp.einsum(
            "elab,elbc->elac", factor, neighbour, preferred_element_type=jnp.float32
        ).astype(jnp.bfloat16)
        term_part = jnp.einsum(
            "elac,elbc->elab", left_part, factor, preferred_element_type=jnp.float32
        )
        running = term_part if running is None else running + term_part
    return symmetric(running).astype(jnp.bfloat16)


def shards(retarded, scatter_in, screen):
    energies_local = retarded.shape[0]
    layers = retarded.shape[1]
    orbital_count = retarded.shape[3]
    half_width = orbital_count // 2
    entry_rows = layers * half_width
    base_part = symmetric(scatter_in)
    screened = symmetric(screen).astype(jnp.bfloat16)
    screen_columns = lax.all_to_all(
        screened.reshape(energies_local, entry_rows, 2 * orbital_count),
        "energy",
        split_axis=1,
        concat_axis=0,
        tiled=True,
    )
    energies = screen_columns.shape[0]
    screen_flat = screen_columns.reshape(energies, -1)
    correction = jnp.zeros(base_part.shape, jnp.float32)
    lesser = None
    self_energy = None
    for iteration in range(ITERS):
        coupling = (base_part + correction).astype(jnp.bfloat16)
        padded = padded_2(coupling, (("layer", 1),), 1)
        lesser = lesser_blocks(retarded, padded, layers)
        columns = lax.all_to_all(
            lesser.reshape(energies_local, entry_rows, 2 * orbital_count),
            "energy",
            split_axis=1,
            concat_axis=0,
            tiled=True,
        )
        self_columns = energy_convolve(columns.reshape(energies, -1), screen_flat).reshape(
            columns.shape
        )
        returned = lax.all_to_all(self_columns, "energy", split_axis=0, concat_axis=1, tiled=True)
        self_energy = returned.reshape(energies_local, layers, orbital_count, orbital_count)
        correction = self_energy.astype(jnp.float32)
    return (lesser, self_energy)


def solution(mesh):
    placed = (
        P("energy", "layer", None, None, None),
        P("energy", "layer", None, None),
        P("energy", "layer", None, None),
    )
    return jax.shard_map(
        shards,
        mesh=mesh,
        in_specs=placed,
        out_specs=(P("energy", "layer", None, None), P("energy", "layer", None, None)),
        check_vma=False,
    )
```

profile of v0, /device:TPU:2, one launch (start us, length us, event | category | flops | bytes accessed | tf_op | source)
XLA Modules:
  0.0 233.2 jit_solution(15291644817943761549)
XLA Ops:
  0.6 1.2 copy.46
  2.7 3.4 %collective-permute-start = (bf16[1,1,256,256]{2,3,1,0:T(8,128)(2,1)S(1)}, bf16[1,1,256,256]{2,3,1,0:T(8,128)(2,1)S(1)}, u32[]{:S(2)}, u32[]{:S(2)}) collective-permute-start(bf16[1,1,256,256]{2,3,1,0:T(8,128)(2,1)S(1)} %get-tuple-element.375), channel_id=1, source_target_pairs={{0,1},{1,2},{2,3},{3,4},{4,5},{5,6},{6,7},{7,8},{8,9},{9,10},{10,1... | collective-permute-start | bytes 393224 | tf_op jit(solution)/shard_map/ppermute | solution.py:17
  7.3 3.1 %reduce.7 = bf16[384,512]{1,0:T(8,128)(2,1)S(1)} reduce(bf16[384,1,512]{2,1,0:T(2,128)(2,1)S(1)} %bitcast.150, bf16[]{:T(256)} %broadcast.35), dimensions={1}, to_apply=%bitcast.109.reduce_sub_computation | reduce | bytes 786434
  11.3 19.9 %all-to-all-start.1 = ((bf16[48,2,2048]{2,1,0:T(2,128)(2,1)}), bf16[48,2,2048]{2,1,0:T(2,128)(2,1)S(1)}, u32[]{:S(2)}, u32[]{:S(2)}) async-start(bf16[48,2,2048]{2,1,0:T(2,128)(2,1)} %reshape.173), calls=%async_computation.1 | async-start | bytes 786432 | tf_op jit(solution)/shard_map/all_to_all | solution.py:76
  31.2 2.4 %collective-permute-start.1 = (bf16[1,1,256,256]{2,3,1,0:T(8,128)(2,1)}, bf16[1,1,256,256]{2,3,1,0:T(8,128)(2,1)}, u32[]{:S(2)}, u32[]{:S(2)}) collective-permute-start(bf16[1,1,256,256]{2,3,1,0:T(8,128)(2,1)} %get-tuple-element.374), channel_id=1, source_target_pairs={{1,0},{2,1},{3,2},{4,3},{5,4},{6,5},{7,6},{8,7},{9,8},{10,9},{11,1... | collective-permute-start | bytes 393224 | tf_op jit(solution)/shard_map/ppermute | solution.py:19
  34.8 4.2 %collective-permute-done.1 = bf16[1,1,256,256]{2,3,1,0:T(8,128)(2,1)} collective-permute-done((bf16[1,1,256,256]{2,3,1,0:T(8,128)(2,1)}, bf16[1,1,256,256]{2,3,1,0:T(8,128)(2,1)}, u32[]{:S(2)}, u32[]{:S(2)}) %collective-permute-start.1) | collective-permute-done | bytes 131104 | tf_op jit(solution)/shard_map/ppermute | solution.py:19
  39.0 1.5 convolution_add_fusion.2
  41.2 3.0 %reduce.6 = bf16[384,512]{1,0:T(8,128)(2,1)S(1)} reduce(bf16[384,1,512]{2,1,0:T(2,128)(2,1)S(1)} %bitcast.151, bf16[]{:T(256)} %broadcast.35), dimensions={1}, to_apply=%bitcast.107.reduce_sub_computation | reduce | bytes 786434
  45.1 3.8 %all-to-all-done.1 = bf16[48,2,2048]{2,1,0:T(2,128)(2,1)S(1)} async-done(((bf16[48,2,2048]{2,1,0:T(2,128)(2,1)}), bf16[48,2,2048]{2,1,0:T(2,128)(2,1)S(1)}, u32[]{:S(2)}, u32[]{:S(2)}) %all-to-all-start.1) | async-done | bytes 393248 | tf_op jit(solution)/shard_map/all_to_all | solution.py:76
  48.9 9.9 %all-to-all-start = ((bf16[48,2,2048]{2,1,0:T(2,128)(2,1)}), bf16[48,2,2048]{2,1,0:T(2,128)(2,1)}, u32[]{:S(2)}, u32[]{:S(2)}) async-start(bf16[48,2,2048]{2,1,0:T(2,128)(2,1)} %reshape.171), calls=%async_computation | async-start | bytes 786432 | tf_op jit(solution)/shard_map/all_to_all | solution.py:92
  59.2 2.3 convert_reduce_fusion
  61.5 1.0 reshape.163
  62.5 16.1 %all-to-all-done = bf16[48,2,2048]{2,1,0:T(2,128)(2,1)} async-done(((bf16[48,2,2048]{2,1,0:T(2,128)(2,1)}), bf16[48,2,2048]{2,1,0:T(2,128)(2,1)}, u32[]{:S(2)}, u32[]{:S(2)}) %all-to-all-start) | async-done | bytes 393248 | tf_op jit(solution)/shard_map/all_to_all | solution.py:92
  78.6 2.7 %reshape.172 = bf16[384,1,512]{2,1,0:T(2,128)(2,1)S(1)} reshape(bf16[48,2,2048]{2,1,0:T(2,128)(2,1)} %all-to-all-done) | data formatting | bytes 786432
  81.3 2.3 bitcast_reduce_fusion.1
  83.6 0.9 convert_element_type.92
  84.6 1.1 pad_convert_fusion.1
  85.7 24.6 %while.34 = (s32[]{:T(128)}, f32[48,4096]{1,0:T(8,128)S(1)}, f32[96,4096]{1,0:T(8,128)S(1)}, f32[48,4096]{1,0:T(8,128)}, s32[]{:T(128)}, /*index=5*/s32[]{:T(128...) while((s32[]{:T(128)}, f32[48,4096]{1,0:T(8,128)S(1)}, ...), condition=%wide.region_1.0_spmd.clone, body=%wide.region_0.0_spmd.clone.sunk | while | flops 3342403 | bytes 8258543 | solution.py:49
  85.7 2.2 constant_dynamic-slice_fusion.18
  88.0 1.7 fusion.84
  89.8 2.2 constant_dynamic-slice_fusion.18
  92.0 1.7 fusion.84
  93.8 2.2 constant_dynamic-slice_fusion.18
  96.1 1.7 fusion.84
  97.9 2.5 %constant_dynamic-slice_fusion.18 = (f32[1,4096]{1,0:T(1,128)S(1)}, f32[1,4096]{1,0:T(1,128)}, f32[1,4096]{1,0:T(1,128)}, f32[1,4096]{1,0:T(1,128)}, f32[1,4096]...) fusion(f32[48,4096]{1,0:T(8,128)} %get-tuple-element.505, s32[]{:T(128)S(6)} %select_n.424, ...), kind=kLoop, calls=%fused_computation.15.clone.1 | loop fusion | bytes 262176 | tf_op jit(solution)/shard_map/while/body/eval_jaxpr/dynamic_slice | solution.py:44
  100.4 1.7 fusion.84
  102.2 2.2 constant_dynamic-slice_fusion.18
  104.4 1.7 fusion.84
  106.2 2.2 constant_dynamic-slice_fusion.18
  108.5 1.7 fusion.84
  110.4 28.0 %all_to_all.20 = bf16[48,8,512]{2,1,0:T(8,128)(2,1)S(1)} all-to-all(bf16[48,8,512]{2,1,0:T(8,128)(2,1)S(1)} %bitcast.169), channel_id=1, replica_groups=mesh['energy'=48,'layer'=16] {'energy'}, dimensions={0} | all-to-all | bytes 786432 | tf_op jit(solution)/shard_map/all_to_all | solution.py:102
  138.6 1.2 copy.59
  139.7 1.3 add_convert_fusion
  141.0 3.1 %collective-permute-start.2 = (bf16[1,1,256,256]{2,3,1,0:T(8,128)(2,1)S(1)}, bf16[1,1,256,256]{2,3,1,0:T(8,128)(2,1)S(1)}, u32[]{:S(2)}, u32[]{:S(2)}) collective-permute-start(bf16[1,1,256,256]{2,3,1,0:T(8,128)(2,1)S(1)} %get-tuple-element.373), channel_id=1, source_target_pairs={{0,1},{1,2},{2,3},{3,4},{4,5},{5,6},{6,7},{7,8},{8,9},{9,10},{10,1... | collective-permute-start | bytes 393224 | tf_op jit(solution)/shard_map/ppermute | solution.py:17
  144.1 3.0 %collective-permute-start.3 = (bf16[1,1,256,256]{2,3,1,0:T(8,128)(2,1)S(1)}, bf16[1,1,256,256]{2,3,1,0:T(8,128)(2,1)S(1)}, u32[]{:S(2)}, u32[]{:S(2)}) collective-permute-start(bf16[1,1,256,256]{2,3,1,0:T(8,128)(2,1)S(1)} %get-tuple-element.372), channel_id=1, source_target_pairs={{1,0},{2,1},{3,2},{4,3},{5,4},{6,5},{7,6},{8,7},{9,8},{10,9},{11,1... | collective-permute-start | bytes 393224 | tf_op jit(solution)/shard_map/ppermute | solution.py:19
  149.0 5.0 %collective-permute-done.3 = bf16[1,1,256,256]{2,3,1,0:T(8,128)(2,1)S(1)} collective-permute-done((bf16[1,1,256,256]{2,3,1,0:T(8,128)(2,1)S(1)}, bf16[1,1,256,256]{2,3,1,0:T(8,128)(2,1)S(1)}, u32[]{:S(2)}, u32[]{:S(2)}) %collective-permute-start.3) | collective-permute-done | bytes 131104 | tf_op jit(solution)/shard_map/ppermute | solution.py:19
  155.3 3.0 %reduce.8 = bf16[384,512]{1,0:T(8,128)(2,1)S(1)} reduce(bf16[384,1,512]{2,1,0:T(2,128)(2,1)S(1)} %bitcast.152, bf16[]{:T(256)} %broadcast.35), dimensions={1}, to_apply=%bitcast.111.reduce_sub_computation | reduce | bytes 786434
  159.2 7.0 %all-to-all-start.3 = ((bf16[48,2,2048]{2,1,0:T(2,128)(2,1)}), bf16[48,2,2048]{2,1,0:T(2,128)(2,1)S(1)}, u32[]{:S(2)}, u32[]{:S(2)}) async-start(bf16[48,2,2048]{2,1,0:T(2,128)(2,1)} %reshape.175), calls=%async_computation.3 | async-start | bytes 786432 | tf_op jit(solution)/shard_map/all_to_all | solution.py:92
  166.2 18.2 %all-to-all-done.3 = bf16[48,2,2048]{2,1,0:T(2,128)(2,1)S(1)} async-done(((bf16[48,2,2048]{2,1,0:T(2,128)(2,1)}), bf16[48,2,2048]{2,1,0:T(2,128)(2,1)S(1)}, u32[]{:S(2)}, u32[]{:S(2)}) %all-to-all-start.3) | async-done | bytes 393248 | tf_op jit(solution)/shard_map/all_to_all | solution.py:92
  184.8 2.3 bitcast_reduce_fusion
  187.4 16.5 %while.35 = (s32[]{:T(128)}, f32[48,4096]{1,0:T(8,128)S(1)}, f32[96,4096]{1,0:T(8,128)S(1)}, f32[48,4096]{1,0:T(8,128)}, s32[]{:T(128)}, /*index=5*/s32[]{:T(128...) while((s32[]{:T(128)}, f32[48,4096]{1,0:T(8,128)S(1)}, ...), condition=%wide.region_3.0_spmd.clone, body=%wide.region_2.0_spmd.clone.sunk | while | flops 3342403 | bytes 8258543 | solution.py:49
  187.5 1.6 constant_dynamic-slice_fusion.19
  190.2 1.6 constant_dynamic-slice_fusion.19
  192.9 1.6 constant_dynamic-slice_fusion.19
  195.6 1.9 constant_dynamic-slice_fusion.19
  198.6 1.6 constant_dynamic-slice_fusion.19
  201.3 1.6 constant_dynamic-slice_fusion.19
  204.1 28.2 %all_to_all.21 = bf16[48,8,512]{2,1,0:T(8,128)(2,1)S(1)} all-to-all(bf16[48,8,512]{2,1,0:T(8,128)(2,1)S(1)} %bitcast.170), channel_id=1, replica_groups=mesh['energy'=48,'layer'=16] {'energy'}, dimensions={0} | all-to-all | bytes 786432 | tf_op jit(solution)/shard_map/all_to_all | solution.py:102
  (58 shorter events, 17.7 us)
Async XLA Ops:
  0.6 1.2 copy-start.3
  1.9 4.4 %copy-start.1 = (f32[1,3,256,256]{2,3,1,0:T(8,128)}, f32[1,3,256,256]{2,3,1,0:T(8,128)S(1)}, u32[]{:S(2)}) copy-start(f32[1,3,256,256]{2,3,1,0:T(8,128)S(1)} %copy.46) | copy-start | bytes 2359300
  1.9 4.2 %copy-start.6 = (bf16[1,3,256,256]{3,2,1,0:T(8,128)(2,1)S(1)}, bf16[1,3,256,256]{3,2,1,0:T(8,128)(2,1)}, u32[]{:S(2)}) copy-start(bf16[1,3,256,256]{3,2,1,0:T(8,128)(2,1)} %param.9) | copy-start | bytes 1179652
  2.7 31.0 %collective-permute-start = (bf16[1,1,256,256]{2,3,1,0:T(8,128)(2,1)S(1)}, bf16[1,1,256,256]{2,3,1,0:T(8,128)(2,1)S(1)}, u32[]{:S(2)}, u32[]{:S(2)}) collective-permute-start(bf16[1,1,256,256]{2,3,1,0:T(8,128)(2,1)S(1)} %get-tuple-element.375), channel_id=1, source_target_pairs={{0,1},{1,2},{2,3},{3,4},{4,5},{5,6},{6,7},{7,8},{8,9},{9,10},{10,1... | collective-permute-start | bytes 393224 | tf_op jit(solution)/shard_map/ppermute | solution.py:17
  7.3 26.4 %copy-start = (bf16[1,3,3,256,256]{4,3,2,1,0:T(8,128)(2,1)S(1)}, bf16[1,3,3,256,256]{4,3,2,1,0:T(8,128)(2,1)}, u32[]{:S(2)}) copy-start(bf16[1,3,3,256,256]{4,3,2,1,0:T(8,128)(2,1)} %param.7) | copy-start | bytes 3538948
  11.3 37.6 %all-to-all-start.1 = ((bf16[48,2,2048]{2,1,0:T(2,128)(2,1)}), bf16[48,2,2048]{2,1,0:T(2,128)(2,1)S(1)}, u32[]{:S(2)}, u32[]{:S(2)}) async-start(bf16[48,2,2048]{2,1,0:T(2,128)(2,1)} %reshape.173), calls=%async_computation.1 | async-start | bytes 786432 | tf_op jit(solution)/shard_map/all_to_all | solution.py:76
  31.2 7.8 %collective-permute-start.1 = (bf16[1,1,256,256]{2,3,1,0:T(8,128)(2,1)}, bf16[1,1,256,256]{2,3,1,0:T(8,128)(2,1)}, u32[]{:S(2)}, u32[]{:S(2)}) collective-permute-start(bf16[1,1,256,256]{2,3,1,0:T(8,128)(2,1)} %get-tuple-element.374), channel_id=1, source_target_pairs={{1,0},{2,1},{3,2},{4,3},{5,4},{6,5},{7,6},{8,7},{9,8},{10,9},{11,1... | collective-permute-start | bytes 393224 | tf_op jit(solution)/shard_map/ppermute | solution.py:19
  48.9 29.7 %all-to-all-start = ((bf16[48,2,2048]{2,1,0:T(2,128)(2,1)}), bf16[48,2,2048]{2,1,0:T(2,128)(2,1)}, u32[]{:S(2)}, u32[]{:S(2)}) async-start(bf16[48,2,2048]{2,1,0:T(2,128)(2,1)} %reshape.171), calls=%async_computation | async-start | bytes 786432 | tf_op jit(solution)/shard_map/all_to_all | solution.py:92
  138.4 1.3 copy-start.2
  138.4 1.3 copy-start.4
  141.0 6.9 %collective-permute-start.2 = (bf16[1,1,256,256]{2,3,1,0:T(8,128)(2,1)S(1)}, bf16[1,1,256,256]{2,3,1,0:T(8,128)(2,1)S(1)}, u32[]{:S(2)}, u32[]{:S(2)}) collective-permute-start(bf16[1,1,256,256]{2,3,1,0:T(8,128)(2,1)S(1)} %get-tuple-element.373), channel_id=1, source_target_pairs={{0,1},{1,2},{2,3},{3,4},{4,5},{5,6},{6,7},{7,8},{8,9},{9,10},{10,1... | collective-permute-start | bytes 393224 | tf_op jit(solution)/shard_map/ppermute | solution.py:17
  144.1 9.8 %collective-permute-start.3 = (bf16[1,1,256,256]{2,3,1,0:T(8,128)(2,1)S(1)}, bf16[1,1,256,256]{2,3,1,0:T(8,128)(2,1)S(1)}, u32[]{:S(2)}, u32[]{:S(2)}) collective-permute-start(bf16[1,1,256,256]{2,3,1,0:T(8,128)(2,1)S(1)} %get-tuple-element.372), channel_id=1, source_target_pairs={{1,0},{2,1},{3,2},{4,3},{5,4},{6,5},{7,6},{8,7},{9,8},{10,9},{11,1... | collective-permute-start | bytes 393224 | tf_op jit(solution)/shard_map/ppermute | solution.py:19
  155.1 3.2 %copy-start.5 = (bf16[1,3,256,256]{3,2,1,0:T(8,128)(2,1)}, bf16[1,3,256,256]{3,2,1,0:T(8,128)(2,1)S(1)}, u32[]{:S(2)}) copy-start(bf16[1,3,256,256]{3,2,1,0:T(8,128)(2,1)S(1)} %copy.66) | copy-start | bytes 1179652
  159.2 25.2 %all-to-all-start.3 = ((bf16[48,2,2048]{2,1,0:T(2,128)(2,1)}), bf16[48,2,2048]{2,1,0:T(2,128)(2,1)S(1)}, u32[]{:S(2)}, u32[]{:S(2)}) async-start(bf16[48,2,2048]{2,1,0:T(2,128)(2,1)} %reshape.175), calls=%async_computation.3 | async-start | bytes 786432 | tf_op jit(solution)/shard_map/all_to_all | solution.py:92
where the time goes:
time: 235 us; the launch traced here: 233 us
  blocking collectives  56.2 us (24%)
  starting transfers between devices  48.7 us (21%)
  waiting for transfers between devices  47.9 us (20%)
  local copies, waits for them, and re-layouts  43.5 us (19%)
  other arithmetic  30.3 us (13%)
  matrix products  4.21 us (2%)
    all_to_all x2, blocking collectives, shards(): lax.all_to_all(self_columns, 'energy', split_axis=0, concat_axis=1, tiled...  56.2 us
    all_to_all x2, waiting for transfers between devices, shards(): lax.all_to_all(lesser.reshape(energies_local, entry_rows, 2 * orbital_cou...  34.2 us
    dynamic_slice x12, local copies, waits for them, and re-layouts, add_group(): weight_row = lax.dynamic_slice_in_dim(kernel_values, lag, 1, 0)  23.8 us
    all_to_all x1, starting transfers between devices, shards(): lax.all_to_all(screened.reshape(energies_local, entry_rows, 2 * orbital_c...  19.9 us
    all_to_all x2, starting transfers between devices, shards(): lax.all_to_all(lesser.reshape(energies_local, entry_rows, 2 * orbital_cou...  16.9 us
    add x12, other arithmetic, add_group(): total = total + moved * weight_row  16 us
    ppermute x2, waiting for transfers between devices, padded_2(): lax.ppermute(head, axis, [((i + 1) % count, i) for i in range(ends)])  9.16 us
    unnamed x5, other arithmetic  9.06 us
  transfers between devices with their start and end apart: 7, of which 6 were waited for; matrix products, arithmetic and copies ran while one was open for 7% of the time, Pallas kernels for 0%

commit v1 on v0

v1 whole, which is shorter than its diff:
```python
import functools

import jax
import jax.numpy as jnp
from jax import lax
from jax.experimental import pallas as pl
from jax.experimental.pallas import tpu as pltpu
from jax.sharding import PartitionSpec as P

ITERS = 2


def symmetric(matrix):
    matrix = matrix.astype(jnp.float32)
    return 0.5 * (matrix + jnp.swapaxes(matrix, -1, -2))


def halo(cells, axis):
    count = lax.axis_size(axis)
    ends = count - 1
    below = lax.ppermute(cells[-1:], axis, [(i, i + 1) for i in range(ends)])
    above = lax.ppermute(cells[:1], axis, [(i + 1, i) for i in range(ends)])
    return below, above


def lesser_blocks(retarded, coupling, below, above):
    layers = coupling.shape[0]
    neighbours = (
        jnp.concatenate([below, coupling[: layers - 1]], axis=0),
        coupling,
        jnp.concatenate([coupling[1:], above], axis=0),
    )
    running = None
    for offset in range(3):
        factor = retarded[:, offset]
        left_part = jnp.einsum(
            "lab,lbc->lac", factor, neighbours[offset], preferred_element_type=jnp.float32
        ).astype(jnp.bfloat16)
        term_part = jnp.einsum(
            "lac,lbc->lab", left_part, factor, preferred_element_type=jnp.float32
        )
        running = term_part if running is None else running + term_part
    return symmetric(running).astype(jnp.bfloat16)


def _conv_kernel(l_ref, s_ref, o_ref, lf, sf, *, l_idx, s_idx):
    energies = o_ref.shape[0]

    def read(ref, idx, e):
        return ref[e] if idx is None else ref[e, idx]

    for e in range(energies):
        lf[e] = read(l_ref, l_idx, e).astype(jnp.float32)
        sf[e] = read(s_ref, s_idx, e).astype(jnp.float32)
    for e in range(energies):
        acc = lf[e] * sf[0]
        for j in range(1, e + 1):
            acc = acc + lf[e - j] * sf[j]
        o_ref[e] = acc.astype(o_ref.dtype)


def energy_convolve(l_arr, l_idx, s_arr, s_idx):
    energies = l_arr.shape[0]
    block = l_arr.shape[-2:]
    elems = energies * block[0] * block[1]
    kernel = functools.partial(_conv_kernel, l_idx=l_idx, s_idx=s_idx)
    return pl.pallas_call(
        kernel,
        out_shape=jax.ShapeDtypeStruct((energies,) + block, jnp.bfloat16),
        scratch_shapes=[
            pltpu.VMEM((energies,) + block, jnp.float32),
            pltpu.VMEM((energies,) + block, jnp.float32),
        ],
        cost_estimate=pl.CostEstimate(
            flops=elems * (energies + 1), bytes_accessed=elems * 6, transcendentals=0
        ),
    )(l_arr, s_arr)


def shards(retarded, scatter_in, screen):
    energies = lax.axis_size("energy")
    layers = retarded.shape[1]
    orbitals = retarded.shape[-1]
    rows = layers * orbitals // energies
    retarded = retarded[0]
    base_part = symmetric(scatter_in[0])
    screened = symmetric(screen[0]).astype(jnp.bfloat16)

    def to_columns(blocks):
        return blocks.reshape(energies, rows, orbitals)

    def to_blocks(columns):
        return columns.reshape(1, layers, orbitals, orbitals)

    correction = None
    screen_columns = None
    lesser = None
    self_energy = None
    for iteration in range(ITERS):
        if correction is None:
            coupling = base_part.astype(jnp.bfloat16)
        else:
            coupling = (base_part + correction).astype(jnp.bfloat16)
        below, above = halo(coupling, "layer")
        lesser = lesser_blocks(retarded, coupling, below, above)
        if screen_columns is None:
            both = jnp.stack([to_columns(lesser), to_columns(screened)], axis=1)
            screen_columns = lax.all_to_all(both, "energy", 0, 0, tiled=True)
            self_columns = energy_convolve(screen_columns, 0, screen_columns, 1)
        else:
            lesser_columns = lax.all_to_all(to_columns(lesser), "energy", 0, 0, tiled=True)
            self_columns = energy_convolve(lesser_columns, None, screen_columns, 1)
        returned = lax.all_to_all(self_columns, "energy", 0, 0, tiled=True)
        self_energy = to_blocks(returned)
        correction = self_energy[0].astype(jnp.float32)
    return (lesser[None], self_energy)


def solution(mesh):
    placed = (
        P("energy", "layer", None, None, None),
        P("energy", "layer", None, None),
        P("energy", "layer", None, None),
    )
    return jax.shard_map(
        shards,
        mesh=mesh,
        in_specs=placed,
        out_specs=(P("energy", "layer", None, None), P("energy", "layer", None, None)),
        check_vma=False,
    )
```

time: 235 us -> 175 us (0.74)
  the two profiles are of different devices: /device:TPU:2 before, /device:TPU:71 now
where the time goes in v1:
time: 175 us
  blocking collectives  123 us (70%)
  starting transfers between devices  24.5 us (14%)
  matrix products  9.85 us (6%)
  local copies, waits for them, and re-layouts  6.77 us (4%)
  Pallas kernels  4.95 us (3%)
  waiting for transfers between devices  2.41 us (1%)
  other arithmetic  1.89 us (1%)
    all_to_all x2, blocking collectives, shards(): returned = lax.all_to_all(self_columns, 'energy', 0, 0, tiled=True)  50 us
    all_to_all x1, blocking collectives, shards(): screen_columns = lax.all_to_all(both, 'energy', 0, 0, tiled=True)  47.3 us
    all_to_all x1, blocking collectives, shards(): lax.all_to_all(to_columns(lesser), 'energy', 0, 0, tiled=True)  26.2 us
    ppermute x2, starting transfers between devices, halo(): below = lax.ppermute(cells[-1:], axis, [(i, i + 1) for i in range(ends)])  20.1 us
    dot_general x6, matrix products, lesser_blocks(): jnp.einsum('lac,lbc->lab', left_part, factor, preferred_element_type=jnp....  9.85 us
    pallas_call x2, Pallas kernels, energy_convolve(): pl.pallas_call(kernel, out_shape=jax.ShapeDtypeStruct((energies,) + block...  4.95 us
    ppermute x2, starting transfers between devices, halo(): above = lax.ppermute(cells[:1], axis, [(i + 1, i) for i in range(ends)])  4.37 us
  transfers between devices with their start and end apart: 4, of which 1 were waited for; matrix products, arithmetic and copies ran while one was open for 5% of the time, Pallas kernels for 0%

profile of v1, /device:TPU:71, one launch (start us, length us, event | category | flops | bytes accessed | tf_op | source)
XLA Modules:
  0.0 174.7 jit_solution(16152874856672828703)
XLA Ops:
  0.6 1.2 copy.5
  1.8 0.1 bitcast_convert_fusion.1
  1.9 0.3 copy.6
  2.1 0.0 copy-start.2
  2.1 0.1 fusion.34
  2.3 0.7 fusion.46
  3.0 2.4 %collective-permute-start.1 = (bf16[1,256,256]{2,1,0:T(8,128)(2,1)}, bf16[1,256,256]{2,1,0:T(8,128)(2,1)}, u32[]{:S(2)}, u32[]{:S(2)}) collective-permute-start(bf16[1,256,256]{2,1,0:T(8,128)(2,1)} %get-tuple-element.8), channel_id=1, source_target_pairs={{1,0},{2,1},{3,2},{4,3},{5,4},{6,5},{7,6},{8,7},{9,8},{10,9},{11,1... | collective-permute-start | bytes 393224 | tf_op jit(solution)/shard_map/ppermute | solution.py:22
  5.4 4.9 %collective-permute-start = (bf16[1,256,256]{2,1,0:T(8,128)(2,1)}, bf16[1,256,256]{2,1,0:T(8,128)(2,1)}, u32[]{:S(2)}, u32[]{:S(2)}) collective-permute-start(bf16[1,256,256]{2,1,0:T(8,128)(2,1)} %get-tuple-element.9), channel_id=1, source_target_pairs={{0,1},{1,2},{2,3},{3,4},{4,5},{5,6},{6,7},{7,8},{8,9},{9,10},{10,1... | collective-permute-start | bytes 393224 | tf_op jit(solution)/shard_map/ppermute | solution.py:21
  10.4 0.0 copy-done.2
  10.4 0.2 copy.9
  10.5 0.1 bitcast_convert_fusion
  10.6 0.3 copy.10
  10.9 0.0 copy-start.1
  10.9 0.1 fusion.6
  11.0 1.2 copy-done.1
  12.2 0.1 copy.19
  12.2 0.7 fusion.45
  13.0 0.0 collective-permute-done
  13.0 2.2 %fusion = f32[3,256,256]{2,1,0:T(8,128)} fusion(bf16[2,256,256]{2,1,0:T(8,128)(2,1)S(1)} %get-tuple-element.7, bf16[1,256,256]{2,1,0:T(8,128)(2,1)} %collective-permute-done, bf16[3,3,256,256]{3,2,0,1:T(8,128)(2,1)S(1)} %bitcast.70), kind=kOutput, calls=%fused_computation.10 | convolution fusion | flops 202309632 | bytes 1966080 | tf_op jit(solution)/shard_map/lac,lbc->lab/dot_general | solution.py:39
  15.2 2.4 %convolution_add_fusion.3 = f32[3,256,256]{2,1,0:T(8,128)} fusion(f32[3,256,256]{2,1,0:T(8,128)} %fusion, bf16[3,256,256]{2,1,0:T(8,128)(2,1)S(1)} %fusion.34, bf16[3,3,256,256]{3,2,0,1:T(8,128)(2,1)S(1)} %bitcast.71), kind=kOutput, calls=%fused_computation.3 | convolution fusion | flops 201719808 | bytes 2752512 | tf_op jit(solution)/shard_map/lac,lbc->lab/dot_general | solution.py:39
  17.6 0.0 collective-permute-done.1
  17.6 1.7 convolution_add_fusion.2
  19.3 1.1 copy.8
  20.5 1.2 fusion.8
  21.7 0.1 pad_maximum_fusion
  21.8 47.3 %all_to_all.20.l_ref.s_ref = bf16[48,2,16,256]{3,2,1,0:T(8,128)(2,1)} all-to-all(bf16[48,2,16,256]{3,2,1,0:T(8,128)(2,1)S(1)} %pad_maximum_fusion), channel_id=1, replica_groups=mesh['energy'=48,'layer'=16] {'energy'}, dimensions={0} | all-to-all | bytes 1572864 | tf_op jit(solution)/shard_map/all_to_all | solution.py:108
  69.1 2.5 %shard_map.50 = bf16[48,16,256]{2,1,0:T(8,128)(2,1)} custom-call(bf16[48,2,16,256]{3,2,1,0:T(8,128)(2,1)} %all_to_all.20.l_ref.s_ref, bf16[48,2,16,256]{3,2,1,0:T(8,128)(2,1)} %all_to_all.20.l_ref.s_ref), custom_call_target="tpu_custom_call" | custom-call | flops 9633792 | bytes 1179648 | tf_op jit(solution)/shard_map/pallas_call | solution.py:67
  71.6 26.2 %all_to_all.21 = bf16[48,16,256]{2,1,0:T(8,128)(2,1)S(1)} all-to-all(bf16[48,16,256]{2,1,0:T(8,128)(2,1)} %shard_map.50), channel_id=1, replica_groups=mesh['energy'=48,'layer'=16] {'energy'}, dimensions={0} | all-to-all | bytes 786432 | tf_op jit(solution)/shard_map/all_to_all | solution.py:113
  97.8 0.1 fusion.2
  98.0 1.9 %collective-permute-start.3 = (bf16[1,256,256]{2,1,0:T(8,128)(2,1)S(1)}, bf16[1,256,256]{2,1,0:T(8,128)(2,1)S(1)}, u32[]{:S(2)}, u32[]{:S(2)}) collective-permute-start(bf16[1,256,256]{2,1,0:T(8,128)(2,1)S(1)} %get-tuple-element.4), channel_id=1, source_target_pairs={{1,0},{2,1},{3,2},{4,3},{5,4},{6,5},{7,6},{8,7},{9,8},{10,9},{11,1... | collective-permute-start | bytes 393224 | tf_op jit(solution)/shard_map/ppermute | solution.py:22
  99.9 15.2 %collective-permute-start.2 = (bf16[1,256,256]{2,1,0:T(8,128)(2,1)S(1)}, bf16[1,256,256]{2,1,0:T(8,128)(2,1)S(1)}, u32[]{:S(2)}, u32[]{:S(2)}) collective-permute-start(bf16[1,256,256]{2,1,0:T(8,128)(2,1)S(1)} %get-tuple-element.5), channel_id=1, source_target_pairs={{0,1},{1,2},{2,3},{3,4},{4,5},{5,6},{6,7},{7,8},{8,9},{9,10},{10,1... | collective-permute-start | bytes 393224 | tf_op jit(solution)/shard_map/ppermute | solution.py:21
  115.2 2.4 %collective-permute-done.2 = bf16[1,256,256]{2,1,0:T(8,128)(2,1)S(1)} collective-permute-done((bf16[1,256,256]{2,1,0:T(8,128)(2,1)S(1)}, bf16[1,256,256]{2,1,0:T(8,128)(2,1)S(1)}, u32[]{:S(2)}, u32[]{:S(2)}) %collective-permute-start.2) | collective-permute-done | bytes 131104 | tf_op jit(solution)/shard_map/ppermute | solution.py:21
  117.6 1.4 fusion.1
  119.0 1.6 convolution_add_fusion.1
  120.6 0.0 collective-permute-done.3
  120.6 0.5 convolution_add_fusion
  121.1 0.3 copy.14
  121.4 0.1 fusion.4
  121.5 0.0 copy-start
  121.5 26.2 %all_to_all.22.l_ref = bf16[48,16,256]{2,1,0:T(8,128)(2,1)} all-to-all(bf16[48,16,256]{2,1,0:T(8,128)(2,1)S(1)} %bitcast.78), channel_id=1, replica_groups=mesh['energy'=48,'layer'=16] {'energy'}, dimensions={0} | all-to-all | bytes 786432 | tf_op jit(solution)/shard_map/all_to_all | solution.py:111
  147.7 2.4 %shard_map.51 = bf16[48,16,256]{2,1,0:T(8,128)(2,1)} custom-call(bf16[48,16,256]{2,1,0:T(8,128)(2,1)} %all_to_all.22.l_ref, bf16[48,2,16,256]{3,2,1,0:T(8,128)(2,1)} %all_to_all.20.l_ref.s_ref), custom_call_target="tpu_custom_call" | custom-call | flops 9633792 | bytes 1179648 | tf_op jit(solution)/shard_map/pallas_call | solution.py:67
  150.1 0.0 copy-done
  150.1 23.8 %all_to_all.23 = bf16[48,16,256]{2,1,0:T(8,128)(2,1)S(1)} all-to-all(bf16[48,16,256]{2,1,0:T(8,128)(2,1)} %shard_map.51), channel_id=1, replica_groups=mesh['energy'=48,'layer'=16] {'energy'}, dimensions={0} | all-to-all | bytes 786432 | tf_op jit(solution)/shard_map/all_to_all | solution.py:113
  173.9 0.7 copy.21
  (2 shorter events, 0.1 us)
Async XLA Ops:
  2.1 8.2 %copy-start.2 = (bf16[1,3,256,256]{3,2,1,0:T(8,128)(2,1)S(1)}, bf16[1,3,256,256]{3,2,1,0:T(8,128)(2,1)}, u32[]{:S(2)}) copy-start(bf16[1,3,256,256]{3,2,1,0:T(8,128)(2,1)} %param.5) | copy-start | bytes 1179652
  3.0 14.7 %collective-permute-start.1 = (bf16[1,256,256]{2,1,0:T(8,128)(2,1)}, bf16[1,256,256]{2,1,0:T(8,128)(2,1)}, u32[]{:S(2)}, u32[]{:S(2)}) collective-permute-start(bf16[1,256,256]{2,1,0:T(8,128)(2,1)} %get-tuple-element.8), channel_id=1, source_target_pairs={{1,0},{2,1},{3,2},{4,3},{5,4},{6,5},{7,6},{8,7},{9,8},{10,9},{11,1... | collective-permute-start | bytes 393224 | tf_op jit(solution)/shard_map/ppermute | solution.py:22
  5.4 7.6 %collective-permute-start = (bf16[1,256,256]{2,1,0:T(8,128)(2,1)}, bf16[1,256,256]{2,1,0:T(8,128)(2,1)}, u32[]{:S(2)}, u32[]{:S(2)}) collective-permute-start(bf16[1,256,256]{2,1,0:T(8,128)(2,1)} %get-tuple-element.9), channel_id=1, source_target_pairs={{0,1},{1,2},{2,3},{3,4},{4,5},{5,6},{6,7},{7,8},{8,9},{9,10},{10,1... | collective-permute-start | bytes 393224 | tf_op jit(solution)/shard_map/ppermute | solution.py:21
  10.9 1.3 copy-start.1
  98.0 22.6 %collective-permute-start.3 = (bf16[1,256,256]{2,1,0:T(8,128)(2,1)S(1)}, bf16[1,256,256]{2,1,0:T(8,128)(2,1)S(1)}, u32[]{:S(2)}, u32[]{:S(2)}) collective-permute-start(bf16[1,256,256]{2,1,0:T(8,128)(2,1)S(1)} %get-tuple-element.4), channel_id=1, source_target_pairs={{1,0},{2,1},{3,2},{4,3},{5,4},{6,5},{7,6},{8,7},{9,8},{10,9},{11,1... | collective-permute-start | bytes 393224 | tf_op jit(solution)/shard_map/ppermute | solution.py:22
  99.9 17.7 %collective-permute-start.2 = (bf16[1,256,256]{2,1,0:T(8,128)(2,1)S(1)}, bf16[1,256,256]{2,1,0:T(8,128)(2,1)S(1)}, u32[]{:S(2)}, u32[]{:S(2)}) collective-permute-start(bf16[1,256,256]{2,1,0:T(8,128)(2,1)S(1)} %get-tuple-element.5), channel_id=1, source_target_pairs={{0,1},{1,2},{2,3},{3,4},{4,5},{5,6},{6,7},{7,8},{8,9},{9,10},{10,1... | collective-permute-start | bytes 393224 | tf_op jit(solution)/shard_map/ppermute | solution.py:21
  121.5 28.6 %copy-start = (bf16[3,256,256]{2,1,0:T(8,128)(2,1)}, bf16[3,256,256]{2,1,0:T(8,128)(2,1)S(1)}, u32[]{:S(2)}) copy-start(bf16[3,256,256]{2,1,0:T(8,128)(2,1)S(1)} %fusion.4) | copy-start | bytes 1179652

commit v2 on v1

--- a/solution.py
+++ b/solution.py
@@ -77,20 +77,49 @@
     )(l_arr, s_arr)
 
 
+def pack_symmetric(blocks):
+    half = blocks.shape[-1] // 2
+    rows = lax.broadcasted_iota(jnp.int32, (half, half), 0)
+    cols = lax.broadcasted_iota(jnp.int32, (half, half), 1)
+    top_left = blocks[:, :half, :half]
+    bottom_right = blocks[:, half:, half:]
+    folded = jnp.where(rows <= cols, top_left, bottom_right)
+    diagonal = jnp.where(rows == cols, bottom_right, jnp.zeros_like(bottom_right))
+    return jnp.concatenate([folded, blocks[:, :half, half:], diagonal], axis=-1)
+
+
+def unpack_symmetric(packed):
+    half = packed.shape[-1] // 3
+    rows = lax.broadcasted_iota(jnp.int32, (half, half), 0)
+    cols = lax.broadcasted_iota(jnp.int32, (half, half), 1)
+    folded = packed[..., :half]
+    off = packed[..., half : 2 * half]
+    diagonal = packed[..., 2 * half :]
+    flipped = jnp.swapaxes(folded, -1, -2)
+    top_left = jnp.where(rows <= cols, folded, flipped)
+    bottom_right = jnp.where(rows > cols, folded, flipped)
+    bottom_right = jnp.where(rows == cols, diagonal, bottom_right)
+    top = jnp.concatenate([top_left, off], axis=-1)
+    bottom = jnp.concatenate([jnp.swapaxes(off, -1, -2), bottom_right], axis=-1)
+    return jnp.concatenate([top, bottom], axis=-2)
+
+
 def shards(retarded, scatter_in, screen):
     energies = lax.axis_size("energy")
     layers = retarded.shape[1]
     orbitals = retarded.shape[-1]
-    rows = layers * orbitals // energies
+    half = orbitals // 2
+    rows = layers * half // energies
     retarded = retarded[0]
     base_part = symmetric(scatter_in[0])
     screened = symmetric(screen[0]).astype(jnp.bfloat16)
 
     def to_columns(blocks):
-        return blocks.reshape(energies, rows, orbitals)
+        packed = pack_symmetric(blocks)
+        return packed.reshape(energies, rows, packed.shape[-1])
 
     def to_blocks(columns):
-        return columns.reshape(1, layers, orbitals, orbitals)
+        return unpack_symmetric(columns.reshape(layers, half, columns.shape[-1]))
 
     correction = None
     screen_columns = None
@@ -111,8 +140,9 @@
             lesser_columns = lax.all_to_all(to_columns(lesser), "energy", 0, 0, tiled=True)
             self_columns = energy_convolve(lesser_columns, None, screen_columns, 1)
         returned = lax.all_to_all(self_columns, "energy", 0, 0, tiled=True)
-        self_energy = to_blocks(returned)
-        correction = self_energy[0].astype(jnp.float32)
+        self_blocks = to_blocks(returned)
+        self_energy = self_blocks[None]
+        correction = self_blocks.astype(jnp.float32)
     return (lesser[None], self_energy)
 
 

time: 175 us -> 162 us (0.926)
  the two profiles are of different devices: /device:TPU:71 before, /device:TPU:7 now
where the time goes in v2:
time: 162 us; the launch traced here: 161 us
  blocking collectives  96.9 us (60%)
  starting transfers between devices  19.8 us (12%)
  waiting for transfers between devices  18.8 us (12%)
  matrix products  8.72 us (5%)
  local copies, waits for them, and re-layouts  7.48 us (5%)
  Pallas kernels  4.97 us (3%)
  other arithmetic  3.64 us (2%)
    all_to_all x1, blocking collectives, shards(): screen_columns = lax.all_to_all(both, 'energy', 0, 0, tiled=True)  44.2 us
    all_to_all x1, blocking collectives, shards(): returned = lax.all_to_all(self_columns, 'energy', 0, 0, tiled=True)  27.5 us
    all_to_all x1, blocking collectives, shards(): lax.all_to_all(to_columns(lesser), 'energy', 0, 0, tiled=True)  25.2 us
    all_to_all x1, waiting for transfers between devices, shards(): returned = lax.all_to_all(self_columns, 'energy', 0, 0, tiled=True)  15.3 us
    dot_general x6, matrix products, lesser_blocks(): jnp.einsum('lac,lbc->lab', left_part, factor, preferred_element_type=jnp....  8.72 us
    all_to_all x1, starting transfers between devices, shards(): returned = lax.all_to_all(self_columns, 'energy', 0, 0, tiled=True)  8.71 us
    ppermute x2, starting transfers between devices, halo(): below = lax.ppermute(cells[-1:], axis, [(i, i + 1) for i in range(ends)])  5.82 us
    ppermute x2, starting transfers between devices, halo(): above = lax.ppermute(cells[:1], axis, [(i + 1, i) for i in range(ends)])  5.28 us
  transfers between devices with their start and end apart: 5, of which 3 were waited for; matrix products, arithmetic and copies ran while one was open for 5% of the time, Pallas kernels for 0%

profile of v2, /device:TPU:7, one launch (start us, length us, event | category | flops | bytes accessed | tf_op | source)
XLA Modules:
  0.0 161.3 jit_solution(8100909648905953339)
XLA Ops:
  0.6 1.2 copy.5
  1.8 0.1 bitcast_convert_fusion.1
  1.9 0.3 copy.6
  2.1 0.1 fusion.33
  2.3 0.7 fusion.45
  3.0 3.9 %collective-permute-start = (bf16[1,256,256]{2,1,0:T(8,128)(2,1)}, bf16[1,256,256]{2,1,0:T(8,128)(2,1)}, u32[]{:S(2)}, u32[]{:S(2)}) collective-permute-start(bf16[1,256,256]{2,1,0:T(8,128)(2,1)} %get-tuple-element.19), channel_id=1, source_target_pairs={{0,1},{1,2},{2,3},{3,4},{4,5},{5,6},{6,7},{7,8},{8,9},{9,10},{10,1... | collective-permute-start | bytes 393224 | tf_op jit(solution)/shard_map/ppermute | solution.py:21
  6.9 1.9 %collective-permute-start.1 = (bf16[1,256,256]{2,1,0:T(8,128)(2,1)}, bf16[1,256,256]{2,1,0:T(8,128)(2,1)}, u32[]{:S(2)}, u32[]{:S(2)}) collective-permute-start(bf16[1,256,256]{2,1,0:T(8,128)(2,1)} %get-tuple-element.18), channel_id=1, source_target_pairs={{1,0},{2,1},{3,2},{4,3},{5,4},{6,5},{7,6},{8,7},{9,8},{10,9},{11,1... | collective-permute-start | bytes 393224 | tf_op jit(solution)/shard_map/ppermute | solution.py:22
  8.8 0.8 fusion.44
  9.6 0.2 copy.9
  9.8 0.1 bitcast_convert_fusion
  9.9 0.3 copy.10
  10.2 0.0 copy-start.1
  10.2 0.1 fusion.5
  10.3 1.1 copy-done.1
  11.4 0.1 copy.26
  11.5 0.6 iota_compare_fusion.2
  12.1 0.2 copy-done.6
  12.4 2.2 %fusion = f32[3,256,256]{2,1,0:T(8,128)} fusion(bf16[2,256,256]{2,1,0:T(8,128)(2,1)S(1)} %copy-done.6, bf16[1,256,256]{2,1,0:T(8,128)(2,1)} %collective-permute-done, bf16[3,3,256,256]{3,2,0,1:T(8,128)(2,1)S(1)} %bitcast.83), kind=kOutput, calls=%fused_computation.10 | convolution fusion | flops 202309632 | bytes 1966080 | tf_op jit(solution)/shard_map/lac,lbc->lab/dot_general | solution.py:39
  14.6 2.4 %convolution_add_fusion.3 = f32[3,256,256]{2,1,0:T(8,128)} fusion(f32[3,256,256]{2,1,0:T(8,128)} %fusion, bf16[3,256,256]{2,1,0:T(8,128)(2,1)S(1)} %fusion.33, bf16[3,3,256,256]{3,2,0,1:T(8,128)(2,1)S(1)} %bitcast.84), kind=kOutput, calls=%fused_computation.3 | convolution fusion | flops 201719808 | bytes 2752512 | tf_op jit(solution)/shard_map/lac,lbc->lab/dot_general | solution.py:39
  17.0 1.7 %convolution_add_fusion.2 = f32[3,256,256]{2,1,0:T(8,128)S(1)} fusion(f32[3,256,256]{2,1,0:T(8,128)} %convolution_add_fusion.3, bf16[1,256,256]{2,1,0:T(8,128)(2,1)} %collective-permute-done.1, bf16[2,256,256]{2,1,0:T(8,128)(2,1)} %get-tuple-element.16, bf16[3,3,256,256]{3,2,0,1:T(8,128)(2,1)S(1)} %bitcast.85), kind=kOutput, calls=%fused_computation.2 | convolution fusion | flops 202506240 | bytes 2752512 | tf_op jit(solution)/shard_map/lac,lbc->lab/dot_general | solution.py:39
  18.7 1.2 copy.8
  19.9 1.3 fusion.7
  21.2 0.1 slice_select_fusion.3
  21.2 0.1 pad_maximum_fusion.1
  21.3 0.1 pad_maximum_fusion
  21.4 44.2 %all_to_all.20.l_ref.s_ref = bf16[48,2,8,384]{3,2,1,0:T(8,128)(2,1)} all-to-all(bf16[48,2,8,384]{3,2,1,0:T(8,128)(2,1)S(1)} %pad_maximum_fusion), channel_id=1, replica_groups=mesh['energy'=48,'layer'=16] {'energy'}, dimensions={0} | all-to-all | bytes 1179648 | tf_op jit(solution)/shard_map/all_to_all | solution.py:137
  65.7 2.6 %shard_map.50 = bf16[48,8,384]{2,1,0:T(8,128)(2,1)} custom-call(bf16[48,2,8,384]{3,2,1,0:T(8,128)(2,1)} %all_to_all.20.l_ref.s_ref, bf16[48,2,8,384]{3,2,1,0:T(8,128)(2,1)} %all_to_all.20.l_ref.s_ref), custom_call_target="tpu_custom_call" | custom-call | flops 7225344 | bytes 884736 | tf_op jit(solution)/shard_map/pallas_call | solution.py:67
  68.2 8.7 %all-to-all-start.1 = ((bf16[48,8,384]{2,1,0:T(8,128)(2,1)}), bf16[48,8,384]{2,1,0:T(8,128)(2,1)S(1)}, u32[]{:S(2)}, u32[]{:S(2)}) async-start(bf16[48,8,384]{2,1,0:T(8,128)(2,1)} %shard_map.50), calls=%async_computation.1 | async-start | bytes 589824 | tf_op jit(solution)/shard_map/all_to_all | solution.py:142
  77.0 15.3 %all-to-all-done.1 = bf16[48,8,384]{2,1,0:T(8,128)(2,1)S(1)} async-done(((bf16[48,8,384]{2,1,0:T(8,128)(2,1)}), bf16[48,8,384]{2,1,0:T(8,128)(2,1)S(1)}, u32[]{:S(2)}, u32[]{:S(2)}) %all-to-all-start.1) | async-done | bytes 294944 | tf_op jit(solution)/shard_map/all_to_all | solution.py:142
  92.3 0.1 copy.11
  92.4 0.1 copy.12
  92.6 0.2 add_convert_fusion
  92.8 1.9 %collective-permute-start.2 = (bf16[1,256,256]{2,1,0:T(8,128)(2,1)S(1)}, bf16[1,256,256]{2,1,0:T(8,128)(2,1)S(1)}, u32[]{:S(2)}, u32[]{:S(2)}) collective-permute-start(bf16[1,256,256]{2,1,0:T(8,128)(2,1)S(1)} %get-tuple-element.10), channel_id=1, source_target_pairs={{0,1},{1,2},{2,3},{3,4},{4,5},{5,6},{6,7},{7,8},{8,9},{9,10},{10,1... | collective-permute-start | bytes 393224 | tf_op jit(solution)/shard_map/ppermute | solution.py:21
  94.7 3.4 %collective-permute-start.3 = (bf16[1,256,256]{2,1,0:T(8,128)(2,1)S(1)}, bf16[1,256,256]{2,1,0:T(8,128)(2,1)}, u32[]{:S(2)}, u32[]{:S(2)}) collective-permute-start(bf16[1,256,256]{2,1,0:T(8,128)(2,1)S(1)} %get-tuple-element.9), channel_id=1, source_target_pairs={{1,0},{2,1},{3,2},{4,3},{5,4},{6,5},{7,6},{8,7},{9,8},{10,9},{11,1... | collective-permute-start | bytes 393224 | tf_op jit(solution)/shard_map/ppermute | solution.py:22
  98.1 0.4 collective-permute-done.2
  98.5 0.5 fusion.1
  99.0 0.5 convolution_add_fusion.1
  99.5 3.2 %collective-permute-done.3 = bf16[1,256,256]{2,1,0:T(8,128)(2,1)} collective-permute-done((bf16[1,256,256]{2,1,0:T(8,128)(2,1)S(1)}, bf16[1,256,256]{2,1,0:T(8,128)(2,1)}, u32[]{:S(2)}, u32[]{:S(2)}) %collective-permute-start.3) | collective-permute-done | bytes 131104 | tf_op jit(solution)/shard_map/ppermute | solution.py:22
  102.6 1.4 convolution_add_fusion
  104.0 0.3 copy.16
  104.3 0.1 fusion.3
  104.4 0.6 copy-done.4
  105.1 25.2 %all_to_all.21.l_ref = bf16[48,8,384]{2,1,0:T(8,128)(2,1)} all-to-all(bf16[48,8,384]{2,1,0:T(8,128)(2,1)S(1)} %bitcast.94), channel_id=1, replica_groups=mesh['energy'=48,'layer'=16] {'energy'}, dimensions={0} | all-to-all | bytes 589824 | tf_op jit(solution)/shard_map/all_to_all | solution.py:140
  130.3 2.4 %shard_map.51 = bf16[48,8,384]{2,1,0:T(8,128)(2,1)} custom-call(bf16[48,8,384]{2,1,0:T(8,128)(2,1)} %all_to_all.21.l_ref, bf16[48,2,8,384]{3,2,1,0:T(8,128)(2,1)} %all_to_all.20.l_ref.s_ref), custom_call_target="tpu_custom_call" | custom-call | flops 7225344 | bytes 884736 | tf_op jit(solution)/shard_map/pallas_call | solution.py:67
  132.7 27.5 %all_to_all.22 = bf16[48,8,384]{2,1,0:T(8,128)(2,1)S(1)} all-to-all(bf16[48,8,384]{2,1,0:T(8,128)(2,1)} %shard_map.51), channel_id=1, replica_groups=mesh['energy'=48,'layer'=16] {'energy'}, dimensions={0} | all-to-all | bytes 589824 | tf_op jit(solution)/shard_map/all_to_all | solution.py:142
  160.2 0.1 copy.24
  160.4 0.1 copy.20
  160.5 0.8 maximum_bitcast_fusion
  (26 shorter events, 0.3 us)
Async XLA Ops:
  2.2 7.4 %copy-start.5 = (bf16[1,3,256,256]{3,2,1,0:T(8,128)(2,1)S(1)}, bf16[1,3,256,256]{3,2,1,0:T(8,128)(2,1)}, u32[]{:S(2)}) copy-start(bf16[1,3,256,256]{3,2,1,0:T(8,128)(2,1)} %param.5) | copy-start | bytes 1179652
  3.0 9.2 %collective-permute-start = (bf16[1,256,256]{2,1,0:T(8,128)(2,1)}, bf16[1,256,256]{2,1,0:T(8,128)(2,1)}, u32[]{:S(2)}, u32[]{:S(2)}) collective-permute-start(bf16[1,256,256]{2,1,0:T(8,128)(2,1)} %get-tuple-element.19), channel_id=1, source_target_pairs={{0,1},{1,2},{2,3},{3,4},{4,5},{5,6},{6,7},{7,8},{8,9},{9,10},{10,1... | collective-permute-start | bytes 393224 | tf_op jit(solution)/shard_map/ppermute | solution.py:21
  6.9 10.2 %collective-permute-start.1 = (bf16[1,256,256]{2,1,0:T(8,128)(2,1)}, bf16[1,256,256]{2,1,0:T(8,128)(2,1)}, u32[]{:S(2)}, u32[]{:S(2)}) collective-permute-start(bf16[1,256,256]{2,1,0:T(8,128)(2,1)} %get-tuple-element.18), channel_id=1, source_target_pairs={{1,0},{2,1},{3,2},{4,3},{5,4},{6,5},{7,6},{8,7},{9,8},{10,9},{11,1... | collective-permute-start | bytes 393224 | tf_op jit(solution)/shard_map/ppermute | solution.py:22
  10.2 1.3 copy-start.1
  11.4 0.9 copy-start.6
  19.9 1.3 copy-start.2
  65.7 26.7 %copy-start.3 = (pred[128,128]{1,0:T(8,128)(4,1)S(1)}, pred[128,128]{1,0:T(8,128)(4,1)}, u32[]{:S(2)}) copy-start(pred[128,128]{1,0:T(8,128)(4,1)} %iota_compare_fusion.2) | copy-start | bytes 49156
  68.2 24.0 %all-to-all-start.1 = ((bf16[48,8,384]{2,1,0:T(8,128)(2,1)}), bf16[48,8,384]{2,1,0:T(8,128)(2,1)S(1)}, u32[]{:S(2)}, u32[]{:S(2)}) async-start(bf16[48,8,384]{2,1,0:T(8,128)(2,1)} %shard_map.50), calls=%async_computation.1 | async-start | bytes 589824 | tf_op jit(solution)/shard_map/all_to_all | solution.py:142
  77.0 15.5 %copy-start.7 = (pred[128,128]{1,0:T(8,128)(4,1)}, pred[128,128]{1,0:T(8,128)(4,1)S(1)}, u32[]{:S(2)}) copy-start(pred[128,128]{1,0:T(8,128)(4,1)S(1)} %iota_compare_fusion) | copy-start | bytes 49156
  92.8 5.7 %collective-permute-start.2 = (bf16[1,256,256]{2,1,0:T(8,128)(2,1)S(1)}, bf16[1,256,256]{2,1,0:T(8,128)(2,1)S(1)}, u32[]{:S(2)}, u32[]{:S(2)}) collective-permute-start(bf16[1,256,256]{2,1,0:T(8,128)(2,1)S(1)} %get-tuple-element.10), channel_id=1, source_target_pairs={{0,1},{1,2},{2,3},{3,4},{4,5},{5,6},{6,7},{7,8},{8,9},{9,10},{10,1... | collective-permute-start | bytes 393224 | tf_op jit(solution)/shard_map/ppermute | solution.py:21
  94.7 7.9 %collective-permute-start.3 = (bf16[1,256,256]{2,1,0:T(8,128)(2,1)S(1)}, bf16[1,256,256]{2,1,0:T(8,128)(2,1)}, u32[]{:S(2)}, u32[]{:S(2)}) collective-permute-start(bf16[1,256,256]{2,1,0:T(8,128)(2,1)S(1)} %get-tuple-element.9), channel_id=1, source_target_pairs={{1,0},{2,1},{3,2},{4,3},{5,4},{6,5},{7,6},{8,7},{9,8},{10,9},{11,1... | collective-permute-start | bytes 393224 | tf_op jit(solution)/shard_map/ppermute | solution.py:22
  104.3 0.7 copy-start.4
  105.0 27.7 %copy-start = (bf16[3,256,256]{2,1,0:T(8,128)(2,1)}, bf16[3,256,256]{2,1,0:T(8,128)(2,1)S(1)}, u32[]{:S(2)}) copy-start(bf16[3,256,256]{2,1,0:T(8,128)(2,1)S(1)} %fusion.3) | copy-start | bytes 1179652
  130.3 30.1 %copy-start.8 = (pred[128,128]{1,0:T(8,128)(4,1)S(1)}, pred[128,128]{1,0:T(8,128)(4,1)}, u32[]{:S(2)}) copy-start(pred[128,128]{1,0:T(8,128)(4,1)} %copy-done.7) | copy-start | bytes 49156

commit v3 on v2

--- a/solution.py
+++ b/solution.py
@@ -23,24 +23,44 @@
     return below, above
 
 
+def _lesser_kernel(r_ref, c_ref, below_ref, above_ref, o_ref):
+    layers = c_ref.shape[0]
+
+    def neighbour(index):
+        if index < 0:
+            return below_ref[0]
+        if index >= layers:
+            return above_ref[0]
+        return c_ref[index]
+
+    for layer in range(layers):
+        running = None
+        for offset in range(3):
+            factor = r_ref[layer, offset]
+            left_part = jnp.dot(
+                factor, neighbour(layer + offset - 1), preferred_element_type=jnp.float32
+            ).astype(jnp.bfloat16)
+            term_part = lax.dot_general(
+                left_part,
+                factor,
+                (((1,), (1,)), ((), ())),
+                preferred_element_type=jnp.float32,
+            )
+            running = term_part if running is None else running + term_part
+        o_ref[layer] = (0.5 * (running + running.T)).astype(o_ref.dtype)
+
+
 def lesser_blocks(retarded, coupling, below, above):
-    layers = coupling.shape[0]
-    neighbours = (
-        jnp.concatenate([below, coupling[: layers - 1]], axis=0),
-        coupling,
-        jnp.concatenate([coupling[1:], above], axis=0),
-    )
-    running = None
-    for offset in range(3):
-        factor = retarded[:, offset]
-        left_part = jnp.einsum(
-            "lab,lbc->lac", factor, neighbours[offset], preferred_element_type=jnp.float32
-        ).astype(jnp.bfloat16)
-        term_part = jnp.einsum(
-            "lac,lbc->lab", left_part, factor, preferred_element_type=jnp.float32
-        )
-        running = term_part if running is None else running + term_part
-    return symmetric(running).astype(jnp.bfloat16)
+    layers, n = coupling.shape[0], coupling.shape[-1]
+    return pl.pallas_call(
+        _lesser_kernel,
+        out_shape=jax.ShapeDtypeStruct(coupling.shape, jnp.bfloat16),
+        cost_estimate=pl.CostEstimate(
+            flops=layers * 3 * 4 * n * n * n,
+            bytes_accessed=(layers * 3 + layers + 2 + layers) * n * n * 2,
+            transcendentals=0,
+        ),
+    )(retarded, coupling, below, above)
 
 
 def _conv_kernel(l_ref, s_ref, o_ref, lf, sf, *, l_idx, s_idx):

time: 162 us -> 162 us (level)
  matrix products: 8.72 us -> 0 us
  waiting for transfers between devices: 18.8 us -> 26.1 us
  Pallas kernels: 4.97 us -> 11.5 us
  local copies, waits for them, and re-layouts: 7.48 us -> 3.88 us
  blocking collectives: 96.9 us -> 95 us
    dot_general x6 -> x0, matrix products: 8.72 us -> none  [lesser_blocks(): jnp.einsum('lac,lbc->lab', left_part, factor, preferred_element_type=jnp....]
    pallas_call x0 -> x2, Pallas kernels: none -> 6.53 us  [lesser_blocks(): pl.pallas_call(_lesser_kernel, out_shape=jax.ShapeDtypeStruct(coupling.sh...]
    ppermute x2, waiting for transfers between devices: 3.17 us -> 9.52 us  [halo(): above = lax.ppermute(cells[:1], axis, [(i + 1, i) for i in range(ends)])]
    all_to_all x1, blocking collectives: 27.5 us -> 22.5 us  [shards(): returned = lax.all_to_all(self_columns, 'energy', 0, 0, tiled=True)]
    all_to_all x1, blocking collectives: 44.2 us -> 48.7 us  [shards(): screen_columns = lax.all_to_all(both, 'energy', 0, 0, tiled=True)]
    select_n x2, other arithmetic: 0.08 us -> 2.04 us  [pack_symmetric(): folded = jnp.where(rows <= cols, top_left, bottom_right)]
    unnamed x22 -> x13, local copies, waits for them, and re-layouts: 3.54 us -> 2.14 us
  transfers between devices with their start and end apart: 5 -> 5, of which waited for: 3 -> 5; matrix products, arithmetic and copies ran while one was open for 5% -> 0% of each run, Pallas kernels for 0% -> 0%
where the time goes in v3:
time: 162 us; the launch traced here: 160 us
  blocking collectives  95 us (59%)
  waiting for transfers between devices  26.1 us (16%)
  starting transfers between devices  18.8 us (12%)
  Pallas kernels  11.5 us (7%)
  local copies, waits for them, and re-layouts  3.88 us (2%)
  other arithmetic  3.64 us (2%)
    all_to_all x1, blocking collectives, shards(): screen_columns = lax.all_to_all(both, 'energy', 0, 0, tiled=True)  48.7 us
    all_to_all x1, blocking collectives, shards(): lax.all_to_all(to_columns(lesser), 'energy', 0, 0, tiled=True)  23.9 us
    all_to_all x1, blocking collectives, shards(): returned = lax.all_to_all(self_columns, 'energy', 0, 0, tiled=True)  22.5 us
    all_to_all x1, waiting for transfers between devices, shards(): returned = lax.all_to_all(self_columns, 'energy', 0, 0, tiled=True)  16.1 us
    ppermute x2, waiting for transfers between devices, halo(): above = lax.ppermute(cells[:1], axis, [(i + 1, i) for i in range(ends)])  9.52 us
    all_to_all x1, starting transfers between devices, shards(): returned = lax.all_to_all(self_columns, 'energy', 0, 0, tiled=True)  7.73 us
    pallas_call x2, Pallas kernels, lesser_blocks(): pl.pallas_call(_lesser_kernel, out_shape=jax.ShapeDtypeStruct(coupling.sh...  6.53 us
    ppermute x2, starting transfers between devices, halo(): below = lax.ppermute(cells[-1:], axis, [(i, i + 1) for i in range(ends)])  5.82 us
  transfers between devices with their start and end apart: 5, of which 5 were waited for; matrix products, arithmetic and copies ran while one was open for 0% of the time, Pallas kernels for 0%

profile of v3, /device:TPU:7, one launch (start us, length us, event | category | flops | bytes accessed | tf_op | source)
XLA Modules:
  0.0 159.8 jit_solution(9761656062807848472)
XLA Ops:
  0.6 1.2 copy.5
  1.8 0.1 bitcast_convert_fusion.1
  1.9 0.3 copy.6
  2.1 0.0 copy-start.2
  2.2 0.1 fusion.3.c_ref
  2.3 0.0 copy-start
  2.3 0.8 fusion.5
  3.1 3.9 %collective-permute-start = (bf16[1,256,256]{2,1,0:T(8,128)(2,1)}, bf16[1,256,256]{2,1,0:T(8,128)(2,1)}, u32[]{:S(2)}, u32[]{:S(2)}) collective-permute-start(bf16[1,256,256]{2,1,0:T(8,128)(2,1)} %get-tuple-element.15), channel_id=1, source_target_pairs={{0,1},{1,2},{2,3},{3,4},{4,5},{5,6},{6,7},{7,8},{8,9},{9,10},{10,1... | collective-permute-start | bytes 393224 | tf_op jit(solution)/shard_map/ppermute | solution.py:21
  7.0 0.0 copy-done
  7.0 1.9 %collective-permute-start.1 = (bf16[1,256,256]{2,1,0:T(8,128)(2,1)}, bf16[1,256,256]{2,1,0:T(8,128)(2,1)}, u32[]{:S(2)}, u32[]{:S(2)}) collective-permute-start(bf16[1,256,256]{2,1,0:T(8,128)(2,1)} %get-tuple-element.14), channel_id=1, source_target_pairs={{1,0},{2,1},{3,2},{4,3},{5,4},{6,5},{7,6},{8,7},{9,8},{10,9},{11,1... | collective-permute-start | bytes 393224 | tf_op jit(solution)/shard_map/ppermute | solution.py:22
  8.9 0.0 copy-done.2
  8.9 0.2 copy.7
  9.1 0.1 bitcast_convert_fusion
  9.2 0.3 copy.8
  9.4 0.1 fusion.1
  9.6 0.1 collective-permute-done.below_ref
  9.6 5.5 %collective-permute-done.1.above_ref = bf16[1,256,256]{2,1,0:T(8,128)(2,1)} collective-permute-done((bf16[1,256,256]{2,1,0:T(8,128)(2,1)}, bf16[1,256,256]{2,1,0:T(8,128)(2,1)}, u32[]{:S(2)}, u32[]{:S(2)}) %collective-permute-start.1) | collective-permute-done | bytes 131104 | tf_op jit(solution)/shard_map/ppermute | solution.py:22
  15.1 3.3 %shard_map.50 = bf16[3,256,256]{2,1,0:T(8,128)(2,1)} custom-call(bf16[3,3,256,256]{3,2,1,0:T(8,128)(2,1)} %bitcast.57, bf16[3,256,256]{2,1,0:T(8,128)(2,1)} %copy-done, bf16[1,256,256]{2,1,0:T(8,128)(2,1)} %collective-permute-done.below_ref, bf16[1,256,256]{2,1,0:T(8,128)(2,1)} %collective-permute-done.1.above_ref), custom_call_target="tpu_custom_call" | custom-call | flops 603979776 | bytes 2228224 | tf_op jit(solution)/shard_map/pallas_call | solution.py:55
  18.4 1.0 slice_select_fusion.3
  19.4 0.1 pad_maximum_fusion.1
  19.5 0.1 pad_maximum_fusion
  19.6 48.7 %all_to_all.20.l_ref.s_ref = bf16[48,2,8,384]{3,2,1,0:T(8,128)(2,1)} all-to-all(bf16[48,2,8,384]{3,2,1,0:T(8,128)(2,1)S(1)} %pad_maximum_fusion), channel_id=1, replica_groups=mesh['energy'=48,'layer'=16] {'energy'}, dimensions={0} | all-to-all | bytes 1179648 | tf_op jit(solution)/shard_map/all_to_all | solution.py:157
  68.3 2.5 %shard_map.51 = bf16[48,8,384]{2,1,0:T(8,128)(2,1)} custom-call(bf16[48,2,8,384]{3,2,1,0:T(8,128)(2,1)} %all_to_all.20.l_ref.s_ref, bf16[48,2,8,384]{3,2,1,0:T(8,128)(2,1)} %all_to_all.20.l_ref.s_ref), custom_call_target="tpu_custom_call" | custom-call | flops 7225344 | bytes 884736 | tf_op jit(solution)/shard_map/pallas_call | solution.py:87
  70.8 7.7 %all-to-all-start.1 = ((bf16[48,8,384]{2,1,0:T(8,128)(2,1)}), bf16[48,8,384]{2,1,0:T(8,128)(2,1)S(1)}, u32[]{:S(2)}, u32[]{:S(2)}) async-start(bf16[48,8,384]{2,1,0:T(8,128)(2,1)} %shard_map.51), calls=%async_computation.1 | async-start | bytes 589824 | tf_op jit(solution)/shard_map/all_to_all | solution.py:162
  78.6 16.1 %all-to-all-done.1 = bf16[48,8,384]{2,1,0:T(8,128)(2,1)S(1)} async-done(((bf16[48,8,384]{2,1,0:T(8,128)(2,1)}), bf16[48,8,384]{2,1,0:T(8,128)(2,1)S(1)}, u32[]{:S(2)}, u32[]{:S(2)}) %all-to-all-start.1) | async-done | bytes 294944 | tf_op jit(solution)/shard_map/all_to_all | solution.py:162
  94.6 0.1 copy.9
  94.8 0.1 copy.10
  95.0 0.2 add_convert_fusion.c_ref
  95.1 0.0 copy-start.1
  95.2 1.9 %collective-permute-start.2 = (bf16[1,256,256]{2,1,0:T(8,128)(2,1)S(1)}, bf16[1,256,256]{2,1,0:T(8,128)(2,1)S(1)}, u32[]{:S(2)}, u32[]{:S(2)}) collective-permute-start(bf16[1,256,256]{2,1,0:T(8,128)(2,1)S(1)} %get-tuple-element.8), channel_id=1, source_target_pairs={{0,1},{1,2},{2,3},{3,4},{4,5},{5,6},{6,7},{7,8},{8,9},{9,10},{10,1... | collective-permute-start | bytes 393224 | tf_op jit(solution)/shard_map/ppermute | solution.py:21
  97.1 3.4 %collective-permute-start.3 = (bf16[1,256,256]{2,1,0:T(8,128)(2,1)S(1)}, bf16[1,256,256]{2,1,0:T(8,128)(2,1)S(1)}, u32[]{:S(2)}, u32[]{:S(2)}) collective-permute-start(bf16[1,256,256]{2,1,0:T(8,128)(2,1)S(1)} %get-tuple-element.7), channel_id=1, source_target_pairs={{1,0},{2,1},{3,2},{4,3},{5,4},{6,5},{7,6},{8,7},{9,8},{10,9},{11,1... | collective-permute-start | bytes 393224 | tf_op jit(solution)/shard_map/ppermute | solution.py:22
  100.5 0.4 collective-permute-done.2.below_ref
  100.9 0.0 copy-start.3
  100.9 4.0 %collective-permute-done.3.above_ref = bf16[1,256,256]{2,1,0:T(8,128)(2,1)S(1)} collective-permute-done((bf16[1,256,256]{2,1,0:T(8,128)(2,1)S(1)}, bf16[1,256,256]{2,1,0:T(8,128)(2,1)S(1)}, u32[]{:S(2)}, u32[]{:S(2)}) %collective-permute-start.3) | collective-permute-done | bytes 131104 | tf_op jit(solution)/shard_map/ppermute | solution.py:22
  104.9 0.0 copy-done.1
  104.9 0.0 copy-done.3
  104.9 0.0 copy-start.4
  104.9 0.7 copy-done.4
  105.6 3.3 %shard_map.52 = bf16[3,256,256]{2,1,0:T(8,128)(2,1)} custom-call(bf16[3,3,256,256]{3,2,1,0:T(8,128)(2,1)} %bitcast.58, bf16[3,256,256]{2,1,0:T(8,128)(2,1)} %copy-done.1, bf16[1,256,256]{2,1,0:T(8,128)(2,1)} %copy-done.3, bf16[1,256,256]{2,1,0:T(8,128)(2,1)} %copy-done.4), custom_call_target="tpu_custom_call" | custom-call | flops 603979776 | bytes 2228224 | tf_op jit(solution)/shard_map/pallas_call | solution.py:55
  108.8 1.0 slice_select_fusion.1
  109.9 23.9 %all_to_all.21.l_ref = bf16[48,8,384]{2,1,0:T(8,128)(2,1)} all-to-all(bf16[48,8,384]{2,1,0:T(8,128)(2,1)S(1)} %bitcast.53), channel_id=1, replica_groups=mesh['energy'=48,'layer'=16] {'energy'}, dimensions={0} | all-to-all | bytes 589824 | tf_op jit(solution)/shard_map/all_to_all | solution.py:160
  133.8 2.4 %shard_map.53 = bf16[48,8,384]{2,1,0:T(8,128)(2,1)} custom-call(bf16[48,8,384]{2,1,0:T(8,128)(2,1)} %all_to_all.21.l_ref, bf16[48,2,8,384]{3,2,1,0:T(8,128)(2,1)} %all_to_all.20.l_ref.s_ref), custom_call_target="tpu_custom_call" | custom-call | flops 7225344 | bytes 884736 | tf_op jit(solution)/shard_map/pallas_call | solution.py:87
  136.2 22.5 %all_to_all.22 = bf16[48,8,384]{2,1,0:T(8,128)(2,1)S(1)} all-to-all(bf16[48,8,384]{2,1,0:T(8,128)(2,1)} %shard_map.53), channel_id=1, replica_groups=mesh['energy'=48,'layer'=16] {'energy'}, dimensions={0} | all-to-all | bytes 589824 | tf_op jit(solution)/shard_map/all_to_all | solution.py:162
  158.7 0.1 copy.15
  158.9 0.1 copy.14
  159.0 0.8 maximum_bitcast_fusion
  (9 shorter events, 0.2 us)
Async XLA Ops:
  2.1 6.8 %copy-start.2 = (bf16[1,3,256,256]{3,2,1,0:T(8,128)(2,1)S(1)}, bf16[1,3,256,256]{3,2,1,0:T(8,128)(2,1)}, u32[]{:S(2)}) copy-start(bf16[1,3,256,256]{3,2,1,0:T(8,128)(2,1)} %param.5) | copy-start | bytes 1179652
  2.3 4.7 %copy-start = (bf16[3,256,256]{2,1,0:T(8,128)(2,1)}, bf16[3,256,256]{2,1,0:T(8,128)(2,1)S(1)}, u32[]{:S(2)}) copy-start(bf16[3,256,256]{2,1,0:T(8,128)(2,1)S(1)} %fusion.3.c_ref) | copy-start | bytes 1179652
  3.1 6.6 %collective-permute-start = (bf16[1,256,256]{2,1,0:T(8,128)(2,1)}, bf16[1,256,256]{2,1,0:T(8,128)(2,1)}, u32[]{:S(2)}, u32[]{:S(2)}) collective-permute-start(bf16[1,256,256]{2,1,0:T(8,128)(2,1)} %get-tuple-element.15), channel_id=1, source_target_pairs={{0,1},{1,2},{2,3},{3,4},{4,5},{5,6},{6,7},{7,8},{8,9},{9,10},{10,1... | collective-permute-start | bytes 393224 | tf_op jit(solution)/shard_map/ppermute | solution.py:21
  7.0 8.1 %collective-permute-start.1 = (bf16[1,256,256]{2,1,0:T(8,128)(2,1)}, bf16[1,256,256]{2,1,0:T(8,128)(2,1)}, u32[]{:S(2)}, u32[]{:S(2)}) collective-permute-start(bf16[1,256,256]{2,1,0:T(8,128)(2,1)} %get-tuple-element.14), channel_id=1, source_target_pairs={{1,0},{2,1},{3,2},{4,3},{5,4},{6,5},{7,6},{8,7},{9,8},{10,9},{11,1... | collective-permute-start | bytes 393224 | tf_op jit(solution)/shard_map/ppermute | solution.py:22
  70.8 23.8 %all-to-all-start.1 = ((bf16[48,8,384]{2,1,0:T(8,128)(2,1)}), bf16[48,8,384]{2,1,0:T(8,128)(2,1)S(1)}, u32[]{:S(2)}, u32[]{:S(2)}) async-start(bf16[48,8,384]{2,1,0:T(8,128)(2,1)} %shard_map.51), calls=%async_computation.1 | async-start | bytes 589824 | tf_op jit(solution)/shard_map/all_to_all | solution.py:162
  95.1 9.8 %copy-start.1 = (bf16[3,256,256]{2,1,0:T(8,128)(2,1)}, bf16[3,256,256]{2,1,0:T(8,128)(2,1)S(1)}, u32[]{:S(2)}) copy-start(bf16[3,256,256]{2,1,0:T(8,128)(2,1)S(1)} %add_convert_fusion.c_ref) | copy-start | bytes 1179652
  95.2 5.7 %collective-permute-start.2 = (bf16[1,256,256]{2,1,0:T(8,128)(2,1)S(1)}, bf16[1,256,256]{2,1,0:T(8,128)(2,1)S(1)}, u32[]{:S(2)}, u32[]{:S(2)}) collective-permute-start(bf16[1,256,256]{2,1,0:T(8,128)(2,1)S(1)} %get-tuple-element.8), channel_id=1, source_target_pairs={{0,1},{1,2},{2,3},{3,4},{4,5},{5,6},{6,7},{7,8},{8,9},{9,10},{10,1... | collective-permute-start | bytes 393224 | tf_op jit(solution)/shard_map/ppermute | solution.py:21
  97.1 7.8 %collective-permute-start.3 = (bf16[1,256,256]{2,1,0:T(8,128)(2,1)S(1)}, bf16[1,256,256]{2,1,0:T(8,128)(2,1)S(1)}, u32[]{:S(2)}, u32[]{:S(2)}) collective-permute-start(bf16[1,256,256]{2,1,0:T(8,128)(2,1)S(1)} %get-tuple-element.7), channel_id=1, source_target_pairs={{1,0},{2,1},{3,2},{4,3},{5,4},{6,5},{7,6},{8,7},{9,8},{10,9},{11,1... | collective-permute-start | bytes 393224 | tf_op jit(solution)/shard_map/ppermute | solution.py:22
  100.9 4.0 %copy-start.3 = (bf16[1,256,256]{2,1,0:T(8,128)(2,1)}, bf16[1,256,256]{2,1,0:T(8,128)(2,1)S(1)}, u32[]{:S(2)}) copy-start(bf16[1,256,256]{2,1,0:T(8,128)(2,1)S(1)} %collective-permute-done.2.below_ref) | copy-start | bytes 393220
  104.9 0.7 copy-start.4

commit v4 on v3

--- a/solution.py
+++ b/solution.py
@@ -63,15 +63,8 @@
     )(retarded, coupling, below, above)
 
 
-def _conv_kernel(l_ref, s_ref, o_ref, lf, sf, *, l_idx, s_idx):
+def _conv_core(lf, sf, o_ref):
     energies = o_ref.shape[0]
-
-    def read(ref, idx, e):
-        return ref[e] if idx is None else ref[e, idx]
-
-    for e in range(energies):
-        lf[e] = read(l_ref, l_idx, e).astype(jnp.float32)
-        sf[e] = read(s_ref, s_idx, e).astype(jnp.float32)
     for e in range(energies):
         acc = lf[e] * sf[0]
         for j in range(1, e + 1):
@@ -79,22 +72,50 @@
         o_ref[e] = acc.astype(o_ref.dtype)
 
 
-def energy_convolve(l_arr, l_idx, s_arr, s_idx):
-    energies = l_arr.shape[0]
-    block = l_arr.shape[-2:]
-    elems = energies * block[0] * block[1]
-    kernel = functools.partial(_conv_kernel, l_idx=l_idx, s_idx=s_idx)
+def _conv_first_kernel(x_ref, o_ref, s_out_ref, lf, sf):
+    energies = o_ref.shape[0]
+    h = x_ref.shape[-1] // 5
+    for e in range(energies):
+        lf[e, :, : 2 * h] = x_ref[e, :, : 2 * h].astype(jnp.float32)
+        sf[e, :, : 2 * h] = x_ref[e, :, 2 * h : 4 * h].astype(jnp.float32)
+        shared = x_ref[e, :, 4 * h :].astype(jnp.float32)
+        lf[e, :, 2 * h :] = shared
+        sf[e, :, 2 * h :] = pltpu.roll(shared, h // 2, 1)
+    _conv_core(lf, sf, o_ref)
+    s_out_ref[...] = sf[...].astype(s_out_ref.dtype)
+
+
+def _conv_kernel(l_ref, s_ref, o_ref, lf, sf):
+    energies = o_ref.shape[0]
+    for e in range(energies):
+        lf[e] = l_ref[e].astype(jnp.float32)
+        sf[e] = s_ref[e].astype(jnp.float32)
+    _conv_core(lf, sf, o_ref)
+
+
+def _conv_call(kernel, outs, block, args):
+    energies = block[0]
+    elems = block[0] * block[1] * block[2]
     return pl.pallas_call(
         kernel,
-        out_shape=jax.ShapeDtypeStruct((energies,) + block, jnp.bfloat16),
-        scratch_shapes=[
-            pltpu.VMEM((energies,) + block, jnp.float32),
-            pltpu.VMEM((energies,) + block, jnp.float32),
-        ],
+        out_shape=outs,
+        scratch_shapes=[pltpu.VMEM(block, jnp.float32), pltpu.VMEM(block, jnp.float32)],
         cost_estimate=pl.CostEstimate(
-            flops=elems * (energies + 1), bytes_accessed=elems * 6, transcendentals=0
+            flops=elems * (energies + 1), bytes_accessed=elems * 8, transcendentals=0
         ),
-    )(l_arr, s_arr)
+    )(*args)
+
+
+def energy_convolve_first(x):
+    energies, rows, width = x.shape
+    block = (energies, rows, width // 5 * 3)
+    outs = (jax.ShapeDtypeStruct(block, jnp.bfloat16), jax.ShapeDtypeStruct(block, jnp.bfloat16))
+    return _conv_call(_conv_first_kernel, outs, block, (x,))
+
+
+def energy_convolve(l_arr, s_arr):
+    block = l_arr.shape
+    return _conv_call(_conv_kernel, jax.ShapeDtypeStruct(block, jnp.bfloat16), block, (l_arr, s_arr))
 
 
 def pack_symmetric(blocks):
@@ -106,6 +127,17 @@
     folded = jnp.where(rows <= cols, top_left, bottom_right)
     diagonal = jnp.where(rows == cols, bottom_right, jnp.zeros_like(bottom_right))
     return jnp.concatenate([folded, blocks[:, :half, half:], diagonal], axis=-1)
+
+
+def pack_symmetric_pair(first, second):
+    half = first.shape[-1] // 2
+    rows = lax.broadcasted_iota(jnp.int32, (half, half), 0)
+    cols = lax.broadcasted_iota(jnp.int32, (half, half), 1)
+    a = pack_symmetric(first)
+    b = pack_symmetric(second)
+    moved = jnp.roll(b[..., 2 * half :], half // 2, axis=-1)
+    shared = jnp.where(rows == cols, a[..., 2 * half :], moved)
+    return jnp.concatenate([a[..., : 2 * half], b[..., : 2 * half], shared], axis=-1)
 
 
 def unpack_symmetric(packed):
@@ -153,12 +185,14 @@
         below, above = halo(coupling, "layer")
         lesser = lesser_blocks(retarded, coupling, below, above)
         if screen_columns is None:
-            both = jnp.stack([to_columns(lesser), to_columns(screened)], axis=1)
-            screen_columns = lax.all_to_all(both, "energy", 0, 0, tiled=True)
-            self_columns = energy_convolve(screen_columns, 0, screen_columns, 1)
+            both = pack_symmetric_pair(lesser, screened)
+            both = lax.all_to_all(
+                both.reshape(energies, rows, both.shape[-1]), "energy", 0, 0, tiled=True
+            )
+            self_columns, screen_columns = energy_convolve_first(both)
         else:
             lesser_columns = lax.all_to_all(to_columns(lesser), "energy", 0, 0, tiled=True)
-            self_columns = energy_convolve(lesser_columns, None, screen_columns, 1)
+            self_columns = energy_convolve(lesser_columns, screen_columns)
         returned = lax.all_to_all(self_columns, "energy", 0, 0, tiled=True)
         self_blocks = to_blocks(returned)
         self_energy = self_blocks[None]

time: 162 us -> 161 us (level)
  blocking collectives: 95 us -> 91.2 us
    all_to_all x1, blocking collectives: 48.7 us -> 44.5 us  [shards(): lax.all_to_all(both.reshape(energies, rows, both.shape[-1]), 'energy', 0,...]
    all_to_all x1, blocking collectives: 22.5 us -> 24.3 us  [shards(): returned = lax.all_to_all(self_columns, 'energy', 0, 0, tiled=True)]
where the time goes in v4:
time: 161 us; the launch traced here: 159 us
  blocking collectives  91.2 us (57%)
  waiting for transfers between devices  27.6 us (17%)
  starting transfers between devices  18.9 us (12%)
  Pallas kernels  11.2 us (7%)
  local copies, waits for them, and re-layouts  4.9 us (3%)
  other arithmetic  4.54 us (3%)
    all_to_all x1, blocking collectives, shards(): lax.all_to_all(both.reshape(energies, rows, both.shape[-1]), 'energy', 0,...  44.5 us
    all_to_all x1, blocking collectives, shards(): returned = lax.all_to_all(self_columns, 'energy', 0, 0, tiled=True)  24.3 us
    all_to_all x1, blocking collectives, shards(): lax.all_to_all(to_columns(lesser), 'energy', 0, 0, tiled=True)  22.4 us
    all_to_all x1, waiting for transfers between devices, shards(): returned = lax.all_to_all(self_columns, 'energy', 0, 0, tiled=True)  16.8 us
    ppermute x2, waiting for transfers between devices, halo(): above = lax.ppermute(cells[:1], axis, [(i + 1, i) for i in range(ends)])  9.52 us
    all_to_all x1, starting transfers between devices, shards(): returned = lax.all_to_all(self_columns, 'energy', 0, 0, tiled=True)  7.81 us
    pallas_call x2, Pallas kernels, lesser_blocks(): pl.pallas_call(_lesser_kernel, out_shape=jax.ShapeDtypeStruct(coupling.sh...  6.53 us
    ppermute x2, starting transfers between devices, halo(): below = lax.ppermute(cells[-1:], axis, [(i, i + 1) for i in range(ends)])  5.82 us
  transfers between devices with their start and end apart: 5, of which 5 were waited for; matrix products, arithmetic and copies ran while one was open for 0% of the time, Pallas kernels for 0%

profile of v4, /device:TPU:7, one launch (start us, length us, event | category | flops | bytes accessed | tf_op | source)
XLA Modules:
  0.0 159.3 jit_solution(12114509657362155191)
XLA Ops:
  0.6 1.2 copy.5
  1.8 0.1 bitcast_convert_fusion.1
  1.9 0.3 copy.6
  2.1 0.0 copy-start.2
  2.2 0.1 fusion.3.c_ref
  2.3 0.0 copy-start
  2.3 0.8 fusion.8
  3.1 3.9 %collective-permute-start = (bf16[1,256,256]{2,1,0:T(8,128)(2,1)}, bf16[1,256,256]{2,1,0:T(8,128)(2,1)}, u32[]{:S(2)}, u32[]{:S(2)}) collective-permute-start(bf16[1,256,256]{2,1,0:T(8,128)(2,1)} %get-tuple-element.18), channel_id=1, source_target_pairs={{0,1},{1,2},{2,3},{3,4},{4,5},{5,6},{6,7},{7,8},{8,9},{9,10},{10,1... | collective-permute-start | bytes 393224 | tf_op jit(solution)/shard_map/ppermute | solution.py:21
  7.0 0.0 copy-done
  7.0 1.9 %collective-permute-start.1 = (bf16[1,256,256]{2,1,0:T(8,128)(2,1)}, bf16[1,256,256]{2,1,0:T(8,128)(2,1)}, u32[]{:S(2)}, u32[]{:S(2)}) collective-permute-start(bf16[1,256,256]{2,1,0:T(8,128)(2,1)} %get-tuple-element.17), channel_id=1, source_target_pairs={{1,0},{2,1},{3,2},{4,3},{5,4},{6,5},{7,6},{8,7},{9,8},{10,9},{11,1... | collective-permute-start | bytes 393224 | tf_op jit(solution)/shard_map/ppermute | solution.py:22
  8.9 0.0 copy-done.2
  8.9 0.2 copy.7
  9.1 0.1 bitcast_convert_fusion
  9.2 0.3 copy.8
  9.4 0.1 fusion.1
  9.6 0.1 collective-permute-done.below_ref
  9.6 5.5 %collective-permute-done.1.above_ref = bf16[1,256,256]{2,1,0:T(8,128)(2,1)} collective-permute-done((bf16[1,256,256]{2,1,0:T(8,128)(2,1)}, bf16[1,256,256]{2,1,0:T(8,128)(2,1)}, u32[]{:S(2)}, u32[]{:S(2)}) %collective-permute-start.1) | collective-permute-done | bytes 131104 | tf_op jit(solution)/shard_map/ppermute | solution.py:22
  15.1 3.3 %shard_map.50 = bf16[3,256,256]{2,1,0:T(8,128)(2,1)} custom-call(bf16[3,3,256,256]{3,2,1,0:T(8,128)(2,1)} %bitcast.55, bf16[3,256,256]{2,1,0:T(8,128)(2,1)} %copy-done, bf16[1,256,256]{2,1,0:T(8,128)(2,1)} %collective-permute-done.below_ref, bf16[1,256,256]{2,1,0:T(8,128)(2,1)} %collective-permute-done.1.above_ref), custom_call_target="tpu_custom_call" | custom-call | flops 603979776 | bytes 2228224 | tf_op jit(solution)/shard_map/pallas_call | solution.py:55
  18.4 1.0 fusion.5
  19.4 0.9 slice_dynamic-update-slice_fusion.1
  20.3 0.1 fusion.4
  20.3 0.1 broadcast_select_fusion.1
  20.4 0.1 fusion.9
  20.5 1.0 fusion.6
  21.5 44.5 %all_to_all.20.x_ref = bf16[48,8,640]{2,1,0:T(8,128)(2,1)} all-to-all(bf16[48,8,640]{2,1,0:T(8,128)(2,1)S(1)} %bitcast.53), channel_id=1, replica_groups=mesh['energy'=48,'layer'=16] {'energy'}, dimensions={0} | all-to-all | bytes 983040 | tf_op jit(solution)/shard_map/all_to_all | solution.py:189
  66.0 2.4 %shard_map.51 = (bf16[48,8,384]{2,1,0:T(8,128)(2,1)}, bf16[48,8,384]{2,1,0:T(8,128)(2,1)}) custom-call(bf16[48,8,640]{2,1,0:T(8,128)(2,1)} %all_to_all.20.x_ref), custom_call_target="tpu_custom_call" | custom-call | flops 7225344 | bytes 1179648 | tf_op jit(solution)/shard_map/pallas_call | solution.py:99
  68.4 7.8 %all-to-all-start.1 = ((bf16[48,8,384]{2,1,0:T(8,128)(2,1)}), bf16[48,8,384]{2,1,0:T(8,128)(2,1)S(1)}, u32[]{:S(2)}, u32[]{:S(2)}) async-start(bf16[48,8,384]{2,1,0:T(8,128)(2,1)} %get-tuple-element.4), calls=%async_computation.1 | async-start | bytes 589824 | tf_op jit(solution)/shard_map/all_to_all | solution.py:196
  76.2 16.8 %all-to-all-done.1 = bf16[48,8,384]{2,1,0:T(8,128)(2,1)S(1)} async-done(((bf16[48,8,384]{2,1,0:T(8,128)(2,1)}), bf16[48,8,384]{2,1,0:T(8,128)(2,1)S(1)}, u32[]{:S(2)}, u32[]{:S(2)}) %all-to-all-start.1) | async-done | bytes 294944 | tf_op jit(solution)/shard_map/all_to_all | solution.py:196
  93.1 0.1 copy.9
  93.3 0.1 copy.10
  93.4 0.2 add_convert_fusion.c_ref
  93.6 0.0 copy-start.1
  93.6 1.9 %collective-permute-start.2 = (bf16[1,256,256]{2,1,0:T(8,128)(2,1)S(1)}, bf16[1,256,256]{2,1,0:T(8,128)(2,1)S(1)}, u32[]{:S(2)}, u32[]{:S(2)}) collective-permute-start(bf16[1,256,256]{2,1,0:T(8,128)(2,1)S(1)} %get-tuple-element.12), channel_id=1, source_target_pairs={{0,1},{1,2},{2,3},{3,4},{4,5},{5,6},{6,7},{7,8},{8,9},{9,10},{10,1... | collective-permute-start | bytes 393224 | tf_op jit(solution)/shard_map/ppermute | solution.py:21
  95.5 3.4 %collective-permute-start.3 = (bf16[1,256,256]{2,1,0:T(8,128)(2,1)S(1)}, bf16[1,256,256]{2,1,0:T(8,128)(2,1)S(1)}, u32[]{:S(2)}, u32[]{:S(2)}) collective-permute-start(bf16[1,256,256]{2,1,0:T(8,128)(2,1)S(1)} %get-tuple-element.11), channel_id=1, source_target_pairs={{1,0},{2,1},{3,2},{4,3},{5,4},{6,5},{7,6},{8,7},{9,8},{10,9},{11,1... | collective-permute-start | bytes 393224 | tf_op jit(solution)/shard_map/ppermute | solution.py:22
  98.9 1.2 collective-permute-done.2.below_ref
  100.1 0.0 copy-start.3
  100.1 4.0 %collective-permute-done.3.above_ref = bf16[1,256,256]{2,1,0:T(8,128)(2,1)S(1)} collective-permute-done((bf16[1,256,256]{2,1,0:T(8,128)(2,1)S(1)}, bf16[1,256,256]{2,1,0:T(8,128)(2,1)S(1)}, u32[]{:S(2)}, u32[]{:S(2)}) %collective-permute-start.3) | collective-permute-done | bytes 131104 | tf_op jit(solution)/shard_map/ppermute | solution.py:22
  104.2 0.0 copy-done.1
  104.2 0.0 copy-done.3
  104.2 0.6 copy-done.4
  104.8 3.3 %shard_map.52 = bf16[3,256,256]{2,1,0:T(8,128)(2,1)} custom-call(bf16[3,3,256,256]{3,2,1,0:T(8,128)(2,1)} %bitcast.56, bf16[3,256,256]{2,1,0:T(8,128)(2,1)} %copy-done.1, bf16[1,256,256]{2,1,0:T(8,128)(2,1)} %copy-done.3, bf16[1,256,256]{2,1,0:T(8,128)(2,1)} %copy-done.4), custom_call_target="tpu_custom_call" | custom-call | flops 603979776 | bytes 2228224 | tf_op jit(solution)/shard_map/pallas_call | solution.py:55
  108.1 1.0 slice_select_fusion.1
  109.2 22.4 %all_to_all.21.l_ref = bf16[48,8,384]{2,1,0:T(8,128)(2,1)} all-to-all(bf16[48,8,384]{2,1,0:T(8,128)(2,1)S(1)} %bitcast.52), channel_id=1, replica_groups=mesh['energy'=48,'layer'=16] {'energy'}, dimensions={0} | all-to-all | bytes 589824 | tf_op jit(solution)/shard_map/all_to_all | solution.py:194
  131.6 2.3 %shard_map.53 = bf16[48,8,384]{2,1,0:T(8,128)(2,1)} custom-call(bf16[48,8,384]{2,1,0:T(8,128)(2,1)} %all_to_all.21.l_ref, bf16[48,8,384]{2,1,0:T(8,128)(2,1)} %get-tuple-element.5.s_ref), custom_call_target="tpu_custom_call" | custom-call | flops 7225344 | bytes 1179648 | tf_op jit(solution)/shard_map/pallas_call | solution.py:99
  133.9 24.3 %all_to_all.22 = bf16[48,8,384]{2,1,0:T(8,128)(2,1)S(1)} all-to-all(bf16[48,8,384]{2,1,0:T(8,128)(2,1)} %shard_map.53), channel_id=1, replica_groups=mesh['energy'=48,'layer'=16] {'energy'}, dimensions={0} | all-to-all | bytes 589824 | tf_op jit(solution)/shard_map/all_to_all | solution.py:196
  158.2 0.1 copy.15
  158.3 0.1 copy.14
  158.5 0.8 maximum_bitcast_fusion
  (9 shorter events, 0.2 us)
Async XLA Ops:
  2.1 6.8 %copy-start.2 = (bf16[1,3,256,256]{3,2,1,0:T(8,128)(2,1)S(1)}, bf16[1,3,256,256]{3,2,1,0:T(8,128)(2,1)}, u32[]{:S(2)}) copy-start(bf16[1,3,256,256]{3,2,1,0:T(8,128)(2,1)} %param.5) | copy-start | bytes 1179652
  2.3 4.7 %copy-start = (bf16[3,256,256]{2,1,0:T(8,128)(2,1)}, bf16[3,256,256]{2,1,0:T(8,128)(2,1)S(1)}, u32[]{:S(2)}) copy-start(bf16[3,256,256]{2,1,0:T(8,128)(2,1)S(1)} %fusion.3.c_ref) | copy-start | bytes 1179652
  3.1 6.6 %collective-permute-start = (bf16[1,256,256]{2,1,0:T(8,128)(2,1)}, bf16[1,256,256]{2,1,0:T(8,128)(2,1)}, u32[]{:S(2)}, u32[]{:S(2)}) collective-permute-start(bf16[1,256,256]{2,1,0:T(8,128)(2,1)} %get-tuple-element.18), channel_id=1, source_target_pairs={{0,1},{1,2},{2,3},{3,4},{4,5},{5,6},{6,7},{7,8},{8,9},{9,10},{10,1... | collective-permute-start | bytes 393224 | tf_op jit(solution)/shard_map/ppermute | solution.py:21
  7.0 8.1 %collective-permute-start.1 = (bf16[1,256,256]{2,1,0:T(8,128)(2,1)}, bf16[1,256,256]{2,1,0:T(8,128)(2,1)}, u32[]{:S(2)}, u32[]{:S(2)}) collective-permute-start(bf16[1,256,256]{2,1,0:T(8,128)(2,1)} %get-tuple-element.17), channel_id=1, source_target_pairs={{1,0},{2,1},{3,2},{4,3},{5,4},{6,5},{7,6},{8,7},{9,8},{10,9},{11,1... | collective-permute-start | bytes 393224 | tf_op jit(solution)/shard_map/ppermute | solution.py:22
  68.4 24.7 %all-to-all-start.1 = ((bf16[48,8,384]{2,1,0:T(8,128)(2,1)}), bf16[48,8,384]{2,1,0:T(8,128)(2,1)S(1)}, u32[]{:S(2)}, u32[]{:S(2)}) async-start(bf16[48,8,384]{2,1,0:T(8,128)(2,1)} %get-tuple-element.4), calls=%async_computation.1 | async-start | bytes 589824 | tf_op jit(solution)/shard_map/all_to_all | solution.py:196
  93.6 10.6 %copy-start.1 = (bf16[3,256,256]{2,1,0:T(8,128)(2,1)}, bf16[3,256,256]{2,1,0:T(8,128)(2,1)S(1)}, u32[]{:S(2)}) copy-start(bf16[3,256,256]{2,1,0:T(8,128)(2,1)S(1)} %add_convert_fusion.c_ref) | copy-start | bytes 1179652
  93.6 6.5 %collective-permute-start.2 = (bf16[1,256,256]{2,1,0:T(8,128)(2,1)S(1)}, bf16[1,256,256]{2,1,0:T(8,128)(2,1)S(1)}, u32[]{:S(2)}, u32[]{:S(2)}) collective-permute-start(bf16[1,256,256]{2,1,0:T(8,128)(2,1)S(1)} %get-tuple-element.12), channel_id=1, source_target_pairs={{0,1},{1,2},{2,3},{3,4},{4,5},{5,6},{6,7},{7,8},{8,9},{9,10},{10,1... | collective-permute-start | bytes 393224 | tf_op jit(solution)/shard_map/ppermute | solution.py:21
  95.5 8.6 %collective-permute-start.3 = (bf16[1,256,256]{2,1,0:T(8,128)(2,1)S(1)}, bf16[1,256,256]{2,1,0:T(8,128)(2,1)S(1)}, u32[]{:S(2)}, u32[]{:S(2)}) collective-permute-start(bf16[1,256,256]{2,1,0:T(8,128)(2,1)S(1)} %get-tuple-element.11), channel_id=1, source_target_pairs={{1,0},{2,1},{3,2},{4,3},{5,4},{6,5},{7,6},{8,7},{9,8},{10,9},{11,1... | collective-permute-start | bytes 393224 | tf_op jit(solution)/shard_map/ppermute | solution.py:22
  100.1 4.0 %copy-start.3 = (bf16[1,256,256]{2,1,0:T(8,128)(2,1)}, bf16[1,256,256]{2,1,0:T(8,128)(2,1)S(1)}, u32[]{:S(2)}) copy-start(bf16[1,256,256]{2,1,0:T(8,128)(2,1)S(1)} %collective-permute-done.2.below_ref) | copy-start | bytes 393220
  104.2 0.6 copy-start.4

commit v5 on v4

--- a/solution.py
+++ b/solution.py
@@ -63,13 +63,23 @@
     )(retarded, coupling, below, above)
 
 
-def _conv_core(lf, sf, o_ref):
+def _conv_core(lf, sf, o_ref, group=4):
     energies = o_ref.shape[0]
-    for e in range(energies):
-        acc = lf[e] * sf[0]
-        for j in range(1, e + 1):
-            acc = acc + lf[e - j] * sf[j]
-        o_ref[e] = acc.astype(o_ref.dtype)
+    for first in range(0, energies, group):
+        last = min(first + group, energies)
+        acc = [None] * (last - first)
+        window = {}
+        for j in range(last):
+            s_row = sf[j]
+            for e in range(max(first, j), last):
+                if e - j not in window:
+                    window[e - j] = lf[e - j]
+                term = window[e - j] * s_row
+                k = e - first
+                acc[k] = term if acc[k] is None else acc[k] + term
+            window.pop(last - 1 - j, None)
+        for k in range(last - first):
+            o_ref[first + k] = acc[k].astype(o_ref.dtype)
 
 
 def _conv_first_kernel(x_ref, o_ref, s_out_ref, lf, sf):

time: 161 us -> 161 us (level)
  no operation moved by 1% of the time
where the time goes in v5:
time: 161 us; the launch traced here: 159 us
  blocking collectives  91.2 us (57%)
  waiting for transfers between devices  27.6 us (17%)
  starting transfers between devices  18.9 us (12%)
  Pallas kernels  11.2 us (7%)
  local copies, waits for them, and re-layouts  4.9 us (3%)
  other arithmetic  4.54 us (3%)
    all_to_all x1, blocking collectives, shards(): lax.all_to_all(both.reshape(energies, rows, both.shape[-1]), 'energy', 0,...  44.5 us
    all_to_all x1, blocking collectives, shards(): returned = lax.all_to_all(self_columns, 'energy', 0, 0, tiled=True)  24.3 us
    all_to_all x1, blocking collectives, shards(): lax.all_to_all(to_columns(lesser), 'energy', 0, 0, tiled=True)  22.4 us
    all_to_all x1, waiting for transfers between devices, shards(): returned = lax.all_to_all(self_columns, 'energy', 0, 0, tiled=True)  16.8 us
    ppermute x2, waiting for transfers between devices, halo(): above = lax.ppermute(cells[:1], axis, [(i + 1, i) for i in range(ends)])  9.52 us
    all_to_all x1, starting transfers between devices, shards(): returned = lax.all_to_all(self_columns, 'energy', 0, 0, tiled=True)  7.81 us
    pallas_call x2, Pallas kernels, lesser_blocks(): pl.pallas_call(_lesser_kernel, out_shape=jax.ShapeDtypeStruct(coupling.sh...  6.53 us
    ppermute x2, starting transfers between devices, halo(): below = lax.ppermute(cells[-1:], axis, [(i, i + 1) for i in range(ends)])  5.82 us
  transfers between devices with their start and end apart: 5, of which 5 were waited for; matrix products, arithmetic and copies ran while one was open for 0% of the time, Pallas kernels for 0%

profile of v5, /device:TPU:7, one launch (start us, length us, event | category | flops | bytes accessed | tf_op | source)
XLA Modules:
  0.0 159.3 jit_solution(3032265751863523510)
XLA Ops:
  0.6 1.2 copy.5
  1.8 0.1 bitcast_convert_fusion.1
  1.9 0.3 copy.6
  2.1 0.0 copy-start.2
  2.2 0.1 fusion.3.c_ref
  2.3 0.0 copy-start
  2.3 0.8 fusion.8
  3.1 3.9 %collective-permute-start = (bf16[1,256,256]{2,1,0:T(8,128)(2,1)}, bf16[1,256,256]{2,1,0:T(8,128)(2,1)}, u32[]{:S(2)}, u32[]{:S(2)}) collective-permute-start(bf16[1,256,256]{2,1,0:T(8,128)(2,1)} %get-tuple-element.18), channel_id=1, source_target_pairs={{0,1},{1,2},{2,3},{3,4},{4,5},{5,6},{6,7},{7,8},{8,9},{9,10},{10,1... | collective-permute-start | bytes 393224 | tf_op jit(solution)/shard_map/ppermute | solution.py:21
  7.0 0.0 copy-done
  7.0 1.9 %collective-permute-start.1 = (bf16[1,256,256]{2,1,0:T(8,128)(2,1)}, bf16[1,256,256]{2,1,0:T(8,128)(2,1)}, u32[]{:S(2)}, u32[]{:S(2)}) collective-permute-start(bf16[1,256,256]{2,1,0:T(8,128)(2,1)} %get-tuple-element.17), channel_id=1, source_target_pairs={{1,0},{2,1},{3,2},{4,3},{5,4},{6,5},{7,6},{8,7},{9,8},{10,9},{11,1... | collective-permute-start | bytes 393224 | tf_op jit(solution)/shard_map/ppermute | solution.py:22
  8.9 0.0 copy-done.2
  8.9 0.2 copy.7
  9.1 0.1 bitcast_convert_fusion
  9.2 0.3 copy.8
  9.4 0.1 fusion.1
  9.6 0.1 collective-permute-done.below_ref
  9.6 5.5 %collective-permute-done.1.above_ref = bf16[1,256,256]{2,1,0:T(8,128)(2,1)} collective-permute-done((bf16[1,256,256]{2,1,0:T(8,128)(2,1)}, bf16[1,256,256]{2,1,0:T(8,128)(2,1)}, u32[]{:S(2)}, u32[]{:S(2)}) %collective-permute-start.1) | collective-permute-done | bytes 131104 | tf_op jit(solution)/shard_map/ppermute | solution.py:22
  15.1 3.3 %shard_map.50 = bf16[3,256,256]{2,1,0:T(8,128)(2,1)} custom-call(bf16[3,3,256,256]{3,2,1,0:T(8,128)(2,1)} %bitcast.55, bf16[3,256,256]{2,1,0:T(8,128)(2,1)} %copy-done, bf16[1,256,256]{2,1,0:T(8,128)(2,1)} %collective-permute-done.below_ref, bf16[1,256,256]{2,1,0:T(8,128)(2,1)} %collective-permute-done.1.above_ref), custom_call_target="tpu_custom_call" | custom-call | flops 603979776 | bytes 2228224 | tf_op jit(solution)/shard_map/pallas_call | solution.py:55
  18.4 1.0 fusion.5
  19.4 0.9 slice_dynamic-update-slice_fusion.1
  20.3 0.1 fusion.4
  20.3 0.1 broadcast_select_fusion.1
  20.4 0.1 fusion.9
  20.5 1.0 fusion.6
  21.5 44.5 %all_to_all.20.x_ref = bf16[48,8,640]{2,1,0:T(8,128)(2,1)} all-to-all(bf16[48,8,640]{2,1,0:T(8,128)(2,1)S(1)} %bitcast.53), channel_id=1, replica_groups=mesh['energy'=48,'layer'=16] {'energy'}, dimensions={0} | all-to-all | bytes 983040 | tf_op jit(solution)/shard_map/all_to_all | solution.py:199
  66.0 2.4 %shard_map.51 = (bf16[48,8,384]{2,1,0:T(8,128)(2,1)}, bf16[48,8,384]{2,1,0:T(8,128)(2,1)}) custom-call(bf16[48,8,640]{2,1,0:T(8,128)(2,1)} %all_to_all.20.x_ref), custom_call_target="tpu_custom_call" | custom-call | flops 7225344 | bytes 1179648 | tf_op jit(solution)/shard_map/pallas_call | solution.py:109
  68.4 7.8 %all-to-all-start.1 = ((bf16[48,8,384]{2,1,0:T(8,128)(2,1)}), bf16[48,8,384]{2,1,0:T(8,128)(2,1)S(1)}, u32[]{:S(2)}, u32[]{:S(2)}) async-start(bf16[48,8,384]{2,1,0:T(8,128)(2,1)} %get-tuple-element.4), calls=%async_computation.1 | async-start | bytes 589824 | tf_op jit(solution)/shard_map/all_to_all | solution.py:206
  76.3 16.8 %all-to-all-done.1 = bf16[48,8,384]{2,1,0:T(8,128)(2,1)S(1)} async-done(((bf16[48,8,384]{2,1,0:T(8,128)(2,1)}), bf16[48,8,384]{2,1,0:T(8,128)(2,1)S(1)}, u32[]{:S(2)}, u32[]{:S(2)}) %all-to-all-start.1) | async-done | bytes 294944 | tf_op jit(solution)/shard_map/all_to_all | solution.py:206
  93.1 0.1 copy.9
  93.3 0.1 copy.10
  93.4 0.2 add_convert_fusion.c_ref
  93.6 0.0 copy-start.1
  93.6 1.9 %collective-permute-start.2 = (bf16[1,256,256]{2,1,0:T(8,128)(2,1)S(1)}, bf16[1,256,256]{2,1,0:T(8,128)(2,1)S(1)}, u32[]{:S(2)}, u32[]{:S(2)}) collective-permute-start(bf16[1,256,256]{2,1,0:T(8,128)(2,1)S(1)} %get-tuple-element.12), channel_id=1, source_target_pairs={{0,1},{1,2},{2,3},{3,4},{4,5},{5,6},{6,7},{7,8},{8,9},{9,10},{10,1... | collective-permute-start | bytes 393224 | tf_op jit(solution)/shard_map/ppermute | solution.py:21
  95.5 3.4 %collective-permute-start.3 = (bf16[1,256,256]{2,1,0:T(8,128)(2,1)S(1)}, bf16[1,256,256]{2,1,0:T(8,128)(2,1)S(1)}, u32[]{:S(2)}, u32[]{:S(2)}) collective-permute-start(bf16[1,256,256]{2,1,0:T(8,128)(2,1)S(1)} %get-tuple-element.11), channel_id=1, source_target_pairs={{1,0},{2,1},{3,2},{4,3},{5,4},{6,5},{7,6},{8,7},{9,8},{10,9},{11,1... | collective-permute-start | bytes 393224 | tf_op jit(solution)/shard_map/ppermute | solution.py:22
  98.9 1.2 collective-permute-done.2.below_ref
  100.1 0.0 copy-start.3
  100.2 4.0 %collective-permute-done.3.above_ref = bf16[1,256,256]{2,1,0:T(8,128)(2,1)S(1)} collective-permute-done((bf16[1,256,256]{2,1,0:T(8,128)(2,1)S(1)}, bf16[1,256,256]{2,1,0:T(8,128)(2,1)S(1)}, u32[]{:S(2)}, u32[]{:S(2)}) %collective-permute-start.3) | collective-permute-done | bytes 131104 | tf_op jit(solution)/shard_map/ppermute | solution.py:22
  104.2 0.0 copy-done.1
  104.2 0.0 copy-done.3
  104.2 0.6 copy-done.4
  104.8 3.3 %shard_map.52 = bf16[3,256,256]{2,1,0:T(8,128)(2,1)} custom-call(bf16[3,3,256,256]{3,2,1,0:T(8,128)(2,1)} %bitcast.56, bf16[3,256,256]{2,1,0:T(8,128)(2,1)} %copy-done.1, bf16[1,256,256]{2,1,0:T(8,128)(2,1)} %copy-done.3, bf16[1,256,256]{2,1,0:T(8,128)(2,1)} %copy-done.4), custom_call_target="tpu_custom_call" | custom-call | flops 603979776 | bytes 2228224 | tf_op jit(solution)/shard_map/pallas_call | solution.py:55
  108.1 1.0 slice_select_fusion.1
  109.2 22.4 %all_to_all.21.l_ref = bf16[48,8,384]{2,1,0:T(8,128)(2,1)} all-to-all(bf16[48,8,384]{2,1,0:T(8,128)(2,1)S(1)} %bitcast.52), channel_id=1, replica_groups=mesh['energy'=48,'layer'=16] {'energy'}, dimensions={0} | all-to-all | bytes 589824 | tf_op jit(solution)/shard_map/all_to_all | solution.py:204
  131.6 2.3 %shard_map.53 = bf16[48,8,384]{2,1,0:T(8,128)(2,1)} custom-call(bf16[48,8,384]{2,1,0:T(8,128)(2,1)} %all_to_all.21.l_ref, bf16[48,8,384]{2,1,0:T(8,128)(2,1)} %get-tuple-element.5.s_ref), custom_call_target="tpu_custom_call" | custom-call | flops 7225344 | bytes 1179648 | tf_op jit(solution)/shard_map/pallas_call | solution.py:109
  133.9 24.3 %all_to_all.22 = bf16[48,8,384]{2,1,0:T(8,128)(2,1)S(1)} all-to-all(bf16[48,8,384]{2,1,0:T(8,128)(2,1)} %shard_map.53), channel_id=1, replica_groups=mesh['energy'=48,'layer'=16] {'energy'}, dimensions={0} | all-to-all | bytes 589824 | tf_op jit(solution)/shard_map/all_to_all | solution.py:206
  158.2 0.1 copy.15
  158.3 0.1 copy.14
  158.5 0.8 maximum_bitcast_fusion
  (9 shorter events, 0.2 us)
Async XLA Ops:
  2.1 6.8 %copy-start.2 = (bf16[1,3,256,256]{3,2,1,0:T(8,128)(2,1)S(1)}, bf16[1,3,256,256]{3,2,1,0:T(8,128)(2,1)}, u32[]{:S(2)}) copy-start(bf16[1,3,256,256]{3,2,1,0:T(8,128)(2,1)} %param.5) | copy-start | bytes 1179652
  2.3 4.7 %copy-start = (bf16[3,256,256]{2,1,0:T(8,128)(2,1)}, bf16[3,256,256]{2,1,0:T(8,128)(2,1)S(1)}, u32[]{:S(2)}) copy-start(bf16[3,256,256]{2,1,0:T(8,128)(2,1)S(1)} %fusion.3.c_ref) | copy-start | bytes 1179652
  3.1 6.6 %collective-permute-start = (bf16[1,256,256]{2,1,0:T(8,128)(2,1)}, bf16[1,256,256]{2,1,0:T(8,128)(2,1)}, u32[]{:S(2)}, u32[]{:S(2)}) collective-permute-start(bf16[1,256,256]{2,1,0:T(8,128)(2,1)} %get-tuple-element.18), channel_id=1, source_target_pairs={{0,1},{1,2},{2,3},{3,4},{4,5},{5,6},{6,7},{7,8},{8,9},{9,10},{10,1... | collective-permute-start | bytes 393224 | tf_op jit(solution)/shard_map/ppermute | solution.py:21
  7.0 8.1 %collective-permute-start.1 = (bf16[1,256,256]{2,1,0:T(8,128)(2,1)}, bf16[1,256,256]{2,1,0:T(8,128)(2,1)}, u32[]{:S(2)}, u32[]{:S(2)}) collective-permute-start(bf16[1,256,256]{2,1,0:T(8,128)(2,1)} %get-tuple-element.17), channel_id=1, source_target_pairs={{1,0},{2,1},{3,2},{4,3},{5,4},{6,5},{7,6},{8,7},{9,8},{10,9},{11,1... | collective-permute-start | bytes 393224 | tf_op jit(solution)/shard_map/ppermute | solution.py:22
  68.4 24.7 %all-to-all-start.1 = ((bf16[48,8,384]{2,1,0:T(8,128)(2,1)}), bf16[48,8,384]{2,1,0:T(8,128)(2,1)S(1)}, u32[]{:S(2)}, u32[]{:S(2)}) async-start(bf16[48,8,384]{2,1,0:T(8,128)(2,1)} %get-tuple-element.4), calls=%async_computation.1 | async-start | bytes 589824 | tf_op jit(solution)/shard_map/all_to_all | solution.py:206
  93.6 10.6 %copy-start.1 = (bf16[3,256,256]{2,1,0:T(8,128)(2,1)}, bf16[3,256,256]{2,1,0:T(8,128)(2,1)S(1)}, u32[]{:S(2)}) copy-start(bf16[3,256,256]{2,1,0:T(8,128)(2,1)S(1)} %add_convert_fusion.c_ref) | copy-start | bytes 1179652
  93.6 6.5 %collective-permute-start.2 = (bf16[1,256,256]{2,1,0:T(8,128)(2,1)S(1)}, bf16[1,256,256]{2,1,0:T(8,128)(2,1)S(1)}, u32[]{:S(2)}, u32[]{:S(2)}) collective-permute-start(bf16[1,256,256]{2,1,0:T(8,128)(2,1)S(1)} %get-tuple-element.12), channel_id=1, source_target_pairs={{0,1},{1,2},{2,3},{3,4},{4,5},{5,6},{6,7},{7,8},{8,9},{9,10},{10,1... | collective-permute-start | bytes 393224 | tf_op jit(solution)/shard_map/ppermute | solution.py:21
  95.5 8.6 %collective-permute-start.3 = (bf16[1,256,256]{2,1,0:T(8,128)(2,1)S(1)}, bf16[1,256,256]{2,1,0:T(8,128)(2,1)S(1)}, u32[]{:S(2)}, u32[]{:S(2)}) collective-permute-start(bf16[1,256,256]{2,1,0:T(8,128)(2,1)S(1)} %get-tuple-element.11), channel_id=1, source_target_pairs={{1,0},{2,1},{3,2},{4,3},{5,4},{6,5},{7,6},{8,7},{9,8},{10,9},{11,1... | collective-permute-start | bytes 393224 | tf_op jit(solution)/shard_map/ppermute | solution.py:22
  100.1 4.0 %copy-start.3 = (bf16[1,256,256]{2,1,0:T(8,128)(2,1)}, bf16[1,256,256]{2,1,0:T(8,128)(2,1)S(1)}, u32[]{:S(2)}) copy-start(bf16[1,256,256]{2,1,0:T(8,128)(2,1)S(1)} %collective-permute-done.2.below_ref) | copy-start | bytes 393220
  104.2 0.6 copy-start.4

commit v6 on v5

--- a/solution.py
+++ b/solution.py
@@ -23,8 +23,16 @@
     return below, above
 
 
-def _lesser_kernel(r_ref, c_ref, below_ref, above_ref, o_ref):
+def _lesser_kernel(r_ref, c_ref, below_ref, above_ref, *rest):
+    if len(rest) == 3:
+        screen_ref, o_ref, packed_ref = rest
+    else:
+        screen_ref, (o_ref, packed_ref) = None, rest
     layers = c_ref.shape[0]
+    n = c_ref.shape[-1]
+    h = n // 2
+    rows = lax.broadcasted_iota(jnp.int32, (h, h), 0)
+    cols = lax.broadcasted_iota(jnp.int32, (h, h), 1)
 
     def neighbour(index):
         if index < 0:
@@ -47,20 +55,41 @@
                 preferred_element_type=jnp.float32,
             )
             running = term_part if running is None else running + term_part
-        o_ref[layer] = (0.5 * (running + running.T)).astype(o_ref.dtype)
-
-
-def lesser_blocks(retarded, coupling, below, above):
+        block = (0.5 * (running + running.T)).astype(o_ref.dtype)
+        o_ref[layer] = block
+        top_left = block[:h, :h]
+        bottom_right = block[h:, h:]
+        packed_ref[layer, :, :h] = jnp.where(rows <= cols, top_left, bottom_right)
+        packed_ref[layer, :, h : 2 * h] = block[:h, h:]
+        if screen_ref is None:
+            packed_ref[layer, :, 2 * h :] = jnp.where(
+                rows == cols, bottom_right, jnp.zeros_like(bottom_right)
+            )
+        else:
+            packed_ref[layer, :, 2 * h : 4 * h] = screen_ref[layer, :, : 2 * h]
+            packed_ref[layer, :, 4 * h :] = jnp.where(
+                rows == cols, bottom_right, screen_ref[layer, :, 2 * h :]
+            )
+
+
+def lesser_blocks(retarded, coupling, below, above, screen_packed=None):
     layers, n = coupling.shape[0], coupling.shape[-1]
+    width = 3 * n // 2 if screen_packed is None else 5 * n // 2
+    args = (retarded, coupling, below, above)
+    if screen_packed is not None:
+        args = args + (screen_packed,)
     return pl.pallas_call(
         _lesser_kernel,
-        out_shape=jax.ShapeDtypeStruct(coupling.shape, jnp.bfloat16),
+        out_shape=(
+            jax.ShapeDtypeStruct(coupling.shape, jnp.bfloat16),
+            jax.ShapeDtypeStruct((layers, n // 2, width), jnp.bfloat16),
+        ),
         cost_estimate=pl.CostEstimate(
             flops=layers * 3 * 4 * n * n * n,
-            bytes_accessed=(layers * 3 + layers + 2 + layers) * n * n * 2,
+            bytes_accessed=(layers * 3 + layers + 2 + layers * 2) * n * n * 2,
             transcendentals=0,
         ),
-    )(retarded, coupling, below, above)
+    )(*args)
 
 
 def _conv_core(lf, sf, o_ref, group=4):
@@ -139,15 +168,11 @@
     return jnp.concatenate([folded, blocks[:, :half, half:], diagonal], axis=-1)
 
 
-def pack_symmetric_pair(first, second):
-    half = first.shape[-1] // 2
-    rows = lax.broadcasted_iota(jnp.int32, (half, half), 0)
-    cols = lax.broadcasted_iota(jnp.int32, (half, half), 1)
-    a = pack_symmetric(first)
-    b = pack_symmetric(second)
-    moved = jnp.roll(b[..., 2 * half :], half // 2, axis=-1)
-    shared = jnp.where(rows == cols, a[..., 2 * half :], moved)
-    return jnp.concatenate([a[..., : 2 * half], b[..., : 2 * half], shared], axis=-1)
+def pack_screened(blocks):
+    half = blocks.shape[-1] // 2
+    packed = pack_symmetric(blocks)
+    moved = jnp.roll(packed[..., 2 * half :], half // 2, axis=-1)
+    return jnp.concatenate([packed[..., : 2 * half], moved], axis=-1)
 
 
 def unpack_symmetric(packed):
@@ -176,10 +201,6 @@
     base_part = symmetric(scatter_in[0])
     screened = symmetric(screen[0]).astype(jnp.bfloat16)
 
-    def to_columns(blocks):
-        packed = pack_symmetric(blocks)
-        return packed.reshape(energies, rows, packed.shape[-1])
-
     def to_blocks(columns):
         return unpack_symmetric(columns.reshape(layers, half, columns.shape[-1]))
 
@@ -193,15 +214,17 @@
         else:
             coupling = (base_part + correction).astype(jnp.bfloat16)
         below, above = halo(coupling, "layer")
-        lesser = lesser_blocks(retarded, coupling, below, above)
         if screen_columns is None:
-            both = pack_symmetric_pair(lesser, screened)
+            lesser, both = lesser_blocks(retarded, coupling, below, above, pack_screened(screened))
             both = lax.all_to_all(
                 both.reshape(energies, rows, both.shape[-1]), "energy", 0, 0, tiled=True
             )
             self_columns, screen_columns = energy_convolve_first(both)
         else:
-            lesser_columns = lax.all_to_all(to_columns(lesser), "energy", 0, 0, tiled=True)
+            lesser, packed = lesser_blocks(retarded, coupling, below, above)
+            lesser_columns = lax.all_to_all(
+                packed.reshape(energies, rows, packed.shape[-1]), "energy", 0, 0, tiled=True
+            )
             self_columns = energy_convolve(lesser_columns, screen_columns)
         returned = lax.all_to_all(self_columns, "energy", 0, 0, tiled=True)
         self_blocks = to_blocks(returned)

time: 161 us -> 158 us (0.981)
  waiting for transfers between devices: 27.6 us -> 25.5 us
  other arithmetic: 4.54 us -> 2.82 us
    ppermute x2, waiting for transfers between devices: 9.52 us -> 7.43 us  [halo(): above = lax.ppermute(cells[:1], axis, [(i + 1, i) for i in range(ends)])]
  transfers between devices with their start and end apart: 5 -> 5, of which waited for: 5 -> 4; matrix products, arithmetic and copies ran while one was open for 0% -> 1% of each run, Pallas kernels for 0% -> 0%
where the time goes in v6:
time: 158 us; the launch traced here: 156 us
  blocking collectives  91.6 us (58%)
  waiting for transfers between devices  25.5 us (16%)
  starting transfers between devices  18.9 us (12%)
  Pallas kernels  11.6 us (7%)
  local copies, waits for them, and re-layouts  4.59 us (3%)
  other arithmetic  2.82 us (2%)
    all_to_all x1, blocking collectives, shards(): lax.all_to_all(both.reshape(energies, rows, both.shape[-1]), 'energy', 0,...  45.5 us
    all_to_all x1, blocking collectives, shards(): returned = lax.all_to_all(self_columns, 'energy', 0, 0, tiled=True)  23.9 us
    all_to_all x1, blocking collectives, shards(): lax.all_to_all(packed.reshape(energies, rows, packed.shape[-1]), 'energy'...  22.2 us
    all_to_all x1, waiting for transfers between devices, shards(): returned = lax.all_to_all(self_columns, 'energy', 0, 0, tiled=True)  16.9 us
    all_to_all x1, starting transfers between devices, shards(): returned = lax.all_to_all(self_columns, 'energy', 0, 0, tiled=True)  7.83 us
    ppermute x2, waiting for transfers between devices, halo(): above = lax.ppermute(cells[:1], axis, [(i + 1, i) for i in range(ends)])  7.43 us
    pallas_call x2, Pallas kernels, lesser_blocks(): pl.pallas_call(_lesser_kernel, out_shape=(jax.ShapeDtypeStruct(coupling.s...  6.94 us
    ppermute x2, starting transfers between devices, halo(): below = lax.ppermute(cells[-1:], axis, [(i, i + 1) for i in range(ends)])  5.82 us
  transfers between devices with their start and end apart: 5, of which 4 were waited for; matrix products, arithmetic and copies ran while one was open for 1% of the time, Pallas kernels for 0%

profile of v6, /device:TPU:7, one launch (start us, length us, event | category | flops | bytes accessed | tf_op | source)
XLA Modules:
  0.0 155.9 jit_solution(17352509728405095983)
XLA Ops:
  0.6 1.2 copy.5
  1.8 0.1 bitcast_convert_fusion.1
  1.9 0.3 copy.6
  2.1 0.0 copy-start.2
  2.2 0.1 fusion.3.c_ref
  2.3 0.0 copy-start
  2.3 0.8 fusion.5
  3.1 3.9 %collective-permute-start = (bf16[1,256,256]{2,1,0:T(8,128)(2,1)}, bf16[1,256,256]{2,1,0:T(8,128)(2,1)}, u32[]{:S(2)}, u32[]{:S(2)}) collective-permute-start(bf16[1,256,256]{2,1,0:T(8,128)(2,1)} %get-tuple-element.22), channel_id=1, source_target_pairs={{0,1},{1,2},{2,3},{3,4},{4,5},{5,6},{6,7},{7,8},{8,9},{9,10},{10,1... | collective-permute-start | bytes 393224 | tf_op jit(solution)/shard_map/ppermute | solution.py:21
  7.0 1.9 %collective-permute-start.1 = (bf16[1,256,256]{2,1,0:T(8,128)(2,1)}, bf16[1,256,256]{2,1,0:T(8,128)(2,1)}, u32[]{:S(2)}, u32[]{:S(2)}) collective-permute-start(bf16[1,256,256]{2,1,0:T(8,128)(2,1)} %get-tuple-element.21), channel_id=1, source_target_pairs={{1,0},{2,1},{3,2},{4,3},{5,4},{6,5},{7,6},{8,7},{9,8},{10,9},{11,1... | collective-permute-start | bytes 393224 | tf_op jit(solution)/shard_map/ppermute | solution.py:22
  8.9 0.6 iota_compare_fusion.1
  9.5 0.0 copy-done.2
  9.5 0.2 copy.7
  9.7 0.1 bitcast_convert_fusion
  9.8 0.0 copy-done
  9.8 0.3 copy.8
  10.1 0.0 copy-start.3
  10.1 0.1 fusion.1
  10.2 0.6 copy-done.3
  10.8 0.1 fusion.6
  10.9 0.8 pad_maximum_fusion.rest_0_
  11.7 0.0 collective-permute-done.below_ref
  11.7 3.4 %collective-permute-done.1.above_ref = bf16[1,256,256]{2,1,0:T(8,128)(2,1)} collective-permute-done((bf16[1,256,256]{2,1,0:T(8,128)(2,1)}, bf16[1,256,256]{2,1,0:T(8,128)(2,1)}, u32[]{:S(2)}, u32[]{:S(2)}) %collective-permute-start.1) | collective-permute-done | bytes 131104 | tf_op jit(solution)/shard_map/ppermute | solution.py:22
  15.1 3.6 %shard_map.50 = (bf16[3,256,256]{2,1,0:T(8,128)(2,1)}, bf16[3,128,640]{2,1,0:T(8,128)(2,1)}) custom-call(bf16[3,3,256,256]{3,2,1,0:T(8,128)(2,1)} %bitcast.54, bf16[3,256,256]{2,1,0:T(8,128)(2,1)} %copy-done, bf16[1,256,256]{2,1,0:T(8,128)(2,1)} %collective-permute-done.below_ref, bf16[1,256,256]{2,1,0:T(8,128)(2,1)} %collective-permute-done.1.above_ref, ...), custom_call_target="tpu_custom_call" | custom-call | flops 603979776 | bytes 2621440 | tf_op jit(solution)/shard_map/pallas_call | solution.py:81
  18.7 45.5 %all_to_all.20.x_ref = bf16[48,8,640]{2,1,0:T(8,128)(2,1)} all-to-all(bf16[48,8,640]{2,1,0:T(8,128)(2,1)} %bitcast.52), channel_id=1, replica_groups=mesh['energy'=48,'layer'=16] {'energy'}, dimensions={0} | all-to-all | bytes 983040 | tf_op jit(solution)/shard_map/all_to_all | solution.py:219
  64.2 2.4 %shard_map.51 = (bf16[48,8,384]{2,1,0:T(8,128)(2,1)}, bf16[48,8,384]{2,1,0:T(8,128)(2,1)}) custom-call(bf16[48,8,640]{2,1,0:T(8,128)(2,1)} %all_to_all.20.x_ref), custom_call_target="tpu_custom_call" | custom-call | flops 7225344 | bytes 1179648 | tf_op jit(solution)/shard_map/pallas_call | solution.py:138
  66.5 7.8 %all-to-all-start.1 = ((bf16[48,8,384]{2,1,0:T(8,128)(2,1)}), bf16[48,8,384]{2,1,0:T(8,128)(2,1)S(1)}, u32[]{:S(2)}, u32[]{:S(2)}) async-start(bf16[48,8,384]{2,1,0:T(8,128)(2,1)} %get-tuple-element.8), calls=%async_computation.1 | async-start | bytes 589824 | tf_op jit(solution)/shard_map/all_to_all | solution.py:229
  74.4 16.9 %all-to-all-done.1 = bf16[48,8,384]{2,1,0:T(8,128)(2,1)S(1)} async-done(((bf16[48,8,384]{2,1,0:T(8,128)(2,1)}), bf16[48,8,384]{2,1,0:T(8,128)(2,1)S(1)}, u32[]{:S(2)}, u32[]{:S(2)}) %all-to-all-start.1) | async-done | bytes 294944 | tf_op jit(solution)/shard_map/all_to_all | solution.py:229
  91.3 0.1 copy.9
  91.5 0.1 copy.10
  91.6 0.2 add_convert_fusion.c_ref
  91.8 0.0 copy-start.1
  91.8 1.9 %collective-permute-start.2 = (bf16[1,256,256]{2,1,0:T(8,128)(2,1)S(1)}, bf16[1,256,256]{2,1,0:T(8,128)(2,1)S(1)}, u32[]{:S(2)}, u32[]{:S(2)}) collective-permute-start(bf16[1,256,256]{2,1,0:T(8,128)(2,1)S(1)} %get-tuple-element.15), channel_id=1, source_target_pairs={{0,1},{1,2},{2,3},{3,4},{4,5},{5,6},{6,7},{7,8},{8,9},{9,10},{10,1... | collective-permute-start | bytes 393224 | tf_op jit(solution)/shard_map/ppermute | solution.py:21
  93.7 3.4 %collective-permute-start.3 = (bf16[1,256,256]{2,1,0:T(8,128)(2,1)S(1)}, bf16[1,256,256]{2,1,0:T(8,128)(2,1)S(1)}, u32[]{:S(2)}, u32[]{:S(2)}) collective-permute-start(bf16[1,256,256]{2,1,0:T(8,128)(2,1)S(1)} %get-tuple-element.14), channel_id=1, source_target_pairs={{1,0},{2,1},{3,2},{4,3},{5,4},{6,5},{7,6},{8,7},{9,8},{10,9},{11,1... | collective-permute-start | bytes 393224 | tf_op jit(solution)/shard_map/ppermute | solution.py:22
  97.1 1.2 collective-permute-done.2.below_ref
  98.3 0.0 copy-start.4
  98.3 4.0 %collective-permute-done.3.above_ref = bf16[1,256,256]{2,1,0:T(8,128)(2,1)S(1)} collective-permute-done((bf16[1,256,256]{2,1,0:T(8,128)(2,1)S(1)}, bf16[1,256,256]{2,1,0:T(8,128)(2,1)S(1)}, u32[]{:S(2)}, u32[]{:S(2)}) %collective-permute-start.3) | collective-permute-done | bytes 131104 | tf_op jit(solution)/shard_map/ppermute | solution.py:22
  102.3 0.0 copy-done.1
  102.3 0.0 copy-done.4
  102.3 0.0 copy-start.5
  102.3 0.6 copy-done.5
  103.0 3.4 %shard_map.52 = (bf16[3,256,256]{2,1,0:T(8,128)(2,1)}, bf16[3,128,384]{2,1,0:T(8,128)(2,1)}) custom-call(bf16[3,3,256,256]{3,2,1,0:T(8,128)(2,1)} %bitcast.55, bf16[3,256,256]{2,1,0:T(8,128)(2,1)} %copy-done.1, bf16[1,256,256]{2,1,0:T(8,128)(2,1)} %copy-done.4, bf16[1,256,256]{2,1,0:T(8,128)(2,1)} %copy-done.5), custom_call_target="tpu_custom_call" | custom-call | flops 603979776 | bytes 2621440 | tf_op jit(solution)/shard_map/pallas_call | solution.py:81
  106.3 22.2 %all_to_all.21.l_ref = bf16[48,8,384]{2,1,0:T(8,128)(2,1)} all-to-all(bf16[48,8,384]{2,1,0:T(8,128)(2,1)} %bitcast.53), channel_id=1, replica_groups=mesh['energy'=48,'layer'=16] {'energy'}, dimensions={0} | all-to-all | bytes 589824 | tf_op jit(solution)/shard_map/all_to_all | solution.py:225
  128.5 2.3 %shard_map.53 = bf16[48,8,384]{2,1,0:T(8,128)(2,1)} custom-call(bf16[48,8,384]{2,1,0:T(8,128)(2,1)} %all_to_all.21.l_ref, bf16[48,8,384]{2,1,0:T(8,128)(2,1)} %get-tuple-element.11.s_ref), custom_call_target="tpu_custom_call" | custom-call | flops 7225344 | bytes 1179648 | tf_op jit(solution)/shard_map/pallas_call | solution.py:138
  130.8 23.9 %all_to_all.22 = bf16[48,8,384]{2,1,0:T(8,128)(2,1)S(1)} all-to-all(bf16[48,8,384]{2,1,0:T(8,128)(2,1)} %shard_map.53), channel_id=1, replica_groups=mesh['energy'=48,'layer'=16] {'energy'}, dimensions={0} | all-to-all | bytes 589824 | tf_op jit(solution)/shard_map/all_to_all | solution.py:229
  154.8 0.1 copy.15
  154.9 0.1 copy.14
  155.1 0.8 maximum_bitcast_fusion
  (7 shorter events, 0.2 us)
Async XLA Ops:
  2.1 7.4 %copy-start.2 = (bf16[1,3,256,256]{3,2,1,0:T(8,128)(2,1)S(1)}, bf16[1,3,256,256]{3,2,1,0:T(8,128)(2,1)}, u32[]{:S(2)}) copy-start(bf16[1,3,256,256]{3,2,1,0:T(8,128)(2,1)} %param.5) | copy-start | bytes 1179652
  2.3 7.5 %copy-start = (bf16[3,256,256]{2,1,0:T(8,128)(2,1)}, bf16[3,256,256]{2,1,0:T(8,128)(2,1)S(1)}, u32[]{:S(2)}) copy-start(bf16[3,256,256]{2,1,0:T(8,128)(2,1)S(1)} %fusion.3.c_ref) | copy-start | bytes 1179652
  3.1 8.7 %collective-permute-start = (bf16[1,256,256]{2,1,0:T(8,128)(2,1)}, bf16[1,256,256]{2,1,0:T(8,128)(2,1)}, u32[]{:S(2)}, u32[]{:S(2)}) collective-permute-start(bf16[1,256,256]{2,1,0:T(8,128)(2,1)} %get-tuple-element.22), channel_id=1, source_target_pairs={{0,1},{1,2},{2,3},{3,4},{4,5},{5,6},{6,7},{7,8},{8,9},{9,10},{10,1... | collective-permute-start | bytes 393224 | tf_op jit(solution)/shard_map/ppermute | solution.py:21
  7.0 8.1 %collective-permute-start.1 = (bf16[1,256,256]{2,1,0:T(8,128)(2,1)}, bf16[1,256,256]{2,1,0:T(8,128)(2,1)}, u32[]{:S(2)}, u32[]{:S(2)}) collective-permute-start(bf16[1,256,256]{2,1,0:T(8,128)(2,1)} %get-tuple-element.21), channel_id=1, source_target_pairs={{1,0},{2,1},{3,2},{4,3},{5,4},{6,5},{7,6},{8,7},{9,8},{10,9},{11,1... | collective-permute-start | bytes 393224 | tf_op jit(solution)/shard_map/ppermute | solution.py:22
  10.1 0.7 copy-start.3
  66.5 24.7 %all-to-all-start.1 = ((bf16[48,8,384]{2,1,0:T(8,128)(2,1)}), bf16[48,8,384]{2,1,0:T(8,128)(2,1)S(1)}, u32[]{:S(2)}, u32[]{:S(2)}) async-start(bf16[48,8,384]{2,1,0:T(8,128)(2,1)} %get-tuple-element.8), calls=%async_computation.1 | async-start | bytes 589824 | tf_op jit(solution)/shard_map/all_to_all | solution.py:229
  91.8 10.6 %copy-start.1 = (bf16[3,256,256]{2,1,0:T(8,128)(2,1)}, bf16[3,256,256]{2,1,0:T(8,128)(2,1)S(1)}, u32[]{:S(2)}) copy-start(bf16[3,256,256]{2,1,0:T(8,128)(2,1)S(1)} %add_convert_fusion.c_ref) | copy-start | bytes 1179652
  91.8 6.5 %collective-permute-start.2 = (bf16[1,256,256]{2,1,0:T(8,128)(2,1)S(1)}, bf16[1,256,256]{2,1,0:T(8,128)(2,1)S(1)}, u32[]{:S(2)}, u32[]{:S(2)}) collective-permute-start(bf16[1,256,256]{2,1,0:T(8,128)(2,1)S(1)} %get-tuple-element.15), channel_id=1, source_target_pairs={{0,1},{1,2},{2,3},{3,4},{4,5},{5,6},{6,7},{7,8},{8,9},{9,10},{10,1... | collective-permute-start | bytes 393224 | tf_op jit(solution)/shard_map/ppermute | solution.py:21
  93.7 8.6 %collective-permute-start.3 = (bf16[1,256,256]{2,1,0:T(8,128)(2,1)S(1)}, bf16[1,256,256]{2,1,0:T(8,128)(2,1)S(1)}, u32[]{:S(2)}, u32[]{:S(2)}) collective-permute-start(bf16[1,256,256]{2,1,0:T(8,128)(2,1)S(1)} %get-tuple-element.14), channel_id=1, source_target_pairs={{1,0},{2,1},{3,2},{4,3},{5,4},{6,5},{7,6},{8,7},{9,8},{10,9},{11,1... | collective-permute-start | bytes 393224 | tf_op jit(solution)/shard_map/ppermute | solution.py:22
  98.3 4.0 %copy-start.4 = (bf16[1,256,256]{2,1,0:T(8,128)(2,1)}, bf16[1,256,256]{2,1,0:T(8,128)(2,1)S(1)}, u32[]{:S(2)}) copy-start(bf16[1,256,256]{2,1,0:T(8,128)(2,1)S(1)} %collective-permute-done.2.below_ref) | copy-start | bytes 393220
  102.3 0.6 copy-start.5

commit v7 on v6

--- a/solution.py
+++ b/solution.py
@@ -213,7 +213,12 @@
             coupling = base_part.astype(jnp.bfloat16)
         else:
             coupling = (base_part + correction).astype(jnp.bfloat16)
-        below, above = halo(coupling, "layer")
+        if screen_columns is None:
+            below, above = halo(scatter_in[0], "layer")
+            below = symmetric(below).astype(jnp.bfloat16)
+            above = symmetric(above).astype(jnp.bfloat16)
+        else:
+            below, above = halo(coupling, "layer")
         if screen_columns is None:
             lesser, both = lesser_blocks(retarded, coupling, below, above, pack_screened(screened))
             both = lax.all_to_all(

time: 158 us -> 160 us (1.013)
  other arithmetic: 2.82 us -> 6.73 us
  waiting for transfers between devices: 25.5 us -> 22.2 us
    ppermute x2, waiting for transfers between devices: 7.43 us -> 4.04 us  [halo(): above = lax.ppermute(cells[:1], axis, [(i + 1, i) for i in range(ends)])]
    convert_element_type x0 -> x2, other arithmetic: none -> 3.17 us  [the longest x1 1.58 us: shards(): above = symmetric(above).astype(jnp.bfloat16)]
    convert_element_type x2 -> x4, local copies, waits for them, and re-layouts: 0.53 us -> 2.53 us  [symmetric(): matrix = matrix.astype(jnp.float32)]
  transfers between devices with their start and end apart: 5 -> 5, of which waited for: 4 -> 3; matrix products, arithmetic and copies ran while one was open for 1% -> 4% of each run, Pallas kernels for 0% -> 0%
where the time goes in v7:
time: 160 us; the launch traced here: 159 us
  blocking collectives  91 us (57%)
  waiting for transfers between devices  22.2 us (14%)
  starting transfers between devices  20.4 us (13%)
  Pallas kernels  11.6 us (7%)
  other arithmetic  6.73 us (4%)
  local copies, waits for them, and re-layouts  5.95 us (4%)
    all_to_all x1, blocking collectives, shards(): lax.all_to_all(both.reshape(energies, rows, both.shape[-1]), 'energy', 0,...  45.5 us
    all_to_all x1, blocking collectives, shards(): returned = lax.all_to_all(self_columns, 'energy', 0, 0, tiled=True)  23.8 us
    all_to_all x1, blocking collectives, shards(): lax.all_to_all(packed.reshape(energies, rows, packed.shape[-1]), 'energy'...  21.7 us
    all_to_all x1, waiting for transfers between devices, shards(): returned = lax.all_to_all(self_columns, 'energy', 0, 0, tiled=True)  16.9 us
    all_to_all x1, starting transfers between devices, shards(): returned = lax.all_to_all(self_columns, 'energy', 0, 0, tiled=True)  7.74 us
    pallas_call x2, Pallas kernels, lesser_blocks(): pl.pallas_call(_lesser_kernel, out_shape=(jax.ShapeDtypeStruct(coupling.s...  6.95 us
    ppermute x2, starting transfers between devices, halo(): below = lax.ppermute(cells[-1:], axis, [(i, i + 1) for i in range(ends)])  6.86 us
    ppermute x2, starting transfers between devices, halo(): above = lax.ppermute(cells[:1], axis, [(i + 1, i) for i in range(ends)])  5.81 us
  transfers between devices with their start and end apart: 5, of which 3 were waited for; matrix products, arithmetic and copies ran while one was open for 4% of the time, Pallas kernels for 0%

profile of v7, /device:TPU:7, one launch (start us, length us, event | category | flops | bytes accessed | tf_op | source)
XLA Modules:
  0.0 158.7 jit_solution(11901368969349570625)
XLA Ops:
  0.6 0.0 copy-start.1
  0.6 1.2 copy.5
  1.9 0.7 slice_bitcast_fusion
  2.6 2.4 %collective-permute-start.1 = (bf16[1,256,256]{1,2,0:T(8,128)(2,1)}, bf16[1,256,256]{1,2,0:T(8,128)(2,1)}, u32[]{:S(2)}, u32[]{:S(2)}) collective-permute-start(bf16[1,256,256]{1,2,0:T(8,128)(2,1)} %get-tuple-element.21), channel_id=1, source_target_pairs={{1,0},{2,1},{3,2},{4,3},{5,4},{6,5},{7,6},{8,7},{9,8},{10,9},{11,1... | collective-permute-start | bytes 393224 | tf_op jit(solution)/shard_map/ppermute | solution.py:22
  5.0 4.9 %collective-permute-start = (bf16[1,256,256]{1,2,0:T(8,128)(2,1)}, bf16[1,256,256]{1,2,0:T(8,128)(2,1)}, u32[]{:S(2)}, u32[]{:S(2)}) collective-permute-start(bf16[1,256,256]{1,2,0:T(8,128)(2,1)} %get-tuple-element.22), channel_id=1, source_target_pairs={{0,1},{1,2},{2,3},{3,4},{4,5},{5,6},{6,7},{7,8},{8,9},{9,10},{10,1... | collective-permute-start | bytes 393224 | tf_op jit(solution)/shard_map/ppermute | solution.py:21
  10.0 0.6 iota_compare_fusion.1
  10.6 0.1 bitcast_convert_fusion.1
  10.7 0.0 copy-done.1
  10.7 0.2 copy.11
  10.8 0.1 bitcast_convert_fusion
  10.9 0.3 copy.12
  11.2 0.1 fusion.1
  11.3 0.3 copy.6
  11.6 0.0 copy-start.2
  11.6 0.8 fusion.3.c_ref
  12.4 0.0 copy-done.2
  12.4 0.1 fusion.9
  12.5 0.8 pad_maximum_fusion.rest_0_
  13.4 0.0 collective-permute-done.1
  13.4 1.0 copy.10
  14.4 1.6 fusion.5.above_ref
  16.0 0.0 collective-permute-done
  16.0 1.0 copy.8
  17.0 1.6 fusion.7.below_ref
  18.6 3.6 %shard_map.50 = (bf16[3,256,256]{2,1,0:T(8,128)(2,1)}, bf16[3,128,640]{2,1,0:T(8,128)(2,1)}) custom-call(bf16[3,3,256,256]{3,2,1,0:T(8,128)(2,1)} %bitcast.70, bf16[3,256,256]{2,1,0:T(8,128)(2,1)} %fusion.3.c_ref, bf16[1,256,256]{2,1,0:T(8,128)(2,1)} %fusion.7.below_ref, bf16[1,256,256]{2,1,0:T(8,128)(2,1)} %fusion.5.above_ref, ...), custom_call_target="tpu_custom_call" | custom-call | flops 603979776 | bytes 2621440 | tf_op jit(solution)/shard_map/pallas_call | solution.py:81
  22.1 45.5 %all_to_all.20.x_ref = bf16[48,8,640]{2,1,0:T(8,128)(2,1)} all-to-all(bf16[48,8,640]{2,1,0:T(8,128)(2,1)} %bitcast.68), channel_id=1, replica_groups=mesh['energy'=48,'layer'=16] {'energy'}, dimensions={0} | all-to-all | bytes 983040 | tf_op jit(solution)/shard_map/all_to_all | solution.py:224
  67.6 2.4 %shard_map.51 = (bf16[48,8,384]{2,1,0:T(8,128)(2,1)}, bf16[48,8,384]{2,1,0:T(8,128)(2,1)}) custom-call(bf16[48,8,640]{2,1,0:T(8,128)(2,1)} %all_to_all.20.x_ref), custom_call_target="tpu_custom_call" | custom-call | flops 7225344 | bytes 1179648 | tf_op jit(solution)/shard_map/pallas_call | solution.py:138
  70.0 7.7 %all-to-all-start.1 = ((bf16[48,8,384]{2,1,0:T(8,128)(2,1)}), bf16[48,8,384]{2,1,0:T(8,128)(2,1)S(1)}, u32[]{:S(2)}, u32[]{:S(2)}) async-start(bf16[48,8,384]{2,1,0:T(8,128)(2,1)} %get-tuple-element.8), calls=%async_computation.1 | async-start | bytes 589824 | tf_op jit(solution)/shard_map/all_to_all | solution.py:234
  77.7 16.9 %all-to-all-done.1 = bf16[48,8,384]{2,1,0:T(8,128)(2,1)S(1)} async-done(((bf16[48,8,384]{2,1,0:T(8,128)(2,1)}), bf16[48,8,384]{2,1,0:T(8,128)(2,1)S(1)}, u32[]{:S(2)}, u32[]{:S(2)}) %all-to-all-start.1) | async-done | bytes 294944 | tf_op jit(solution)/shard_map/all_to_all | solution.py:234
  94.7 0.1 copy.13
  94.8 0.1 copy.14
  95.0 0.2 add_convert_fusion.c_ref
  95.1 0.0 copy-start
  95.2 1.9 %collective-permute-start.2 = (bf16[1,256,256]{2,1,0:T(8,128)(2,1)S(1)}, bf16[1,256,256]{2,1,0:T(8,128)(2,1)S(1)}, u32[]{:S(2)}, u32[]{:S(2)}) collective-permute-start(bf16[1,256,256]{2,1,0:T(8,128)(2,1)S(1)} %get-tuple-element.15), channel_id=1, source_target_pairs={{0,1},{1,2},{2,3},{3,4},{4,5},{5,6},{6,7},{7,8},{8,9},{9,10},{10,1... | collective-permute-start | bytes 393224 | tf_op jit(solution)/shard_map/ppermute | solution.py:21
  97.1 3.4 %collective-permute-start.3 = (bf16[1,256,256]{2,1,0:T(8,128)(2,1)S(1)}, bf16[1,256,256]{2,1,0:T(8,128)(2,1)S(1)}, u32[]{:S(2)}, u32[]{:S(2)}) collective-permute-start(bf16[1,256,256]{2,1,0:T(8,128)(2,1)S(1)} %get-tuple-element.14), channel_id=1, source_target_pairs={{1,0},{2,1},{3,2},{4,3},{5,4},{6,5},{7,6},{8,7},{9,8},{10,9},{11,1... | collective-permute-start | bytes 393224 | tf_op jit(solution)/shard_map/ppermute | solution.py:22
  100.5 1.3 collective-permute-done.2.below_ref
  101.7 0.0 copy-start.3
  101.7 4.0 %collective-permute-done.3.above_ref = bf16[1,256,256]{2,1,0:T(8,128)(2,1)S(1)} collective-permute-done((bf16[1,256,256]{2,1,0:T(8,128)(2,1)S(1)}, bf16[1,256,256]{2,1,0:T(8,128)(2,1)S(1)}, u32[]{:S(2)}, u32[]{:S(2)}) %collective-permute-start.3) | collective-permute-done | bytes 131104 | tf_op jit(solution)/shard_map/ppermute | solution.py:22
  105.8 0.0 copy-done
  105.8 0.0 copy-done.3
  105.8 0.7 copy-done.4
  106.4 3.4 %shard_map.52 = (bf16[3,256,256]{2,1,0:T(8,128)(2,1)}, bf16[3,128,384]{2,1,0:T(8,128)(2,1)}) custom-call(bf16[3,3,256,256]{3,2,1,0:T(8,128)(2,1)} %bitcast.71, bf16[3,256,256]{2,1,0:T(8,128)(2,1)} %copy-done, bf16[1,256,256]{2,1,0:T(8,128)(2,1)} %copy-done.3, bf16[1,256,256]{2,1,0:T(8,128)(2,1)} %copy-done.4), custom_call_target="tpu_custom_call" | custom-call | flops 603979776 | bytes 2621440 | tf_op jit(solution)/shard_map/pallas_call | solution.py:81
  109.8 21.7 %all_to_all.21.l_ref = bf16[48,8,384]{2,1,0:T(8,128)(2,1)} all-to-all(bf16[48,8,384]{2,1,0:T(8,128)(2,1)} %bitcast.69), channel_id=1, replica_groups=mesh['energy'=48,'layer'=16] {'energy'}, dimensions={0} | all-to-all | bytes 589824 | tf_op jit(solution)/shard_map/all_to_all | solution.py:230
  131.5 2.3 %shard_map.53 = bf16[48,8,384]{2,1,0:T(8,128)(2,1)} custom-call(bf16[48,8,384]{2,1,0:T(8,128)(2,1)} %all_to_all.21.l_ref, bf16[48,8,384]{2,1,0:T(8,128)(2,1)} %get-tuple-element.11.s_ref), custom_call_target="tpu_custom_call" | custom-call | flops 7225344 | bytes 1179648 | tf_op jit(solution)/shard_map/pallas_call | solution.py:138
  133.8 23.8 %all_to_all.22 = bf16[48,8,384]{2,1,0:T(8,128)(2,1)S(1)} all-to-all(bf16[48,8,384]{2,1,0:T(8,128)(2,1)} %shard_map.53), channel_id=1, replica_groups=mesh['energy'=48,'layer'=16] {'energy'}, dimensions={0} | all-to-all | bytes 589824 | tf_op jit(solution)/shard_map/all_to_all | solution.py:234
  157.6 0.1 copy.19
  157.8 0.1 copy.18
  157.9 0.8 maximum_bitcast_fusion
  (8 shorter events, 0.2 us)
Async XLA Ops:
  0.6 10.0 %copy-start.1 = (bf16[1,3,256,256]{3,2,1,0:T(8,128)(2,1)S(1)}, bf16[1,3,256,256]{3,2,1,0:T(8,128)(2,1)}, u32[]{:S(2)}) copy-start(bf16[1,3,256,256]{3,2,1,0:T(8,128)(2,1)} %param.5) | copy-start | bytes 1179652
  2.6 10.8 %collective-permute-start.1 = (bf16[1,256,256]{1,2,0:T(8,128)(2,1)}, bf16[1,256,256]{1,2,0:T(8,128)(2,1)}, u32[]{:S(2)}, u32[]{:S(2)}) collective-permute-start(bf16[1,256,256]{1,2,0:T(8,128)(2,1)} %get-tuple-element.21), channel_id=1, source_target_pairs={{1,0},{2,1},{3,2},{4,3},{5,4},{6,5},{7,6},{8,7},{9,8},{10,9},{11,1... | collective-permute-start | bytes 393224 | tf_op jit(solution)/shard_map/ppermute | solution.py:22
  5.0 10.9 %collective-permute-start = (bf16[1,256,256]{1,2,0:T(8,128)(2,1)}, bf16[1,256,256]{1,2,0:T(8,128)(2,1)}, u32[]{:S(2)}, u32[]{:S(2)}) collective-permute-start(bf16[1,256,256]{1,2,0:T(8,128)(2,1)} %get-tuple-element.22), channel_id=1, source_target_pairs={{0,1},{1,2},{2,3},{3,4},{4,5},{5,6},{6,7},{7,8},{8,9},{9,10},{10,1... | collective-permute-start | bytes 393224 | tf_op jit(solution)/shard_map/ppermute | solution.py:21
  11.6 0.9 copy-start.2
  70.0 24.7 %all-to-all-start.1 = ((bf16[48,8,384]{2,1,0:T(8,128)(2,1)}), bf16[48,8,384]{2,1,0:T(8,128)(2,1)S(1)}, u32[]{:S(2)}, u32[]{:S(2)}) async-start(bf16[48,8,384]{2,1,0:T(8,128)(2,1)} %get-tuple-element.8), calls=%async_computation.1 | async-start | bytes 589824 | tf_op jit(solution)/shard_map/all_to_all | solution.py:234
  95.1 10.7 %copy-start = (bf16[3,256,256]{2,1,0:T(8,128)(2,1)}, bf16[3,256,256]{2,1,0:T(8,128)(2,1)S(1)}, u32[]{:S(2)}) copy-start(bf16[3,256,256]{2,1,0:T(8,128)(2,1)S(1)} %add_convert_fusion.c_ref) | copy-start | bytes 1179652
  95.2 6.6 %collective-permute-start.2 = (bf16[1,256,256]{2,1,0:T(8,128)(2,1)S(1)}, bf16[1,256,256]{2,1,0:T(8,128)(2,1)S(1)}, u32[]{:S(2)}, u32[]{:S(2)}) collective-permute-start(bf16[1,256,256]{2,1,0:T(8,128)(2,1)S(1)} %get-tuple-element.15), channel_id=1, source_target_pairs={{0,1},{1,2},{2,3},{3,4},{4,5},{5,6},{6,7},{7,8},{8,9},{9,10},{10,1... | collective-permute-start | bytes 393224 | tf_op jit(solution)/shard_map/ppermute | solution.py:21
  97.1 8.7 %collective-permute-start.3 = (bf16[1,256,256]{2,1,0:T(8,128)(2,1)S(1)}, bf16[1,256,256]{2,1,0:T(8,128)(2,1)S(1)}, u32[]{:S(2)}, u32[]{:S(2)}) collective-permute-start(bf16[1,256,256]{2,1,0:T(8,128)(2,1)S(1)} %get-tuple-element.14), channel_id=1, source_target_pairs={{1,0},{2,1},{3,2},{4,3},{5,4},{6,5},{7,6},{8,7},{9,8},{10,9},{11,1... | collective-permute-start | bytes 393224 | tf_op jit(solution)/shard_map/ppermute | solution.py:22
  101.7 4.0 %copy-start.3 = (bf16[1,256,256]{2,1,0:T(8,128)(2,1)}, bf16[1,256,256]{2,1,0:T(8,128)(2,1)S(1)}, u32[]{:S(2)}) copy-start(bf16[1,256,256]{2,1,0:T(8,128)(2,1)S(1)} %collective-permute-done.2.below_ref) | copy-start | bytes 393220
  105.8 0.7 copy-start.4

commit v8 on v6

--- a/solution.py
+++ b/solution.py
@@ -23,38 +23,52 @@
     return below, above
 
 
-def _lesser_kernel(r_ref, c_ref, below_ref, above_ref, *rest):
+def _interior_kernel(r_ref, c_ref, o_ref):
+    layers = c_ref.shape[0]
+    for layer in range(layers):
+        running = None
+        for offset in range(3):
+            index = layer + offset - 1
+            if 0 <= index < layers:
+                factor = r_ref[layer, offset]
+                left_part = jnp.dot(
+                    factor, c_ref[index], preferred_element_type=jnp.float32
+                ).astype(jnp.bfloat16)
+                term_part = lax.dot_general(
+                    left_part,
+                    factor,
+                    (((1,), (1,)), ((), ())),
+                    preferred_element_type=jnp.float32,
+                )
+                running = term_part if running is None else running + term_part
+        o_ref[layer] = running
+
+
+def _lesser_kernel(part_ref, r_edge_ref, below_ref, above_ref, *rest):
     if len(rest) == 3:
         screen_ref, o_ref, packed_ref = rest
     else:
         screen_ref, (o_ref, packed_ref) = None, rest
-    layers = c_ref.shape[0]
-    n = c_ref.shape[-1]
+    layers = part_ref.shape[0]
+    n = part_ref.shape[-1]
     h = n // 2
     rows = lax.broadcasted_iota(jnp.int32, (h, h), 0)
     cols = lax.broadcasted_iota(jnp.int32, (h, h), 1)
 
-    def neighbour(index):
-        if index < 0:
-            return below_ref[0]
-        if index >= layers:
-            return above_ref[0]
-        return c_ref[index]
+    def edge_term(factor, neighbour):
+        left_part = jnp.dot(factor, neighbour, preferred_element_type=jnp.float32).astype(
+            jnp.bfloat16
+        )
+        return lax.dot_general(
+            left_part, factor, (((1,), (1,)), ((), ())), preferred_element_type=jnp.float32
+        )
 
     for layer in range(layers):
-        running = None
-        for offset in range(3):
-            factor = r_ref[layer, offset]
-            left_part = jnp.dot(
-                factor, neighbour(layer + offset - 1), preferred_element_type=jnp.float32
-            ).astype(jnp.bfloat16)
-            term_part = lax.dot_general(
-                left_part,
-                factor,
-                (((1,), (1,)), ((), ())),
-                preferred_element_type=jnp.float32,
-            )
-            running = term_part if running is None else running + term_part
+        running = part_ref[layer]
+        if layer == 0:
+            running = running + edge_term(r_edge_ref[0], below_ref[0])
+        if layer == layers - 1:
+            running = running + edge_term(r_edge_ref[1], above_ref[0])
         block = (0.5 * (running + running.T)).astype(o_ref.dtype)
         o_ref[layer] = block
         top_left = block[:h, :h]
@@ -74,8 +88,18 @@
 
 def lesser_blocks(retarded, coupling, below, above, screen_packed=None):
     layers, n = coupling.shape[0], coupling.shape[-1]
+    interior = pl.pallas_call(
+        _interior_kernel,
+        out_shape=jax.ShapeDtypeStruct(coupling.shape, jnp.float32),
+        cost_estimate=pl.CostEstimate(
+            flops=(3 * layers - 2) * 4 * n * n * n,
+            bytes_accessed=(layers * 3 + layers + layers * 2) * n * n * 2,
+            transcendentals=0,
+        ),
+    )(retarded, coupling)
+    edges = jnp.stack([retarded[0, 0], retarded[layers - 1, 2]])
     width = 3 * n // 2 if screen_packed is None else 5 * n // 2
-    args = (retarded, coupling, below, above)
+    args = (interior, edges, below, above)
     if screen_packed is not None:
         args = args + (screen_packed,)
     return pl.pallas_call(
@@ -85,8 +109,8 @@
             jax.ShapeDtypeStruct((layers, n // 2, width), jnp.bfloat16),
         ),
         cost_estimate=pl.CostEstimate(
-            flops=layers * 3 * 4 * n * n * n,
-            bytes_accessed=(layers * 3 + layers + 2 + layers * 2) * n * n * 2,
+            flops=2 * 4 * n * n * n,
+            bytes_accessed=(layers * 2 + 4 + layers * 2) * n * n * 2,
             transcendentals=0,
         ),
     )(*args)

time: 158 us -> 158 us (level); the launches traced: 156 us -> 157 us
  waiting for transfers between devices: 25.5 us -> 18.1 us
  Pallas kernels: 11.6 us -> 16.3 us
  starting transfers between devices: 18.9 us -> 21.4 us
    pallas_call x0 -> x2, Pallas kernels: none -> 6.26 us  [lesser_blocks(): pl.pallas_call(_interior_kernel, out_shape=jax.ShapeDtypeStruct(coupling....]
    ppermute x2, waiting for transfers between devices: 7.43 us -> 1.31 us  [halo(): above = lax.ppermute(cells[:1], axis, [(i + 1, i) for i in range(ends)])]
    all_to_all x1, blocking collectives: 45.5 us -> 40.3 us  [shards(): lax.all_to_all(both.reshape(energies, rows, both.shape[-1]), 'energy', 0,...]
    all_to_all x1, blocking collectives: 23.9 us -> 28.9 us  [shards(): returned = lax.all_to_all(self_columns, 'energy', 0, 0, tiled=True)]
    all_to_all x1, starting transfers between devices: 7.83 us -> 10.3 us  [shards(): returned = lax.all_to_all(self_columns, 'energy', 0, 0, tiled=True)]
  transfers between devices with their start and end apart: 5 -> 5, of which waited for: 4 -> 2; matrix products, arithmetic and copies ran while one was open for 1% -> 2% of each run, Pallas kernels for 0% -> 4%
where the time goes in v8:
time: 158 us; the launch traced here: 157 us
  blocking collectives  91.7 us (58%)
  starting transfers between devices  21.4 us (14%)
  waiting for transfers between devices  18.1 us (11%)
  Pallas kernels  16.3 us (10%)
  local copies, waits for them, and re-layouts  5.58 us (4%)
  other arithmetic  3.56 us (2%)
    all_to_all x1, blocking collectives, shards(): lax.all_to_all(both.reshape(energies, rows, both.shape[-1]), 'energy', 0,...  40.3 us
    all_to_all x1, blocking collectives, shards(): returned = lax.all_to_all(self_columns, 'energy', 0, 0, tiled=True)  28.9 us
    all_to_all x1, blocking collectives, shards(): lax.all_to_all(packed.reshape(energies, rows, packed.shape[-1]), 'energy'...  22.5 us
    all_to_all x1, waiting for transfers between devices, shards(): returned = lax.all_to_all(self_columns, 'energy', 0, 0, tiled=True)  16.8 us
    all_to_all x1, starting transfers between devices, shards(): returned = lax.all_to_all(self_columns, 'energy', 0, 0, tiled=True)  10.3 us
    pallas_call x2, Pallas kernels, lesser_blocks(): pl.pallas_call(_interior_kernel, out_shape=jax.ShapeDtypeStruct(coupling....  6.26 us
    ppermute x2, starting transfers between devices, halo(): below = lax.ppermute(cells[-1:], axis, [(i, i + 1) for i in range(ends)])  5.82 us
    pallas_call x2, Pallas kernels, lesser_blocks(): pl.pallas_call(_lesser_kernel, out_shape=(jax.ShapeDtypeStruct(coupling.s...  5.38 us
  transfers between devices with their start and end apart: 5, of which 2 were waited for; matrix products, arithmetic and copies ran while one was open for 2% of the time, Pallas kernels for 4%

profile of v8, /device:TPU:7, one launch (start us, length us, event | category | flops | bytes accessed | tf_op | source)
XLA Modules:
  0.0 157.5 jit_solution(13917328122607579004)
XLA Ops:
  0.6 1.2 copy.5
  1.8 0.1 bitcast_convert_fusion.1
  1.9 0.3 copy.6
  2.1 0.0 copy-start.2
  2.2 0.1 fusion.3.c_ref
  2.3 0.0 copy-start
  2.3 0.8 fusion.5
  3.1 3.9 %collective-permute-start = (bf16[1,256,256]{2,1,0:T(8,128)(2,1)}, bf16[1,256,256]{2,1,0:T(8,128)(2,1)}, u32[]{:S(2)}, u32[]{:S(2)}) collective-permute-start(bf16[1,256,256]{2,1,0:T(8,128)(2,1)} %get-tuple-element.24), channel_id=1, source_target_pairs={{0,1},{1,2},{2,3},{3,4},{4,5},{5,6},{6,7},{7,8},{8,9},{9,10},{10,1... | collective-permute-start | bytes 393224 | tf_op jit(solution)/shard_map/ppermute | solution.py:21
  7.0 1.9 %collective-permute-start.1 = (bf16[1,256,256]{2,1,0:T(8,128)(2,1)}, bf16[1,256,256]{2,1,0:T(8,128)(2,1)}, u32[]{:S(2)}, u32[]{:S(2)}) collective-permute-start(bf16[1,256,256]{2,1,0:T(8,128)(2,1)} %get-tuple-element.23), channel_id=1, source_target_pairs={{1,0},{2,1},{3,2},{4,3},{5,4},{6,5},{7,6},{8,7},{9,8},{10,9},{11,1... | collective-permute-start | bytes 393224 | tf_op jit(solution)/shard_map/ppermute | solution.py:22
  8.9 0.6 iota_compare_fusion.1
  9.5 0.0 copy-done.2
  9.5 0.2 copy.7
  9.7 0.1 bitcast_convert_fusion
  9.8 0.0 copy-done
  9.8 0.3 copy.8
  10.1 0.0 copy-start.3
  10.1 0.1 fusion.1
  10.2 0.6 copy-done.3
  10.8 0.1 fusion.6
  10.9 1.0 slice_bitcast_fusion.1
  11.9 0.7 pad_maximum_fusion.1.r_edge_ref
  12.6 3.1 %shard_map.50.part_ref = f32[3,256,256]{2,1,0:T(8,128)} custom-call(bf16[3,3,256,256]{3,2,1,0:T(8,128)(2,1)} %bitcast.53, bf16[3,256,256]{2,1,0:T(8,128)(2,1)} %copy-done), custom_call_target="tpu_custom_call" | custom-call | flops 469762048 | bytes 2359296 | tf_op jit(solution)/shard_map/pallas_call | solution.py:91
  15.7 0.8 pad_maximum_fusion.rest_0_
  16.6 0.0 collective-permute-done.below_ref
  16.6 0.0 collective-permute-done.1.above_ref
  16.6 2.8 %shard_map.51 = (bf16[3,256,256]{2,1,0:T(8,128)(2,1)}, bf16[3,128,640]{2,1,0:T(8,128)(2,1)}) custom-call(f32[3,256,256]{2,1,0:T(8,128)} %shard_map.50.part_ref, bf16[2,256,256]{2,1,0:T(8,128)(2,1)} %pad_maximum_fusion.1.r_edge_ref, bf16[1,256,256]{2,1,0:T(8,128)(2,1)} %collective-permute-done.below_ref, ...), custom_call_target="tpu_custom_call" | custom-call | flops 134217728 | bytes 2097152 | tf_op jit(solution)/shard_map/pallas_call | solution.py:105
  19.4 40.3 %all_to_all.20.x_ref = bf16[48,8,640]{2,1,0:T(8,128)(2,1)} all-to-all(bf16[48,8,640]{2,1,0:T(8,128)(2,1)} %bitcast.59), channel_id=1, replica_groups=mesh['energy'=48,'layer'=16] {'energy'}, dimensions={0} | all-to-all | bytes 983040 | tf_op jit(solution)/shard_map/all_to_all | solution.py:243
  59.7 2.4 %shard_map.52 = (bf16[48,8,384]{2,1,0:T(8,128)(2,1)}, bf16[48,8,384]{2,1,0:T(8,128)(2,1)}) custom-call(bf16[48,8,640]{2,1,0:T(8,128)(2,1)} %all_to_all.20.x_ref), custom_call_target="tpu_custom_call" | custom-call | flops 7225344 | bytes 1179648 | tf_op jit(solution)/shard_map/pallas_call | solution.py:162
  62.1 10.3 %all-to-all-start.1 = ((bf16[48,8,384]{2,1,0:T(8,128)(2,1)}), bf16[48,8,384]{2,1,0:T(8,128)(2,1)S(1)}, u32[]{:S(2)}, u32[]{:S(2)}) async-start(bf16[48,8,384]{2,1,0:T(8,128)(2,1)} %get-tuple-element.8), calls=%async_computation.1 | async-start | bytes 589824 | tf_op jit(solution)/shard_map/all_to_all | solution.py:253
  72.4 16.8 %all-to-all-done.1 = bf16[48,8,384]{2,1,0:T(8,128)(2,1)S(1)} async-done(((bf16[48,8,384]{2,1,0:T(8,128)(2,1)}), bf16[48,8,384]{2,1,0:T(8,128)(2,1)S(1)}, u32[]{:S(2)}, u32[]{:S(2)}) %all-to-all-start.1) | async-done | bytes 294944 | tf_op jit(solution)/shard_map/all_to_all | solution.py:253
  89.2 0.1 copy.9
  89.4 0.1 copy.10
  89.5 0.2 add_convert_fusion.c_ref
  89.7 0.0 copy-start.1
  89.7 1.9 %collective-permute-start.2 = (bf16[1,256,256]{2,1,0:T(8,128)(2,1)S(1)}, bf16[1,256,256]{2,1,0:T(8,128)(2,1)S(1)}, u32[]{:S(2)}, u32[]{:S(2)}) collective-permute-start(bf16[1,256,256]{2,1,0:T(8,128)(2,1)S(1)} %get-tuple-element.17), channel_id=1, source_target_pairs={{0,1},{1,2},{2,3},{3,4},{4,5},{5,6},{6,7},{7,8},{8,9},{9,10},{10,1... | collective-permute-start | bytes 393224 | tf_op jit(solution)/shard_map/ppermute | solution.py:21
  91.6 3.4 %collective-permute-start.3 = (bf16[1,256,256]{2,1,0:T(8,128)(2,1)S(1)}, bf16[1,256,256]{2,1,0:T(8,128)(2,1)S(1)}, u32[]{:S(2)}, u32[]{:S(2)}) collective-permute-start(bf16[1,256,256]{2,1,0:T(8,128)(2,1)S(1)} %get-tuple-element.16), channel_id=1, source_target_pairs={{1,0},{2,1},{3,2},{4,3},{5,4},{6,5},{7,6},{8,7},{9,8},{10,9},{11,1... | collective-permute-start | bytes 393224 | tf_op jit(solution)/shard_map/ppermute | solution.py:22
  95.0 0.0 copy-done.1
  95.0 3.1 %shard_map.53.part_ref = f32[3,256,256]{2,1,0:T(8,128)} custom-call(bf16[3,3,256,256]{3,2,1,0:T(8,128)(2,1)} %bitcast.54, bf16[3,256,256]{2,1,0:T(8,128)(2,1)} %copy-done.1), custom_call_target="tpu_custom_call" | custom-call | flops 469762048 | bytes 2359296 | tf_op jit(solution)/shard_map/pallas_call | solution.py:91
  98.1 0.0 collective-permute-done.2.below_ref
  98.1 1.3 collective-permute-done.3.above_ref
  99.4 0.7 copy-done.5
  100.1 2.6 %shard_map.54 = (bf16[3,256,256]{2,1,0:T(8,128)(2,1)}, bf16[3,128,384]{2,1,0:T(8,128)(2,1)}) custom-call(f32[3,256,256]{2,1,0:T(8,128)} %shard_map.53.part_ref, bf16[2,256,256]{2,1,0:T(8,128)(2,1)} %pad_maximum_fusion.1.r_edge_ref, bf16[1,256,256]{2,1,0:T(8,128)(2,1)} %copy-done.4, bf16[1,256,256]{2,1,0:T(8,128)(2,1)} %copy-done.5), custom_call_target="tpu_custom_call" | custom-call | flops 134217728 | bytes 2097152 | tf_op jit(solution)/shard_map/pallas_call | solution.py:105
  102.7 22.5 %all_to_all.21.l_ref = bf16[48,8,384]{2,1,0:T(8,128)(2,1)} all-to-all(bf16[48,8,384]{2,1,0:T(8,128)(2,1)} %bitcast.60), channel_id=1, replica_groups=mesh['energy'=48,'layer'=16] {'energy'}, dimensions={0} | all-to-all | bytes 589824 | tf_op jit(solution)/shard_map/all_to_all | solution.py:249
  125.2 2.3 %shard_map.55 = bf16[48,8,384]{2,1,0:T(8,128)(2,1)} custom-call(bf16[48,8,384]{2,1,0:T(8,128)(2,1)} %all_to_all.21.l_ref, bf16[48,8,384]{2,1,0:T(8,128)(2,1)} %get-tuple-element.11.s_ref), custom_call_target="tpu_custom_call" | custom-call | flops 7225344 | bytes 1179648 | tf_op jit(solution)/shard_map/pallas_call | solution.py:162
  127.5 28.9 %all_to_all.22 = bf16[48,8,384]{2,1,0:T(8,128)(2,1)S(1)} all-to-all(bf16[48,8,384]{2,1,0:T(8,128)(2,1)} %shard_map.55), channel_id=1, replica_groups=mesh['energy'=48,'layer'=16] {'energy'}, dimensions={0} | all-to-all | bytes 589824 | tf_op jit(solution)/shard_map/all_to_all | solution.py:253
  156.4 0.1 copy.15
  156.6 0.1 copy.14
  156.7 0.8 maximum_bitcast_fusion
  (10 shorter events, 0.2 us)
Async XLA Ops:
  2.1 7.4 %copy-start.2 = (bf16[1,3,256,256]{3,2,1,0:T(8,128)(2,1)S(1)}, bf16[1,3,256,256]{3,2,1,0:T(8,128)(2,1)}, u32[]{:S(2)}) copy-start(bf16[1,3,256,256]{3,2,1,0:T(8,128)(2,1)} %param.5) | copy-start | bytes 1179652
  2.3 7.5 %copy-start = (bf16[3,256,256]{2,1,0:T(8,128)(2,1)}, bf16[3,256,256]{2,1,0:T(8,128)(2,1)S(1)}, u32[]{:S(2)}) copy-start(bf16[3,256,256]{2,1,0:T(8,128)(2,1)S(1)} %fusion.3.c_ref) | copy-start | bytes 1179652
  3.1 13.5 %collective-permute-start = (bf16[1,256,256]{2,1,0:T(8,128)(2,1)}, bf16[1,256,256]{2,1,0:T(8,128)(2,1)}, u32[]{:S(2)}, u32[]{:S(2)}) collective-permute-start(bf16[1,256,256]{2,1,0:T(8,128)(2,1)} %get-tuple-element.24), channel_id=1, source_target_pairs={{0,1},{1,2},{2,3},{3,4},{4,5},{5,6},{6,7},{7,8},{8,9},{9,10},{10,1... | collective-permute-start | bytes 393224 | tf_op jit(solution)/shard_map/ppermute | solution.py:21
  7.0 9.6 %collective-permute-start.1 = (bf16[1,256,256]{2,1,0:T(8,128)(2,1)}, bf16[1,256,256]{2,1,0:T(8,128)(2,1)}, u32[]{:S(2)}, u32[]{:S(2)}) collective-permute-start(bf16[1,256,256]{2,1,0:T(8,128)(2,1)} %get-tuple-element.23), channel_id=1, source_target_pairs={{1,0},{2,1},{3,2},{4,3},{5,4},{6,5},{7,6},{8,7},{9,8},{10,9},{11,1... | collective-permute-start | bytes 393224 | tf_op jit(solution)/shard_map/ppermute | solution.py:22
  10.1 0.7 copy-start.3
  62.1 27.1 %all-to-all-start.1 = ((bf16[48,8,384]{2,1,0:T(8,128)(2,1)}), bf16[48,8,384]{2,1,0:T(8,128)(2,1)S(1)}, u32[]{:S(2)}, u32[]{:S(2)}) async-start(bf16[48,8,384]{2,1,0:T(8,128)(2,1)} %get-tuple-element.8), calls=%async_computation.1 | async-start | bytes 589824 | tf_op jit(solution)/shard_map/all_to_all | solution.py:253
  89.7 5.3 %copy-start.1 = (bf16[3,256,256]{2,1,0:T(8,128)(2,1)}, bf16[3,256,256]{2,1,0:T(8,128)(2,1)S(1)}, u32[]{:S(2)}) copy-start(bf16[3,256,256]{2,1,0:T(8,128)(2,1)S(1)} %add_convert_fusion.c_ref) | copy-start | bytes 1179652
  89.7 8.4 %collective-permute-start.2 = (bf16[1,256,256]{2,1,0:T(8,128)(2,1)S(1)}, bf16[1,256,256]{2,1,0:T(8,128)(2,1)S(1)}, u32[]{:S(2)}, u32[]{:S(2)}) collective-permute-start(bf16[1,256,256]{2,1,0:T(8,128)(2,1)S(1)} %get-tuple-element.17), channel_id=1, source_target_pairs={{0,1},{1,2},{2,3},{3,4},{4,5},{5,6},{6,7},{7,8},{8,9},{9,10},{10,1... | collective-permute-start | bytes 393224 | tf_op jit(solution)/shard_map/ppermute | solution.py:21
  91.6 7.8 %collective-permute-start.3 = (bf16[1,256,256]{2,1,0:T(8,128)(2,1)S(1)}, bf16[1,256,256]{2,1,0:T(8,128)(2,1)S(1)}, u32[]{:S(2)}, u32[]{:S(2)}) collective-permute-start(bf16[1,256,256]{2,1,0:T(8,128)(2,1)S(1)} %get-tuple-element.16), channel_id=1, source_target_pairs={{1,0},{2,1},{3,2},{4,3},{5,4},{6,5},{7,6},{8,7},{9,8},{10,9},{11,1... | collective-permute-start | bytes 393224 | tf_op jit(solution)/shard_map/ppermute | solution.py:22
  98.1 1.3 copy-start.4
  99.4 0.7 copy-start.5

commit v9 on v6

--- a/solution.py
+++ b/solution.py
@@ -31,58 +31,69 @@
     layers = c_ref.shape[0]
     n = c_ref.shape[-1]
     h = n // 2
+    layer = pl.program_id(0)
     rows = lax.broadcasted_iota(jnp.int32, (h, h), 0)
     cols = lax.broadcasted_iota(jnp.int32, (h, h), 1)
-
-    def neighbour(index):
-        if index < 0:
-            return below_ref[0]
-        if index >= layers:
-            return above_ref[0]
-        return c_ref[index]
-
-    for layer in range(layers):
-        running = None
-        for offset in range(3):
-            factor = r_ref[layer, offset]
-            left_part = jnp.dot(
-                factor, neighbour(layer + offset - 1), preferred_element_type=jnp.float32
-            ).astype(jnp.bfloat16)
-            term_part = lax.dot_general(
-                left_part,
-                factor,
-                (((1,), (1,)), ((), ())),
-                preferred_element_type=jnp.float32,
-            )
-            running = term_part if running is None else running + term_part
-        block = (0.5 * (running + running.T)).astype(o_ref.dtype)
-        o_ref[layer] = block
-        top_left = block[:h, :h]
-        bottom_right = block[h:, h:]
-        packed_ref[layer, :, :h] = jnp.where(rows <= cols, top_left, bottom_right)
-        packed_ref[layer, :, h : 2 * h] = block[:h, h:]
-        if screen_ref is None:
-            packed_ref[layer, :, 2 * h :] = jnp.where(
-                rows == cols, bottom_right, jnp.zeros_like(bottom_right)
-            )
-        else:
-            packed_ref[layer, :, 2 * h : 4 * h] = screen_ref[layer, :, : 2 * h]
-            packed_ref[layer, :, 4 * h :] = jnp.where(
-                rows == cols, bottom_right, screen_ref[layer, :, 2 * h :]
-            )
+    neighbours = (
+        jnp.where(layer == 0, below_ref[0], c_ref[jnp.maximum(layer - 1, 0)]),
+        c_ref[layer],
+        jnp.where(layer == layers - 1, above_ref[0], c_ref[jnp.minimum(layer + 1, layers - 1)]),
+    )
+    running = None
+    for offset in range(3):
+        factor = r_ref[0, offset]
+        left_part = jnp.dot(
+            factor, neighbours[offset], preferred_element_type=jnp.float32
+        ).astype(jnp.bfloat16)
+        term_part = lax.dot_general(
+            left_part,
+            factor,
+            (((1,), (1,)), ((), ())),
+            preferred_element_type=jnp.float32,
+        )
+        running = term_part if running is None else running + term_part
+    block = (0.5 * (running + running.T)).astype(o_ref.dtype)
+    o_ref[0] = block
+    top_left = block[:h, :h]
+    bottom_right = block[h:, h:]
+    packed_ref[0, :, :h] = jnp.where(rows <= cols, top_left, bottom_right)
+    packed_ref[0, :, h : 2 * h] = block[:h, h:]
+    if screen_ref is None:
+        packed_ref[0, :, 2 * h :] = jnp.where(
+            rows == cols, bottom_right, jnp.zeros_like(bottom_right)
+        )
+    else:
+        packed_ref[0, :, 2 * h : 4 * h] = screen_ref[0, :, : 2 * h]
+        packed_ref[0, :, 4 * h :] = jnp.where(
+            rows == cols, bottom_right, screen_ref[0, :, 2 * h :]
+        )
 
 
 def lesser_blocks(retarded, coupling, below, above, screen_packed=None):
     layers, n = coupling.shape[0], coupling.shape[-1]
+    h = n // 2
     width = 3 * n // 2 if screen_packed is None else 5 * n // 2
     args = (retarded, coupling, below, above)
+    in_specs = [
+        pl.BlockSpec((1, 3, n, n), lambda l: (l, 0, 0, 0)),
+        pl.BlockSpec((layers, n, n), lambda l: (0, 0, 0)),
+        pl.BlockSpec((1, n, n), lambda l: (0, 0, 0)),
+        pl.BlockSpec((1, n, n), lambda l: (0, 0, 0)),
+    ]
     if screen_packed is not None:
         args = args + (screen_packed,)
+        in_specs.append(pl.BlockSpec((1, h, 3 * h), lambda l: (l, 0, 0)))
     return pl.pallas_call(
         _lesser_kernel,
+        grid=(layers,),
+        in_specs=in_specs,
+        out_specs=(
+            pl.BlockSpec((1, n, n), lambda l: (l, 0, 0)),
+            pl.BlockSpec((1, h, width), lambda l: (l, 0, 0)),
+        ),
         out_shape=(
             jax.ShapeDtypeStruct(coupling.shape, jnp.bfloat16),
-            jax.ShapeDtypeStruct((layers, n // 2, width), jnp.bfloat16),
+            jax.ShapeDtypeStruct((layers, h, width), jnp.bfloat16),
         ),
         cost_estimate=pl.CostEstimate(
             flops=layers * 3 * 4 * n * n * n,

time: 158 us -> 160 us (1.013)
  no operation moved by 1% of the time
where the time goes in v9:
time: 160 us; the launch traced here: 157 us
  blocking collectives  91.6 us (57%)
  waiting for transfers between devices  25.4 us (16%)
  starting transfers between devices  19 us (12%)
  Pallas kernels  13.2 us (8%)
  local copies, waits for them, and re-layouts  4.59 us (3%)
  other arithmetic  2.82 us (2%)
    all_to_all x1, blocking collectives, shards(): lax.all_to_all(both.reshape(energies, rows, both.shape[-1]), 'energy', 0,...  45.4 us
    all_to_all x1, blocking collectives, shards(): returned = lax.all_to_all(self_columns, 'energy', 0, 0, tiled=True)  23.9 us
    all_to_all x1, blocking collectives, shards(): lax.all_to_all(packed.reshape(energies, rows, packed.shape[-1]), 'energy'...  22.3 us
    all_to_all x1, waiting for transfers between devices, shards(): returned = lax.all_to_all(self_columns, 'energy', 0, 0, tiled=True)  16.8 us
    pallas_call x2, Pallas kernels, lesser_blocks(): pl.pallas_call(_lesser_kernel, grid=(layers,), in_specs=in_specs, out_spe...  8.49 us
    all_to_all x1, starting transfers between devices, shards(): returned = lax.all_to_all(self_columns, 'energy', 0, 0, tiled=True)  7.89 us
    ppermute x2, waiting for transfers between devices, halo(): above = lax.ppermute(cells[:1], axis, [(i + 1, i) for i in range(ends)])  7.43 us
    ppermute x2, starting transfers between devices, halo(): below = lax.ppermute(cells[-1:], axis, [(i, i + 1) for i in range(ends)])  5.82 us
  transfers between devices with their start and end apart: 5, of which 4 were waited for; matrix products, arithmetic and copies ran while one was open for 1% of the time, Pallas kernels for 0%

profile of v9, /device:TPU:7, one launch (start us, length us, event | category | flops | bytes accessed | tf_op | source)
XLA Modules:
  0.0 157.4 jit_solution(1874410079031644215)
XLA Ops:
  0.6 1.2 copy.5
  1.8 0.1 bitcast_convert_fusion.1
  1.9 0.3 copy.6
  2.1 0.0 copy-start.2
  2.2 0.1 fusion.3.c_ref
  2.3 0.0 copy-start
  2.3 0.8 fusion.5
  3.1 3.9 %collective-permute-start = (bf16[1,256,256]{2,1,0:T(8,128)(2,1)}, bf16[1,256,256]{2,1,0:T(8,128)(2,1)}, u32[]{:S(2)}, u32[]{:S(2)}) collective-permute-start(bf16[1,256,256]{2,1,0:T(8,128)(2,1)} %get-tuple-element.22), channel_id=1, source_target_pairs={{0,1},{1,2},{2,3},{3,4},{4,5},{5,6},{6,7},{7,8},{8,9},{9,10},{10,1... | collective-permute-start | bytes 393224 | tf_op jit(solution)/shard_map/ppermute | solution.py:21
  7.0 1.9 %collective-permute-start.1 = (bf16[1,256,256]{2,1,0:T(8,128)(2,1)}, bf16[1,256,256]{2,1,0:T(8,128)(2,1)}, u32[]{:S(2)}, u32[]{:S(2)}) collective-permute-start(bf16[1,256,256]{2,1,0:T(8,128)(2,1)} %get-tuple-element.21), channel_id=1, source_target_pairs={{1,0},{2,1},{3,2},{4,3},{5,4},{6,5},{7,6},{8,7},{9,8},{10,9},{11,1... | collective-permute-start | bytes 393224 | tf_op jit(solution)/shard_map/ppermute | solution.py:22
  8.9 0.6 iota_compare_fusion.1
  9.5 0.0 copy-done.2
  9.5 0.2 copy.7
  9.7 0.1 bitcast_convert_fusion
  9.8 0.0 copy-done
  9.8 0.3 copy.8
  10.1 0.0 copy-start.3
  10.1 0.1 fusion.1
  10.2 0.6 copy-done.3
  10.8 0.1 fusion.6
  10.9 0.8 pad_maximum_fusion.rest_0_
  11.7 0.0 collective-permute-done.below_ref
  11.7 3.4 %collective-permute-done.1.above_ref = bf16[1,256,256]{2,1,0:T(8,128)(2,1)} collective-permute-done((bf16[1,256,256]{2,1,0:T(8,128)(2,1)}, bf16[1,256,256]{2,1,0:T(8,128)(2,1)}, u32[]{:S(2)}, u32[]{:S(2)}) %collective-permute-start.1) | collective-permute-done | bytes 131104 | tf_op jit(solution)/shard_map/ppermute | solution.py:22
  15.1 4.3 %shard_map.50 = (bf16[3,256,256]{2,1,0:T(8,128)(2,1)}, bf16[3,128,640]{2,1,0:T(8,128)(2,1)}) custom-call(bf16[3,3,256,256]{3,2,1,0:T(8,128)(2,1)} %bitcast.54, bf16[3,256,256]{2,1,0:T(8,128)(2,1)} %copy-done, bf16[1,256,256]{2,1,0:T(8,128)(2,1)} %collective-permute-done.below_ref, bf16[1,256,256]{2,1,0:T(8,128)(2,1)} %collective-permute-done.1.above_ref, ...), custom_call_target="tpu_custom_call" | custom-call | flops 603979776 | bytes 2621440 | tf_op jit(solution)/shard_map/pallas_call | solution.py:86
  19.4 45.4 %all_to_all.20.x_ref = bf16[48,8,640]{2,1,0:T(8,128)(2,1)} all-to-all(bf16[48,8,640]{2,1,0:T(8,128)(2,1)} %bitcast.52), channel_id=1, replica_groups=mesh['energy'=48,'layer'=16] {'energy'}, dimensions={0} | all-to-all | bytes 983040 | tf_op jit(solution)/shard_map/all_to_all | solution.py:230
  64.9 2.4 %shard_map.51 = (bf16[48,8,384]{2,1,0:T(8,128)(2,1)}, bf16[48,8,384]{2,1,0:T(8,128)(2,1)}) custom-call(bf16[48,8,640]{2,1,0:T(8,128)(2,1)} %all_to_all.20.x_ref), custom_call_target="tpu_custom_call" | custom-call | flops 7225344 | bytes 1179648 | tf_op jit(solution)/shard_map/pallas_call | solution.py:149
  67.3 7.9 %all-to-all-start.1 = ((bf16[48,8,384]{2,1,0:T(8,128)(2,1)}), bf16[48,8,384]{2,1,0:T(8,128)(2,1)S(1)}, u32[]{:S(2)}, u32[]{:S(2)}) async-start(bf16[48,8,384]{2,1,0:T(8,128)(2,1)} %get-tuple-element.8), calls=%async_computation.1 | async-start | bytes 589824 | tf_op jit(solution)/shard_map/all_to_all | solution.py:240
  75.2 16.8 %all-to-all-done.1 = bf16[48,8,384]{2,1,0:T(8,128)(2,1)S(1)} async-done(((bf16[48,8,384]{2,1,0:T(8,128)(2,1)}), bf16[48,8,384]{2,1,0:T(8,128)(2,1)S(1)}, u32[]{:S(2)}, u32[]{:S(2)}) %all-to-all-start.1) | async-done | bytes 294944 | tf_op jit(solution)/shard_map/all_to_all | solution.py:240
  92.0 0.1 copy.9
  92.2 0.1 copy.10
  92.3 0.2 add_convert_fusion.c_ref
  92.5 0.0 copy-start.1
  92.5 1.9 %collective-permute-start.2 = (bf16[1,256,256]{2,1,0:T(8,128)(2,1)S(1)}, bf16[1,256,256]{2,1,0:T(8,128)(2,1)S(1)}, u32[]{:S(2)}, u32[]{:S(2)}) collective-permute-start(bf16[1,256,256]{2,1,0:T(8,128)(2,1)S(1)} %get-tuple-element.15), channel_id=1, source_target_pairs={{0,1},{1,2},{2,3},{3,4},{4,5},{5,6},{6,7},{7,8},{8,9},{9,10},{10,1... | collective-permute-start | bytes 393224 | tf_op jit(solution)/shard_map/ppermute | solution.py:21
  94.5 3.4 %collective-permute-start.3 = (bf16[1,256,256]{2,1,0:T(8,128)(2,1)S(1)}, bf16[1,256,256]{2,1,0:T(8,128)(2,1)S(1)}, u32[]{:S(2)}, u32[]{:S(2)}) collective-permute-start(bf16[1,256,256]{2,1,0:T(8,128)(2,1)S(1)} %get-tuple-element.14), channel_id=1, source_target_pairs={{1,0},{2,1},{3,2},{4,3},{5,4},{6,5},{7,6},{8,7},{9,8},{10,9},{11,1... | collective-permute-start | bytes 393224 | tf_op jit(solution)/shard_map/ppermute | solution.py:22
  97.8 1.1 collective-permute-done.2.below_ref
  98.9 0.0 copy-start.4
  98.9 4.0 %collective-permute-done.3.above_ref = bf16[1,256,256]{2,1,0:T(8,128)(2,1)S(1)} collective-permute-done((bf16[1,256,256]{2,1,0:T(8,128)(2,1)S(1)}, bf16[1,256,256]{2,1,0:T(8,128)(2,1)S(1)}, u32[]{:S(2)}, u32[]{:S(2)}) %collective-permute-start.3) | collective-permute-done | bytes 131104 | tf_op jit(solution)/shard_map/ppermute | solution.py:22
  103.0 0.0 copy-done.1
  103.0 0.0 copy-done.4
  103.0 0.0 copy-start.5
  103.0 0.6 copy-done.5
  103.6 4.2 %shard_map.52 = (bf16[3,256,256]{2,1,0:T(8,128)(2,1)}, bf16[3,128,384]{2,1,0:T(8,128)(2,1)}) custom-call(bf16[3,3,256,256]{3,2,1,0:T(8,128)(2,1)} %bitcast.55, bf16[3,256,256]{2,1,0:T(8,128)(2,1)} %copy-done.1, bf16[1,256,256]{2,1,0:T(8,128)(2,1)} %copy-done.4, bf16[1,256,256]{2,1,0:T(8,128)(2,1)} %copy-done.5), custom_call_target="tpu_custom_call" | custom-call | flops 603979776 | bytes 2621440 | tf_op jit(solution)/shard_map/pallas_call | solution.py:86
  107.8 22.3 %all_to_all.21.l_ref = bf16[48,8,384]{2,1,0:T(8,128)(2,1)} all-to-all(bf16[48,8,384]{2,1,0:T(8,128)(2,1)} %bitcast.53), channel_id=1, replica_groups=mesh['energy'=48,'layer'=16] {'energy'}, dimensions={0} | all-to-all | bytes 589824 | tf_op jit(solution)/shard_map/all_to_all | solution.py:236
  130.1 2.3 %shard_map.53 = bf16[48,8,384]{2,1,0:T(8,128)(2,1)} custom-call(bf16[48,8,384]{2,1,0:T(8,128)(2,1)} %all_to_all.21.l_ref, bf16[48,8,384]{2,1,0:T(8,128)(2,1)} %get-tuple-element.11.s_ref), custom_call_target="tpu_custom_call" | custom-call | flops 7225344 | bytes 1179648 | tf_op jit(solution)/shard_map/pallas_call | solution.py:149
  132.4 23.9 %all_to_all.22 = bf16[48,8,384]{2,1,0:T(8,128)(2,1)S(1)} all-to-all(bf16[48,8,384]{2,1,0:T(8,128)(2,1)} %shard_map.53), channel_id=1, replica_groups=mesh['energy'=48,'layer'=16] {'energy'}, dimensions={0} | all-to-all | bytes 589824 | tf_op jit(solution)/shard_map/all_to_all | solution.py:240
  156.3 0.1 copy.15
  156.5 0.1 copy.14
  156.6 0.8 maximum_bitcast_fusion
  (7 shorter events, 0.2 us)
Async XLA Ops:
  2.1 7.4 %copy-start.2 = (bf16[1,3,256,256]{3,2,1,0:T(8,128)(2,1)S(1)}, bf16[1,3,256,256]{3,2,1,0:T(8,128)(2,1)}, u32[]{:S(2)}) copy-start(bf16[1,3,256,256]{3,2,1,0:T(8,128)(2,1)} %param.5) | copy-start | bytes 1179652
  2.3 7.5 %copy-start = (bf16[3,256,256]{2,1,0:T(8,128)(2,1)}, bf16[3,256,256]{2,1,0:T(8,128)(2,1)S(1)}, u32[]{:S(2)}) copy-start(bf16[3,256,256]{2,1,0:T(8,128)(2,1)S(1)} %fusion.3.c_ref) | copy-start | bytes 1179652
  3.1 8.7 %collective-permute-start = (bf16[1,256,256]{2,1,0:T(8,128)(2,1)}, bf16[1,256,256]{2,1,0:T(8,128)(2,1)}, u32[]{:S(2)}, u32[]{:S(2)}) collective-permute-start(bf16[1,256,256]{2,1,0:T(8,128)(2,1)} %get-tuple-element.22), channel_id=1, source_target_pairs={{0,1},{1,2},{2,3},{3,4},{4,5},{5,6},{6,7},{7,8},{8,9},{9,10},{10,1... | collective-permute-start | bytes 393224 | tf_op jit(solution)/shard_map/ppermute | solution.py:21
  7.0 8.1 %collective-permute-start.1 = (bf16[1,256,256]{2,1,0:T(8,128)(2,1)}, bf16[1,256,256]{2,1,0:T(8,128)(2,1)}, u32[]{:S(2)}, u32[]{:S(2)}) collective-permute-start(bf16[1,256,256]{2,1,0:T(8,128)(2,1)} %get-tuple-element.21), channel_id=1, source_target_pairs={{1,0},{2,1},{3,2},{4,3},{5,4},{6,5},{7,6},{8,7},{9,8},{10,9},{11,1... | collective-permute-start | bytes 393224 | tf_op jit(solution)/shard_map/ppermute | solution.py:22
  10.1 0.7 copy-start.3
  67.3 24.8 %all-to-all-start.1 = ((bf16[48,8,384]{2,1,0:T(8,128)(2,1)}), bf16[48,8,384]{2,1,0:T(8,128)(2,1)S(1)}, u32[]{:S(2)}, u32[]{:S(2)}) async-start(bf16[48,8,384]{2,1,0:T(8,128)(2,1)} %get-tuple-element.8), calls=%async_computation.1 | async-start | bytes 589824 | tf_op jit(solution)/shard_map/all_to_all | solution.py:240
  92.5 10.5 %copy-start.1 = (bf16[3,256,256]{2,1,0:T(8,128)(2,1)}, bf16[3,256,256]{2,1,0:T(8,128)(2,1)S(1)}, u32[]{:S(2)}) copy-start(bf16[3,256,256]{2,1,0:T(8,128)(2,1)S(1)} %add_convert_fusion.c_ref) | copy-start | bytes 1179652
  92.5 6.4 %collective-permute-start.2 = (bf16[1,256,256]{2,1,0:T(8,128)(2,1)S(1)}, bf16[1,256,256]{2,1,0:T(8,128)(2,1)S(1)}, u32[]{:S(2)}, u32[]{:S(2)}) collective-permute-start(bf16[1,256,256]{2,1,0:T(8,128)(2,1)S(1)} %get-tuple-element.15), channel_id=1, source_target_pairs={{0,1},{1,2},{2,3},{3,4},{4,5},{5,6},{6,7},{7,8},{8,9},{9,10},{10,1... | collective-permute-start | bytes 393224 | tf_op jit(solution)/shard_map/ppermute | solution.py:21
  94.5 8.5 %collective-permute-start.3 = (bf16[1,256,256]{2,1,0:T(8,128)(2,1)S(1)}, bf16[1,256,256]{2,1,0:T(8,128)(2,1)S(1)}, u32[]{:S(2)}, u32[]{:S(2)}) collective-permute-start(bf16[1,256,256]{2,1,0:T(8,128)(2,1)S(1)} %get-tuple-element.14), channel_id=1, source_target_pairs={{1,0},{2,1},{3,2},{4,3},{5,4},{6,5},{7,6},{8,7},{9,8},{10,9},{11,1... | collective-permute-start | bytes 393224 | tf_op jit(solution)/shard_map/ppermute | solution.py:22
  98.9 4.0 %copy-start.4 = (bf16[1,256,256]{2,1,0:T(8,128)(2,1)}, bf16[1,256,256]{2,1,0:T(8,128)(2,1)S(1)}, u32[]{:S(2)}) copy-start(bf16[1,256,256]{2,1,0:T(8,128)(2,1)S(1)} %collective-permute-done.2.below_ref) | copy-start | bytes 393220
  103.0 0.6 copy-start.5

commit v10 on v6

--- a/solution.py
+++ b/solution.py
@@ -92,7 +92,7 @@
     )(*args)
 
 
-def _conv_core(lf, sf, o_ref, group=4):
+def _conv_core(lf, sf, o_ref, group=8):
     energies = o_ref.shape[0]
     for first in range(0, energies, group):
         last = min(first + group, energies)

time: 158 us -> 159 us (level)
  no operation moved by 1% of the time
where the time goes in v10:
time: 159 us; the launch traced here: 156 us
  blocking collectives  91.6 us (58%)
  waiting for transfers between devices  25.5 us (16%)
  starting transfers between devices  18.9 us (12%)
  Pallas kernels  12.2 us (8%)
  local copies, waits for them, and re-layouts  4.59 us (3%)
  other arithmetic  2.82 us (2%)
    all_to_all x1, blocking collectives, shards(): lax.all_to_all(both.reshape(energies, rows, both.shape[-1]), 'energy', 0,...  45.5 us
    all_to_all x1, blocking collectives, shards(): returned = lax.all_to_all(self_columns, 'energy', 0, 0, tiled=True)  23.9 us
    all_to_all x1, blocking collectives, shards(): lax.all_to_all(packed.reshape(energies, rows, packed.shape[-1]), 'energy'...  22.2 us
    all_to_all x1, waiting for transfers between devices, shards(): returned = lax.all_to_all(self_columns, 'energy', 0, 0, tiled=True)  16.9 us
    all_to_all x1, starting transfers between devices, shards(): returned = lax.all_to_all(self_columns, 'energy', 0, 0, tiled=True)  7.83 us
    ppermute x2, waiting for transfers between devices, halo(): above = lax.ppermute(cells[:1], axis, [(i + 1, i) for i in range(ends)])  7.43 us
    pallas_call x2, Pallas kernels, lesser_blocks(): pl.pallas_call(_lesser_kernel, out_shape=(jax.ShapeDtypeStruct(coupling.s...  6.94 us
    ppermute x2, starting transfers between devices, halo(): below = lax.ppermute(cells[-1:], axis, [(i, i + 1) for i in range(ends)])  5.82 us
  transfers between devices with their start and end apart: 5, of which 4 were waited for; matrix products, arithmetic and copies ran while one was open for 1% of the time, Pallas kernels for 0%

profile of v10, /device:TPU:7, one launch (start us, length us, event | category | flops | bytes accessed | tf_op | source)
XLA Modules:
  0.0 156.4 jit_solution(1702836469593784326)
XLA Ops:
  0.6 1.2 copy.5
  1.8 0.1 bitcast_convert_fusion.1
  1.9 0.3 copy.6
  2.1 0.0 copy-start.2
  2.2 0.1 fusion.3.c_ref
  2.3 0.0 copy-start
  2.3 0.8 fusion.5
  3.1 3.9 %collective-permute-start = (bf16[1,256,256]{2,1,0:T(8,128)(2,1)}, bf16[1,256,256]{2,1,0:T(8,128)(2,1)}, u32[]{:S(2)}, u32[]{:S(2)}) collective-permute-start(bf16[1,256,256]{2,1,0:T(8,128)(2,1)} %get-tuple-element.22), channel_id=1, source_target_pairs={{0,1},{1,2},{2,3},{3,4},{4,5},{5,6},{6,7},{7,8},{8,9},{9,10},{10,1... | collective-permute-start | bytes 393224 | tf_op jit(solution)/shard_map/ppermute | solution.py:21
  7.0 1.9 %collective-permute-start.1 = (bf16[1,256,256]{2,1,0:T(8,128)(2,1)}, bf16[1,256,256]{2,1,0:T(8,128)(2,1)}, u32[]{:S(2)}, u32[]{:S(2)}) collective-permute-start(bf16[1,256,256]{2,1,0:T(8,128)(2,1)} %get-tuple-element.21), channel_id=1, source_target_pairs={{1,0},{2,1},{3,2},{4,3},{5,4},{6,5},{7,6},{8,7},{9,8},{10,9},{11,1... | collective-permute-start | bytes 393224 | tf_op jit(solution)/shard_map/ppermute | solution.py:22
  8.9 0.6 iota_compare_fusion.1
  9.5 0.0 copy-done.2
  9.5 0.2 copy.7
  9.7 0.1 bitcast_convert_fusion
  9.8 0.0 copy-done
  9.8 0.3 copy.8
  10.1 0.0 copy-start.3
  10.1 0.1 fusion.1
  10.2 0.6 copy-done.3
  10.8 0.1 fusion.6
  10.9 0.8 pad_maximum_fusion.rest_0_
  11.7 0.0 collective-permute-done.below_ref
  11.7 3.4 %collective-permute-done.1.above_ref = bf16[1,256,256]{2,1,0:T(8,128)(2,1)} collective-permute-done((bf16[1,256,256]{2,1,0:T(8,128)(2,1)}, bf16[1,256,256]{2,1,0:T(8,128)(2,1)}, u32[]{:S(2)}, u32[]{:S(2)}) %collective-permute-start.1) | collective-permute-done | bytes 131104 | tf_op jit(solution)/shard_map/ppermute | solution.py:22
  15.1 3.6 %shard_map.50 = (bf16[3,256,256]{2,1,0:T(8,128)(2,1)}, bf16[3,128,640]{2,1,0:T(8,128)(2,1)}) custom-call(bf16[3,3,256,256]{3,2,1,0:T(8,128)(2,1)} %bitcast.54, bf16[3,256,256]{2,1,0:T(8,128)(2,1)} %copy-done, bf16[1,256,256]{2,1,0:T(8,128)(2,1)} %collective-permute-done.below_ref, bf16[1,256,256]{2,1,0:T(8,128)(2,1)} %collective-permute-done.1.above_ref, ...), custom_call_target="tpu_custom_call" | custom-call | flops 603979776 | bytes 2621440 | tf_op jit(solution)/shard_map/pallas_call | solution.py:81
  18.7 45.5 %all_to_all.20.x_ref = bf16[48,8,640]{2,1,0:T(8,128)(2,1)} all-to-all(bf16[48,8,640]{2,1,0:T(8,128)(2,1)} %bitcast.52), channel_id=1, replica_groups=mesh['energy'=48,'layer'=16] {'energy'}, dimensions={0} | all-to-all | bytes 983040 | tf_op jit(solution)/shard_map/all_to_all | solution.py:219
  64.2 2.7 %shard_map.51 = (bf16[48,8,384]{2,1,0:T(8,128)(2,1)}, bf16[48,8,384]{2,1,0:T(8,128)(2,1)}) custom-call(bf16[48,8,640]{2,1,0:T(8,128)(2,1)} %all_to_all.20.x_ref), custom_call_target="tpu_custom_call" | custom-call | flops 7225344 | bytes 1179648 | tf_op jit(solution)/shard_map/pallas_call | solution.py:138
  66.9 7.8 %all-to-all-start.1 = ((bf16[48,8,384]{2,1,0:T(8,128)(2,1)}), bf16[48,8,384]{2,1,0:T(8,128)(2,1)S(1)}, u32[]{:S(2)}, u32[]{:S(2)}) async-start(bf16[48,8,384]{2,1,0:T(8,128)(2,1)} %get-tuple-element.8), calls=%async_computation.1 | async-start | bytes 589824 | tf_op jit(solution)/shard_map/all_to_all | solution.py:229
  74.7 16.9 %all-to-all-done.1 = bf16[48,8,384]{2,1,0:T(8,128)(2,1)S(1)} async-done(((bf16[48,8,384]{2,1,0:T(8,128)(2,1)}), bf16[48,8,384]{2,1,0:T(8,128)(2,1)S(1)}, u32[]{:S(2)}, u32[]{:S(2)}) %all-to-all-start.1) | async-done | bytes 294944 | tf_op jit(solution)/shard_map/all_to_all | solution.py:229
  91.6 0.1 copy.9
  91.8 0.1 copy.10
  91.9 0.2 add_convert_fusion.c_ref
  92.1 0.0 copy-start.1
  92.1 1.9 %collective-permute-start.2 = (bf16[1,256,256]{2,1,0:T(8,128)(2,1)S(1)}, bf16[1,256,256]{2,1,0:T(8,128)(2,1)S(1)}, u32[]{:S(2)}, u32[]{:S(2)}) collective-permute-start(bf16[1,256,256]{2,1,0:T(8,128)(2,1)S(1)} %get-tuple-element.15), channel_id=1, source_target_pairs={{0,1},{1,2},{2,3},{3,4},{4,5},{5,6},{6,7},{7,8},{8,9},{9,10},{10,1... | collective-permute-start | bytes 393224 | tf_op jit(solution)/shard_map/ppermute | solution.py:21
  94.1 3.4 %collective-permute-start.3 = (bf16[1,256,256]{2,1,0:T(8,128)(2,1)S(1)}, bf16[1,256,256]{2,1,0:T(8,128)(2,1)S(1)}, u32[]{:S(2)}, u32[]{:S(2)}) collective-permute-start(bf16[1,256,256]{2,1,0:T(8,128)(2,1)S(1)} %get-tuple-element.14), channel_id=1, source_target_pairs={{1,0},{2,1},{3,2},{4,3},{5,4},{6,5},{7,6},{8,7},{9,8},{10,9},{11,1... | collective-permute-start | bytes 393224 | tf_op jit(solution)/shard_map/ppermute | solution.py:22
  97.4 1.2 collective-permute-done.2.below_ref
  98.6 0.0 copy-start.4
  98.6 4.0 %collective-permute-done.3.above_ref = bf16[1,256,256]{2,1,0:T(8,128)(2,1)S(1)} collective-permute-done((bf16[1,256,256]{2,1,0:T(8,128)(2,1)S(1)}, bf16[1,256,256]{2,1,0:T(8,128)(2,1)S(1)}, u32[]{:S(2)}, u32[]{:S(2)}) %collective-permute-start.3) | collective-permute-done | bytes 131104 | tf_op jit(solution)/shard_map/ppermute | solution.py:22
  102.6 0.0 copy-done.1
  102.6 0.0 copy-done.4
  102.6 0.0 copy-start.5
  102.6 0.6 copy-done.5
  103.3 3.4 %shard_map.52 = (bf16[3,256,256]{2,1,0:T(8,128)(2,1)}, bf16[3,128,384]{2,1,0:T(8,128)(2,1)}) custom-call(bf16[3,3,256,256]{3,2,1,0:T(8,128)(2,1)} %bitcast.55, bf16[3,256,256]{2,1,0:T(8,128)(2,1)} %copy-done.1, bf16[1,256,256]{2,1,0:T(8,128)(2,1)} %copy-done.4, bf16[1,256,256]{2,1,0:T(8,128)(2,1)} %copy-done.5), custom_call_target="tpu_custom_call" | custom-call | flops 603979776 | bytes 2621440 | tf_op jit(solution)/shard_map/pallas_call | solution.py:81
  106.7 22.2 %all_to_all.21.l_ref = bf16[48,8,384]{2,1,0:T(8,128)(2,1)} all-to-all(bf16[48,8,384]{2,1,0:T(8,128)(2,1)} %bitcast.53), channel_id=1, replica_groups=mesh['energy'=48,'layer'=16] {'energy'}, dimensions={0} | all-to-all | bytes 589824 | tf_op jit(solution)/shard_map/all_to_all | solution.py:225
  128.8 2.5 %shard_map.53 = bf16[48,8,384]{2,1,0:T(8,128)(2,1)} custom-call(bf16[48,8,384]{2,1,0:T(8,128)(2,1)} %all_to_all.21.l_ref, bf16[48,8,384]{2,1,0:T(8,128)(2,1)} %get-tuple-element.11.s_ref), custom_call_target="tpu_custom_call" | custom-call | flops 7225344 | bytes 1179648 | tf_op jit(solution)/shard_map/pallas_call | solution.py:138
  131.4 23.9 %all_to_all.22 = bf16[48,8,384]{2,1,0:T(8,128)(2,1)S(1)} all-to-all(bf16[48,8,384]{2,1,0:T(8,128)(2,1)} %shard_map.53), channel_id=1, replica_groups=mesh['energy'=48,'layer'=16] {'energy'}, dimensions={0} | all-to-all | bytes 589824 | tf_op jit(solution)/shard_map/all_to_all | solution.py:229
  155.3 0.1 copy.15
  155.5 0.1 copy.14
  155.6 0.8 maximum_bitcast_fusion
  (7 shorter events, 0.2 us)
Async XLA Ops:
  2.1 7.4 %copy-start.2 = (bf16[1,3,256,256]{3,2,1,0:T(8,128)(2,1)S(1)}, bf16[1,3,256,256]{3,2,1,0:T(8,128)(2,1)}, u32[]{:S(2)}) copy-start(bf16[1,3,256,256]{3,2,1,0:T(8,128)(2,1)} %param.5) | copy-start | bytes 1179652
  2.3 7.5 %copy-start = (bf16[3,256,256]{2,1,0:T(8,128)(2,1)}, bf16[3,256,256]{2,1,0:T(8,128)(2,1)S(1)}, u32[]{:S(2)}) copy-start(bf16[3,256,256]{2,1,0:T(8,128)(2,1)S(1)} %fusion.3.c_ref) | copy-start | bytes 1179652
  3.1 8.7 %collective-permute-start = (bf16[1,256,256]{2,1,0:T(8,128)(2,1)}, bf16[1,256,256]{2,1,0:T(8,128)(2,1)}, u32[]{:S(2)}, u32[]{:S(2)}) collective-permute-start(bf16[1,256,256]{2,1,0:T(8,128)(2,1)} %get-tuple-element.22), channel_id=1, source_target_pairs={{0,1},{1,2},{2,3},{3,4},{4,5},{5,6},{6,7},{7,8},{8,9},{9,10},{10,1... | collective-permute-start | bytes 393224 | tf_op jit(solution)/shard_map/ppermute | solution.py:21
  7.0 8.1 %collective-permute-start.1 = (bf16[1,256,256]{2,1,0:T(8,128)(2,1)}, bf16[1,256,256]{2,1,0:T(8,128)(2,1)}, u32[]{:S(2)}, u32[]{:S(2)}) collective-permute-start(bf16[1,256,256]{2,1,0:T(8,128)(2,1)} %get-tuple-element.21), channel_id=1, source_target_pairs={{1,0},{2,1},{3,2},{4,3},{5,4},{6,5},{7,6},{8,7},{9,8},{10,9},{11,1... | collective-permute-start | bytes 393224 | tf_op jit(solution)/shard_map/ppermute | solution.py:22
  10.1 0.7 copy-start.3
  66.9 24.7 %all-to-all-start.1 = ((bf16[48,8,384]{2,1,0:T(8,128)(2,1)}), bf16[48,8,384]{2,1,0:T(8,128)(2,1)S(1)}, u32[]{:S(2)}, u32[]{:S(2)}) async-start(bf16[48,8,384]{2,1,0:T(8,128)(2,1)} %get-tuple-element.8), calls=%async_computation.1 | async-start | bytes 589824 | tf_op jit(solution)/shard_map/all_to_all | solution.py:229
  92.1 10.6 %copy-start.1 = (bf16[3,256,256]{2,1,0:T(8,128)(2,1)}, bf16[3,256,256]{2,1,0:T(8,128)(2,1)S(1)}, u32[]{:S(2)}) copy-start(bf16[3,256,256]{2,1,0:T(8,128)(2,1)S(1)} %add_convert_fusion.c_ref) | copy-start | bytes 1179652
  92.1 6.5 %collective-permute-start.2 = (bf16[1,256,256]{2,1,0:T(8,128)(2,1)S(1)}, bf16[1,256,256]{2,1,0:T(8,128)(2,1)S(1)}, u32[]{:S(2)}, u32[]{:S(2)}) collective-permute-start(bf16[1,256,256]{2,1,0:T(8,128)(2,1)S(1)} %get-tuple-element.15), channel_id=1, source_target_pairs={{0,1},{1,2},{2,3},{3,4},{4,5},{5,6},{6,7},{7,8},{8,9},{9,10},{10,1... | collective-permute-start | bytes 393224 | tf_op jit(solution)/shard_map/ppermute | solution.py:21
  94.1 8.6 %collective-permute-start.3 = (bf16[1,256,256]{2,1,0:T(8,128)(2,1)S(1)}, bf16[1,256,256]{2,1,0:T(8,128)(2,1)S(1)}, u32[]{:S(2)}, u32[]{:S(2)}) collective-permute-start(bf16[1,256,256]{2,1,0:T(8,128)(2,1)S(1)} %get-tuple-element.14), channel_id=1, source_target_pairs={{1,0},{2,1},{3,2},{4,3},{5,4},{6,5},{7,6},{8,7},{9,8},{10,9},{11,1... | collective-permute-start | bytes 393224 | tf_op jit(solution)/shard_map/ppermute | solution.py:22
  98.6 4.0 %copy-start.4 = (bf16[1,256,256]{2,1,0:T(8,128)(2,1)}, bf16[1,256,256]{2,1,0:T(8,128)(2,1)S(1)}, u32[]{:S(2)}) copy-start(bf16[1,256,256]{2,1,0:T(8,128)(2,1)S(1)} %collective-permute-done.2.below_ref) | copy-start | bytes 393220
  102.6 0.6 copy-start.5

commit v11 on v6

--- a/solution.py
+++ b/solution.py
@@ -23,23 +23,30 @@
     return below, above
 
 
-def _lesser_kernel(r_ref, c_ref, below_ref, above_ref, *rest):
+def _lesser_kernel(r_ref, s_ref, corr_ref, below_ref, above_ref, *rest):
     if len(rest) == 3:
         screen_ref, o_ref, packed_ref = rest
     else:
         screen_ref, (o_ref, packed_ref) = None, rest
-    layers = c_ref.shape[0]
-    n = c_ref.shape[-1]
+    layers = s_ref.shape[0]
+    n = s_ref.shape[-1]
     h = n // 2
     rows = lax.broadcasted_iota(jnp.int32, (h, h), 0)
     cols = lax.broadcasted_iota(jnp.int32, (h, h), 1)
+    couplings = []
+    for layer in range(layers):
+        raw = s_ref[layer].astype(jnp.float32)
+        base = 0.5 * (raw + raw.T)
+        if corr_ref is not None:
+            base = base + corr_ref[layer].astype(jnp.float32)
+        couplings.append(base.astype(jnp.bfloat16))
 
     def neighbour(index):
         if index < 0:
             return below_ref[0]
         if index >= layers:
             return above_ref[0]
-        return c_ref[index]
+        return couplings[index]
 
     for layer in range(layers):
         running = None
@@ -72,21 +79,27 @@
             )
 
 
-def lesser_blocks(retarded, coupling, below, above, screen_packed=None):
-    layers, n = coupling.shape[0], coupling.shape[-1]
+def lesser_blocks(retarded, scatter, correction, below, above, screen_packed=None):
+    layers, n = scatter.shape[0], scatter.shape[-1]
     width = 3 * n // 2 if screen_packed is None else 5 * n // 2
-    args = (retarded, coupling, below, above)
+    args = [retarded, scatter] + ([] if correction is None else [correction]) + [below, above]
     if screen_packed is not None:
-        args = args + (screen_packed,)
+        args.append(screen_packed)
+
+    def kernel(*refs):
+        if correction is None:
+            refs = refs[:2] + (None,) + refs[2:]
+        _lesser_kernel(*refs)
+
     return pl.pallas_call(
-        _lesser_kernel,
+        kernel,
         out_shape=(
-            jax.ShapeDtypeStruct(coupling.shape, jnp.bfloat16),
+            jax.ShapeDtypeStruct(scatter.shape, jnp.bfloat16),
             jax.ShapeDtypeStruct((layers, n // 2, width), jnp.bfloat16),
         ),
         cost_estimate=pl.CostEstimate(
             flops=layers * 3 * 4 * n * n * n,
-            bytes_accessed=(layers * 3 + layers + 2 + layers * 2) * n * n * 2,
+            bytes_accessed=(layers * 3 + layers * 2 + 2 + layers * 2) * n * n * 2,
             transcendentals=0,
         ),
     )(*args)
@@ -198,30 +211,34 @@
     half = orbitals // 2
     rows = layers * half // energies
     retarded = retarded[0]
-    base_part = symmetric(scatter_in[0])
     screened = symmetric(screen[0]).astype(jnp.bfloat16)
 
     def to_blocks(columns):
         return unpack_symmetric(columns.reshape(layers, half, columns.shape[-1]))
 
+    scatter = scatter_in[0]
     correction = None
     screen_columns = None
     lesser = None
     self_energy = None
     for iteration in range(ITERS):
-        if correction is None:
-            coupling = base_part.astype(jnp.bfloat16)
-        else:
-            coupling = (base_part + correction).astype(jnp.bfloat16)
-        below, above = halo(coupling, "layer")
+        edges = symmetric(jnp.concatenate([scatter[-1:], scatter[:1]], axis=0))
+        if correction is not None:
+            edges = edges + jnp.concatenate([correction[-1:], correction[:1]], axis=0).astype(
+                jnp.float32
+            )
+        edges = edges.astype(jnp.bfloat16)
+        below, above = halo(jnp.concatenate([edges[1:], edges[:1]], axis=0), "layer")
         if screen_columns is None:
-            lesser, both = lesser_blocks(retarded, coupling, below, above, pack_screened(screened))
+            lesser, both = lesser_blocks(
+                retarded, scatter, None, below, above, pack_screened(screened)
+            )
             both = lax.all_to_all(
                 both.reshape(energies, rows, both.shape[-1]), "energy", 0, 0, tiled=True
             )
             self_columns, screen_columns = energy_convolve_first(both)
         else:
-            lesser, packed = lesser_blocks(retarded, coupling, below, above)
+            lesser, packed = lesser_blocks(retarded, scatter, correction, below, above)
             lesser_columns = lax.all_to_all(
                 packed.reshape(energies, rows, packed.shape[-1]), "energy", 0, 0, tiled=True
             )
@@ -229,7 +246,7 @@
         returned = lax.all_to_all(self_columns, "energy", 0, 0, tiled=True)
         self_blocks = to_blocks(returned)
         self_energy = self_blocks[None]
-        correction = self_blocks.astype(jnp.float32)
+        correction = self_blocks
     return (lesser[None], self_energy)
 
 

time: 158 us -> 157 us (level)
  no operation moved by 1% of the time
where the time goes in v11:
time: 157 us; the launch traced here: 155 us
  blocking collectives  91.2 us (58%)
  waiting for transfers between devices  26.4 us (17%)
  starting transfers between devices  18.9 us (12%)
  Pallas kernels  11.9 us (8%)
  local copies, waits for them, and re-layouts  3.74 us (2%)
  other arithmetic  2.18 us (1%)
    all_to_all x1, blocking collectives, shards(): lax.all_to_all(both.reshape(energies, rows, both.shape[-1]), 'energy', 0,...  44.7 us
    all_to_all x1, blocking collectives, shards(): returned = lax.all_to_all(self_columns, 'energy', 0, 0, tiled=True)  23.9 us
    all_to_all x1, blocking collectives, shards(): lax.all_to_all(packed.reshape(energies, rows, packed.shape[-1]), 'energy'...  22.7 us
    all_to_all x1, waiting for transfers between devices, shards(): returned = lax.all_to_all(self_columns, 'energy', 0, 0, tiled=True)  16.8 us
    ppermute x2, waiting for transfers between devices, halo(): above = lax.ppermute(cells[:1], axis, [(i + 1, i) for i in range(ends)])  8.42 us
    all_to_all x1, starting transfers between devices, shards(): returned = lax.all_to_all(self_columns, 'energy', 0, 0, tiled=True)  7.78 us
    pallas_call x2, Pallas kernels, lesser_blocks(): pl.pallas_call(kernel, out_shape=(jax.ShapeDtypeStruct(scatter.shape, jnp...  7.2 us
    ppermute x2, starting transfers between devices, halo(): below = lax.ppermute(cells[-1:], axis, [(i, i + 1) for i in range(ends)])  5.82 us
  transfers between devices with their start and end apart: 5, of which 4 were waited for; matrix products, arithmetic and copies ran while one was open for 1% of the time, Pallas kernels for 0%

profile of v11, /device:TPU:7, one launch (start us, length us, event | category | flops | bytes accessed | tf_op | source)
XLA Modules:
  0.0 155.2 jit_solution(13035450270034415463)
XLA Ops:
  0.6 1.0 fusion.5
  1.6 0.1 copy.16
  1.7 0.1 copy.17
  1.9 0.0 copy-start.1
  1.9 0.2 copy.7
  2.1 0.1 fusion.3
  2.2 3.9 %collective-permute-start = (bf16[1,256,256]{2,1,0:T(8,128)(2,1)S(1)}, bf16[1,256,256]{2,1,0:T(8,128)(2,1)}, u32[]{:S(2)}, u32[]{:S(2)}) collective-permute-start(bf16[1,256,256]{2,1,0:T(8,128)(2,1)S(1)} %get-tuple-element.30), channel_id=1, source_target_pairs={{0,1},{1,2},{2,3},{3,4},{4,5},{5,6},{6,7},{7,8},{8,9},{9,10},{10,1... | collective-permute-start | bytes 393224 | tf_op jit(solution)/shard_map/ppermute | solution.py:21
  6.1 1.9 %collective-permute-start.1 = (bf16[1,256,256]{2,1,0:T(8,128)(2,1)S(1)}, bf16[1,256,256]{2,1,0:T(8,128)(2,1)}, u32[]{:S(2)}, u32[]{:S(2)}) collective-permute-start(bf16[1,256,256]{2,1,0:T(8,128)(2,1)S(1)} %get-tuple-element.29), channel_id=1, source_target_pairs={{1,0},{2,1},{3,2},{4,3},{5,4},{6,5},{7,6},{8,7},{9,8},{10,9},{11,1... | collective-permute-start | bytes 393224 | tf_op jit(solution)/shard_map/ppermute | solution.py:22
  8.1 0.0 copy-done.1
  8.1 0.2 copy.8
  8.3 0.1 bitcast_convert_fusion
  8.3 0.3 copy.9
  8.6 0.1 fusion.1
  8.7 0.1 fusion.8
  8.8 0.8 pad_maximum_fusion.refs_4_
  9.7 0.0 collective-permute-done.refs_2_
  9.7 4.4 %collective-permute-done.1.refs_3_ = bf16[1,256,256]{2,1,0:T(8,128)(2,1)} collective-permute-done((bf16[1,256,256]{2,1,0:T(8,128)(2,1)S(1)}, bf16[1,256,256]{2,1,0:T(8,128)(2,1)}, u32[]{:S(2)}, u32[]{:S(2)}) %collective-permute-start.1) | collective-permute-done | bytes 131104 | tf_op jit(solution)/shard_map/ppermute | solution.py:22
  14.1 3.6 %shard_map.50 = (bf16[3,256,256]{2,1,0:T(8,128)(2,1)}, bf16[3,128,640]{2,1,0:T(8,128)(2,1)}) custom-call(bf16[3,3,256,256]{3,2,1,0:T(8,128)(2,1)} %bitcast.58, bf16[3,256,256]{2,1,0:T(8,128)(2,1)} %bitcast.56, bf16[1,256,256]{2,1,0:T(8,128)(2,1)} %collective-permute-done.refs_2_, bf16[1,256,256]{2,1,0:T(8,128)(2,1)} %collective-permute-done.1.refs_3_, ...), custom_call_target="tpu_custom_call" | custom-call | flops 603979776 | bytes 3014656 | tf_op jit(solution)/shard_map/pallas_call | solution.py:94
  17.7 44.7 %all_to_all.20.x_ref = bf16[48,8,640]{2,1,0:T(8,128)(2,1)} all-to-all(bf16[48,8,640]{2,1,0:T(8,128)(2,1)} %bitcast.54), channel_id=1, replica_groups=mesh['energy'=48,'layer'=16] {'energy'}, dimensions={0} | all-to-all | bytes 983040 | tf_op jit(solution)/shard_map/all_to_all | solution.py:236
  62.4 2.4 %shard_map.51 = (bf16[48,8,384]{2,1,0:T(8,128)(2,1)}, bf16[48,8,384]{2,1,0:T(8,128)(2,1)}) custom-call(bf16[48,8,640]{2,1,0:T(8,128)(2,1)} %all_to_all.20.x_ref), custom_call_target="tpu_custom_call" | custom-call | flops 7225344 | bytes 1179648 | tf_op jit(solution)/shard_map/pallas_call | solution.py:151
  64.7 7.8 %all-to-all-start.1 = ((bf16[48,8,384]{2,1,0:T(8,128)(2,1)}), bf16[48,8,384]{2,1,0:T(8,128)(2,1)S(1)}, u32[]{:S(2)}, u32[]{:S(2)}) async-start(bf16[48,8,384]{2,1,0:T(8,128)(2,1)} %get-tuple-element.8), calls=%async_computation.1 | async-start | bytes 589824 | tf_op jit(solution)/shard_map/all_to_all | solution.py:246
  72.5 16.8 %all-to-all-done.1 = bf16[48,8,384]{2,1,0:T(8,128)(2,1)S(1)} async-done(((bf16[48,8,384]{2,1,0:T(8,128)(2,1)}), bf16[48,8,384]{2,1,0:T(8,128)(2,1)S(1)}, u32[]{:S(2)}, u32[]{:S(2)}) %all-to-all-start.1) | async-done | bytes 294944 | tf_op jit(solution)/shard_map/all_to_all | solution.py:246
  89.4 0.1 copy.10
  89.5 0.1 copy.11
  89.7 0.1 maximum_maximum_fusion.refs_2_
  89.7 0.0 copy-start
  89.8 0.1 add_convert_fusion
  89.9 0.6 copy-done
  90.5 1.9 %collective-permute-start.2 = (bf16[1,256,256]{2,1,0:T(8,128)(2,1)S(1)}, bf16[1,256,256]{2,1,0:T(8,128)(2,1)S(1)}, u32[]{:S(2)}, u32[]{:S(2)}) collective-permute-start(bf16[1,256,256]{2,1,0:T(8,128)(2,1)S(1)} %get-tuple-element.28), channel_id=1, source_target_pairs={{0,1},{1,2},{2,3},{3,4},{4,5},{5,6},{6,7},{7,8},{8,9},{9,10},{10,1... | collective-permute-start | bytes 393224 | tf_op jit(solution)/shard_map/ppermute | solution.py:21
  92.4 3.4 %collective-permute-start.3 = (bf16[1,256,256]{2,1,0:T(8,128)(2,1)S(1)}, bf16[1,256,256]{2,1,0:T(8,128)(2,1)S(1)}, u32[]{:S(2)}, u32[]{:S(2)}) collective-permute-start(bf16[1,256,256]{2,1,0:T(8,128)(2,1)S(1)} %get-tuple-element.27), channel_id=1, source_target_pairs={{1,0},{2,1},{3,2},{4,3},{5,4},{6,5},{7,6},{8,7},{9,8},{10,9},{11,1... | collective-permute-start | bytes 393224 | tf_op jit(solution)/shard_map/ppermute | solution.py:22
  95.8 1.2 collective-permute-done.2.refs_3_
  97.0 0.0 copy-start.2
  97.0 4.0 %collective-permute-done.3.refs_4_ = bf16[1,256,256]{2,1,0:T(8,128)(2,1)S(1)} collective-permute-done((bf16[1,256,256]{2,1,0:T(8,128)(2,1)S(1)}, bf16[1,256,256]{2,1,0:T(8,128)(2,1)S(1)}, u32[]{:S(2)}, u32[]{:S(2)}) %collective-permute-start.3) | collective-permute-done | bytes 131104 | tf_op jit(solution)/shard_map/ppermute | solution.py:22
  101.0 0.0 copy-done.2
  101.0 0.0 copy-start.3
  101.0 0.6 copy-done.3
  101.7 3.6 %shard_map.52 = (bf16[3,256,256]{2,1,0:T(8,128)(2,1)}, bf16[3,128,384]{2,1,0:T(8,128)(2,1)}) custom-call(bf16[3,3,256,256]{3,2,1,0:T(8,128)(2,1)} %bitcast.59, bf16[3,256,256]{2,1,0:T(8,128)(2,1)} %bitcast.57, bf16[3,256,256]{2,1,0:T(8,128)(2,1)} %copy-done, bf16[1,256,256]{2,1,0:T(8,128)(2,1)} %copy-done.2, bf16[1,256,256]{2,1,0:T(8,128)(2,1)} %copy-done.3), custom_call_target="tpu_custom_call" | custom-call | flops 603979776 | bytes 3014656 | tf_op jit(solution)/shard_map/pallas_call | solution.py:94
  105.3 22.7 %all_to_all.21.l_ref = bf16[48,8,384]{2,1,0:T(8,128)(2,1)} all-to-all(bf16[48,8,384]{2,1,0:T(8,128)(2,1)} %bitcast.55), channel_id=1, replica_groups=mesh['energy'=48,'layer'=16] {'energy'}, dimensions={0} | all-to-all | bytes 589824 | tf_op jit(solution)/shard_map/all_to_all | solution.py:242
  127.9 2.3 %shard_map.53 = bf16[48,8,384]{2,1,0:T(8,128)(2,1)} custom-call(bf16[48,8,384]{2,1,0:T(8,128)(2,1)} %all_to_all.21.l_ref, bf16[48,8,384]{2,1,0:T(8,128)(2,1)} %get-tuple-element.11.s_ref), custom_call_target="tpu_custom_call" | custom-call | flops 7225344 | bytes 1179648 | tf_op jit(solution)/shard_map/pallas_call | solution.py:151
  130.2 23.9 %all_to_all.22 = bf16[48,8,384]{2,1,0:T(8,128)(2,1)S(1)} all-to-all(bf16[48,8,384]{2,1,0:T(8,128)(2,1)} %shard_map.53), channel_id=1, replica_groups=mesh['energy'=48,'layer'=16] {'energy'}, dimensions={0} | all-to-all | bytes 589824 | tf_op jit(solution)/shard_map/all_to_all | solution.py:246
  154.1 0.1 copy.18
  154.3 0.1 copy.15
  154.4 0.8 maximum_bitcast_fusion
  (11 shorter events, 0.3 us)
Async XLA Ops:
  1.9 6.2 %copy-start.1 = (bf16[1,3,256,256]{3,2,1,0:T(8,128)(2,1)S(1)}, bf16[1,3,256,256]{3,2,1,0:T(8,128)(2,1)}, u32[]{:S(2)}) copy-start(bf16[1,3,256,256]{3,2,1,0:T(8,128)(2,1)} %param.5) | copy-start | bytes 1179652
  2.2 7.5 %collective-permute-start = (bf16[1,256,256]{2,1,0:T(8,128)(2,1)S(1)}, bf16[1,256,256]{2,1,0:T(8,128)(2,1)}, u32[]{:S(2)}, u32[]{:S(2)}) collective-permute-start(bf16[1,256,256]{2,1,0:T(8,128)(2,1)S(1)} %get-tuple-element.30), channel_id=1, source_target_pairs={{0,1},{1,2},{2,3},{3,4},{4,5},{5,6},{6,7},{7,8},{8,9},{9,10},{10,1... | collective-permute-start | bytes 393224 | tf_op jit(solution)/shard_map/ppermute | solution.py:21
  6.1 7.9 %collective-permute-start.1 = (bf16[1,256,256]{2,1,0:T(8,128)(2,1)S(1)}, bf16[1,256,256]{2,1,0:T(8,128)(2,1)}, u32[]{:S(2)}, u32[]{:S(2)}) collective-permute-start(bf16[1,256,256]{2,1,0:T(8,128)(2,1)S(1)} %get-tuple-element.29), channel_id=1, source_target_pairs={{1,0},{2,1},{3,2},{4,3},{5,4},{6,5},{7,6},{8,7},{9,8},{10,9},{11,1... | collective-permute-start | bytes 393224 | tf_op jit(solution)/shard_map/ppermute | solution.py:22
  64.7 24.6 %all-to-all-start.1 = ((bf16[48,8,384]{2,1,0:T(8,128)(2,1)}), bf16[48,8,384]{2,1,0:T(8,128)(2,1)S(1)}, u32[]{:S(2)}, u32[]{:S(2)}) async-start(bf16[48,8,384]{2,1,0:T(8,128)(2,1)} %get-tuple-element.8), calls=%async_computation.1 | async-start | bytes 589824 | tf_op jit(solution)/shard_map/all_to_all | solution.py:246
  89.7 0.7 copy-start
  90.5 6.5 %collective-permute-start.2 = (bf16[1,256,256]{2,1,0:T(8,128)(2,1)S(1)}, bf16[1,256,256]{2,1,0:T(8,128)(2,1)S(1)}, u32[]{:S(2)}, u32[]{:S(2)}) collective-permute-start(bf16[1,256,256]{2,1,0:T(8,128)(2,1)S(1)} %get-tuple-element.28), channel_id=1, source_target_pairs={{0,1},{1,2},{2,3},{3,4},{4,5},{5,6},{6,7},{7,8},{8,9},{9,10},{10,1... | collective-permute-start | bytes 393224 | tf_op jit(solution)/shard_map/ppermute | solution.py:21
  92.4 8.6 %collective-permute-start.3 = (bf16[1,256,256]{2,1,0:T(8,128)(2,1)S(1)}, bf16[1,256,256]{2,1,0:T(8,128)(2,1)S(1)}, u32[]{:S(2)}, u32[]{:S(2)}) collective-permute-start(bf16[1,256,256]{2,1,0:T(8,128)(2,1)S(1)} %get-tuple-element.27), channel_id=1, source_target_pairs={{1,0},{2,1},{3,2},{4,3},{5,4},{6,5},{7,6},{8,7},{9,8},{10,9},{11,1... | collective-permute-start | bytes 393224 | tf_op jit(solution)/shard_map/ppermute | solution.py:22
  97.0 4.0 %copy-start.2 = (bf16[1,256,256]{2,1,0:T(8,128)(2,1)}, bf16[1,256,256]{2,1,0:T(8,128)(2,1)S(1)}, u32[]{:S(2)}) copy-start(bf16[1,256,256]{2,1,0:T(8,128)(2,1)S(1)} %collective-permute-done.2.refs_3_) | copy-start | bytes 393220
  101.0 0.6 copy-start.3

commit v12 on v11

--- a/solution.py
+++ b/solution.py
@@ -38,7 +38,22 @@
         raw = s_ref[layer].astype(jnp.float32)
         base = 0.5 * (raw + raw.T)
         if corr_ref is not None:
-            base = base + corr_ref[layer].astype(jnp.float32)
+            packed = corr_ref[layer]
+            folded = packed[:, :h]
+            off = packed[:, h : 2 * h]
+            flipped = folded.T
+            top_left = jnp.where(rows <= cols, folded, flipped)
+            bottom_right = jnp.where(
+                rows == cols, packed[:, 2 * h :], jnp.where(rows > cols, folded, flipped)
+            )
+            full = jnp.concatenate(
+                [
+                    jnp.concatenate([top_left, off], axis=1),
+                    jnp.concatenate([off.T, bottom_right], axis=1),
+                ],
+                axis=0,
+            )
+            base = base + full.astype(jnp.float32)
         couplings.append(base.astype(jnp.bfloat16))
 
     def neighbour(index):
@@ -224,9 +239,8 @@
     for iteration in range(ITERS):
         edges = symmetric(jnp.concatenate([scatter[-1:], scatter[:1]], axis=0))
         if correction is not None:
-            edges = edges + jnp.concatenate([correction[-1:], correction[:1]], axis=0).astype(
-                jnp.float32
-            )
+            edge_packed = jnp.concatenate([correction[-1:], correction[:1]], axis=0)
+            edges = edges + unpack_symmetric(edge_packed).astype(jnp.float32)
         edges = edges.astype(jnp.bfloat16)
         below, above = halo(jnp.concatenate([edges[1:], edges[:1]], axis=0), "layer")
         if screen_columns is None:
@@ -244,9 +258,8 @@
             )
             self_columns = energy_convolve(lesser_columns, screen_columns)
         returned = lax.all_to_all(self_columns, "energy", 0, 0, tiled=True)
-        self_blocks = to_blocks(returned)
-        self_energy = self_blocks[None]
-        correction = self_blocks
+        correction = returned.reshape(layers, half, returned.shape[-1])
+    self_energy = to_blocks(returned)[None]
     return (lesser[None], self_energy)
 
 

time: 157 us -> 157 us (level)
  no operation moved by 1% of the time
where the time goes in v12:
time: 157 us; the launch traced here: 155 us
  blocking collectives  91.2 us (58%)
  waiting for transfers between devices  26.4 us (17%)
  starting transfers between devices  18.9 us (12%)
  Pallas kernels  11.8 us (8%)
  local copies, waits for them, and re-layouts  3.38 us (2%)
  other arithmetic  2.16 us (1%)
    all_to_all x1, blocking collectives, shards(): lax.all_to_all(both.reshape(energies, rows, both.shape[-1]), 'energy', 0,...  44.7 us
    all_to_all x1, blocking collectives, shards(): returned = lax.all_to_all(self_columns, 'energy', 0, 0, tiled=True)  23.9 us
    all_to_all x1, blocking collectives, shards(): lax.all_to_all(packed.reshape(energies, rows, packed.shape[-1]), 'energy'...  22.7 us
    all_to_all x1, waiting for transfers between devices, shards(): returned = lax.all_to_all(self_columns, 'energy', 0, 0, tiled=True)  16.8 us
    ppermute x2, waiting for transfers between devices, halo(): above = lax.ppermute(cells[:1], axis, [(i + 1, i) for i in range(ends)])  8.42 us
    all_to_all x1, starting transfers between devices, shards(): returned = lax.all_to_all(self_columns, 'energy', 0, 0, tiled=True)  7.78 us
    pallas_call x2, Pallas kernels, lesser_blocks(): pl.pallas_call(kernel, out_shape=(jax.ShapeDtypeStruct(scatter.shape, jnp...  7.18 us
    ppermute x2, starting transfers between devices, halo(): below = lax.ppermute(cells[-1:], axis, [(i, i + 1) for i in range(ends)])  5.84 us
  transfers between devices with their start and end apart: 5, of which 4 were waited for; matrix products, arithmetic and copies ran while one was open for 1% of the time, Pallas kernels for 0%

profile of v12, /device:TPU:7, one launch (start us, length us, event | category | flops | bytes accessed | tf_op | source)
XLA Modules:
  0.0 154.8 jit_solution(11384762569030045329)
XLA Ops:
  0.6 1.0 fusion.7
  1.6 0.1 copy.16
  1.7 0.1 copy.17
  1.9 0.0 copy-start.1
  1.9 0.2 copy.7
  2.1 0.1 fusion.3
  2.2 3.9 %collective-permute-start = (bf16[1,256,256]{2,1,0:T(8,128)(2,1)S(1)}, bf16[1,256,256]{2,1,0:T(8,128)(2,1)}, u32[]{:S(2)}, u32[]{:S(2)}) collective-permute-start(bf16[1,256,256]{2,1,0:T(8,128)(2,1)S(1)} %get-tuple-element.26), channel_id=1, source_target_pairs={{0,1},{1,2},{2,3},{3,4},{4,5},{5,6},{6,7},{7,8},{8,9},{9,10},{10,1... | collective-permute-start | bytes 393224 | tf_op jit(solution)/shard_map/ppermute | solution.py:21
  6.1 1.9 %collective-permute-start.1 = (bf16[1,256,256]{2,1,0:T(8,128)(2,1)S(1)}, bf16[1,256,256]{2,1,0:T(8,128)(2,1)}, u32[]{:S(2)}, u32[]{:S(2)}) collective-permute-start(bf16[1,256,256]{2,1,0:T(8,128)(2,1)S(1)} %get-tuple-element.25), channel_id=1, source_target_pairs={{1,0},{2,1},{3,2},{4,3},{5,4},{6,5},{7,6},{8,7},{9,8},{10,9},{11,1... | collective-permute-start | bytes 393224 | tf_op jit(solution)/shard_map/ppermute | solution.py:22
  8.1 0.0 copy-done.1
  8.1 0.2 copy.8
  8.3 0.1 bitcast_convert_fusion
  8.3 0.3 copy.9
  8.6 0.1 fusion.1
  8.7 0.1 fusion.10
  8.8 0.8 pad_maximum_fusion.refs_4_
  9.7 0.0 collective-permute-done.refs_2_
  9.7 4.4 %collective-permute-done.1.refs_3_ = bf16[1,256,256]{2,1,0:T(8,128)(2,1)} collective-permute-done((bf16[1,256,256]{2,1,0:T(8,128)(2,1)S(1)}, bf16[1,256,256]{2,1,0:T(8,128)(2,1)}, u32[]{:S(2)}, u32[]{:S(2)}) %collective-permute-start.1) | collective-permute-done | bytes 131104 | tf_op jit(solution)/shard_map/ppermute | solution.py:22
  14.1 3.6 %shard_map.50 = (bf16[3,256,256]{2,1,0:T(8,128)(2,1)}, bf16[3,128,640]{2,1,0:T(8,128)(2,1)}) custom-call(bf16[3,3,256,256]{3,2,1,0:T(8,128)(2,1)} %bitcast.61, bf16[3,256,256]{2,1,0:T(8,128)(2,1)} %bitcast.59, bf16[1,256,256]{2,1,0:T(8,128)(2,1)} %collective-permute-done.refs_2_, bf16[1,256,256]{2,1,0:T(8,128)(2,1)} %collective-permute-done.1.refs_3_, ...), custom_call_target="tpu_custom_call" | custom-call | flops 603979776 | bytes 3014656 | tf_op jit(solution)/shard_map/pallas_call | solution.py:109
  17.7 44.7 %all_to_all.20.x_ref = bf16[48,8,640]{2,1,0:T(8,128)(2,1)} all-to-all(bf16[48,8,640]{2,1,0:T(8,128)(2,1)} %bitcast.57), channel_id=1, replica_groups=mesh['energy'=48,'layer'=16] {'energy'}, dimensions={0} | all-to-all | bytes 983040 | tf_op jit(solution)/shard_map/all_to_all | solution.py:250
  62.4 2.4 %shard_map.51 = (bf16[48,8,384]{2,1,0:T(8,128)(2,1)}, bf16[48,8,384]{2,1,0:T(8,128)(2,1)}) custom-call(bf16[48,8,640]{2,1,0:T(8,128)(2,1)} %all_to_all.20.x_ref), custom_call_target="tpu_custom_call" | custom-call | flops 7225344 | bytes 1179648 | tf_op jit(solution)/shard_map/pallas_call | solution.py:166
  64.7 7.8 %all-to-all-start.1 = ((bf16[48,8,384]{2,1,0:T(8,128)(2,1)}), bf16[48,8,384]{2,1,0:T(8,128)(2,1)S(1)}, u32[]{:S(2)}, u32[]{:S(2)}) async-start(bf16[48,8,384]{2,1,0:T(8,128)(2,1)} %get-tuple-element.8), calls=%async_computation.1 | async-start | bytes 589824 | tf_op jit(solution)/shard_map/all_to_all | solution.py:260
  72.5 16.8 %all-to-all-done.1 = bf16[48,8,384]{2,1,0:T(8,128)(2,1)S(1)} async-done(((bf16[48,8,384]{2,1,0:T(8,128)(2,1)}), bf16[48,8,384]{2,1,0:T(8,128)(2,1)S(1)}, u32[]{:S(2)}, u32[]{:S(2)}) %all-to-all-start.1) | async-done | bytes 294944 | tf_op jit(solution)/shard_map/all_to_all | solution.py:260
  89.3 0.0 copy-start
  89.4 0.1 copy.10
  89.5 0.1 copy.11
  89.7 0.1 bitcast_select_fusion.3
  89.7 0.1 add_convert_fusion
  89.8 0.2 copy-done
  90.1 1.9 %collective-permute-start.2 = (bf16[1,256,256]{2,1,0:T(8,128)(2,1)S(1)}, bf16[1,256,256]{2,1,0:T(8,128)(2,1)S(1)}, u32[]{:S(2)}, u32[]{:S(2)}) collective-permute-start(bf16[1,256,256]{2,1,0:T(8,128)(2,1)S(1)} %get-tuple-element.24), channel_id=1, source_target_pairs={{0,1},{1,2},{2,3},{3,4},{4,5},{5,6},{6,7},{7,8},{8,9},{9,10},{10,1... | collective-permute-start | bytes 393224 | tf_op jit(solution)/shard_map/ppermute | solution.py:21
  92.0 3.4 %collective-permute-start.3 = (bf16[1,256,256]{2,1,0:T(8,128)(2,1)S(1)}, bf16[1,256,256]{2,1,0:T(8,128)(2,1)S(1)}, u32[]{:S(2)}, u32[]{:S(2)}) collective-permute-start(bf16[1,256,256]{2,1,0:T(8,128)(2,1)S(1)} %get-tuple-element.23), channel_id=1, source_target_pairs={{1,0},{2,1},{3,2},{4,3},{5,4},{6,5},{7,6},{8,7},{9,8},{10,9},{11,1... | collective-permute-start | bytes 393224 | tf_op jit(solution)/shard_map/ppermute | solution.py:22
  95.4 1.2 collective-permute-done.2.refs_3_
  96.6 0.0 copy-start.2
  96.6 4.0 %collective-permute-done.3.refs_4_ = bf16[1,256,256]{2,1,0:T(8,128)(2,1)S(1)} collective-permute-done((bf16[1,256,256]{2,1,0:T(8,128)(2,1)S(1)}, bf16[1,256,256]{2,1,0:T(8,128)(2,1)S(1)}, u32[]{:S(2)}, u32[]{:S(2)}) %collective-permute-start.3) | collective-permute-done | bytes 131104 | tf_op jit(solution)/shard_map/ppermute | solution.py:22
  100.6 0.0 copy-start.3
  100.6 0.0 copy-done.2
  100.6 0.6 copy-done.3
  101.3 3.6 %shard_map.52 = (bf16[3,256,256]{2,1,0:T(8,128)(2,1)}, bf16[3,128,384]{2,1,0:T(8,128)(2,1)}) custom-call(bf16[3,3,256,256]{3,2,1,0:T(8,128)(2,1)} %bitcast.62, bf16[3,256,256]{2,1,0:T(8,128)(2,1)} %bitcast.60, bf16[3,128,384]{2,1,0:T(8,128)(2,1)} %bitcast.55, bf16[1,256,256]{2,1,0:T(8,128)(2,1)} %copy-done.2, bf16[1,256,256]{2,1,0:T(8,128)(2,1)} %copy-done.3), custom_call_target="tpu_custom_call" | custom-call | flops 603979776 | bytes 3014656 | tf_op jit(solution)/shard_map/pallas_call | solution.py:109
  104.9 22.7 %all_to_all.21.l_ref = bf16[48,8,384]{2,1,0:T(8,128)(2,1)} all-to-all(bf16[48,8,384]{2,1,0:T(8,128)(2,1)} %bitcast.58), channel_id=1, replica_groups=mesh['energy'=48,'layer'=16] {'energy'}, dimensions={0} | all-to-all | bytes 589824 | tf_op jit(solution)/shard_map/all_to_all | solution.py:256
  127.5 2.3 %shard_map.53 = bf16[48,8,384]{2,1,0:T(8,128)(2,1)} custom-call(bf16[48,8,384]{2,1,0:T(8,128)(2,1)} %all_to_all.21.l_ref, bf16[48,8,384]{2,1,0:T(8,128)(2,1)} %get-tuple-element.11.s_ref), custom_call_target="tpu_custom_call" | custom-call | flops 7225344 | bytes 1179648 | tf_op jit(solution)/shard_map/pallas_call | solution.py:166
  129.8 23.9 %all_to_all.22 = bf16[48,8,384]{2,1,0:T(8,128)(2,1)S(1)} all-to-all(bf16[48,8,384]{2,1,0:T(8,128)(2,1)} %shard_map.53), channel_id=1, replica_groups=mesh['energy'=48,'layer'=16] {'energy'}, dimensions={0} | all-to-all | bytes 589824 | tf_op jit(solution)/shard_map/all_to_all | solution.py:260
  153.7 0.1 copy.18
  153.9 0.1 copy.15
  154.0 0.8 maximum_bitcast_fusion
  (10 shorter events, 0.2 us)
Async XLA Ops:
  1.9 6.2 %copy-start.1 = (bf16[1,3,256,256]{3,2,1,0:T(8,128)(2,1)S(1)}, bf16[1,3,256,256]{3,2,1,0:T(8,128)(2,1)}, u32[]{:S(2)}) copy-start(bf16[1,3,256,256]{3,2,1,0:T(8,128)(2,1)} %param.5) | copy-start | bytes 1179652
  2.2 7.5 %collective-permute-start = (bf16[1,256,256]{2,1,0:T(8,128)(2,1)S(1)}, bf16[1,256,256]{2,1,0:T(8,128)(2,1)}, u32[]{:S(2)}, u32[]{:S(2)}) collective-permute-start(bf16[1,256,256]{2,1,0:T(8,128)(2,1)S(1)} %get-tuple-element.26), channel_id=1, source_target_pairs={{0,1},{1,2},{2,3},{3,4},{4,5},{5,6},{6,7},{7,8},{8,9},{9,10},{10,1... | collective-permute-start | bytes 393224 | tf_op jit(solution)/shard_map/ppermute | solution.py:21
  6.1 7.9 %collective-permute-start.1 = (bf16[1,256,256]{2,1,0:T(8,128)(2,1)S(1)}, bf16[1,256,256]{2,1,0:T(8,128)(2,1)}, u32[]{:S(2)}, u32[]{:S(2)}) collective-permute-start(bf16[1,256,256]{2,1,0:T(8,128)(2,1)S(1)} %get-tuple-element.25), channel_id=1, source_target_pairs={{1,0},{2,1},{3,2},{4,3},{5,4},{6,5},{7,6},{8,7},{9,8},{10,9},{11,1... | collective-permute-start | bytes 393224 | tf_op jit(solution)/shard_map/ppermute | solution.py:22
  64.7 24.6 %all-to-all-start.1 = ((bf16[48,8,384]{2,1,0:T(8,128)(2,1)}), bf16[48,8,384]{2,1,0:T(8,128)(2,1)S(1)}, u32[]{:S(2)}, u32[]{:S(2)}) async-start(bf16[48,8,384]{2,1,0:T(8,128)(2,1)} %get-tuple-element.8), calls=%async_computation.1 | async-start | bytes 589824 | tf_op jit(solution)/shard_map/all_to_all | solution.py:260
  89.3 0.7 copy-start
  90.1 6.5 %collective-permute-start.2 = (bf16[1,256,256]{2,1,0:T(8,128)(2,1)S(1)}, bf16[1,256,256]{2,1,0:T(8,128)(2,1)S(1)}, u32[]{:S(2)}, u32[]{:S(2)}) collective-permute-start(bf16[1,256,256]{2,1,0:T(8,128)(2,1)S(1)} %get-tuple-element.24), channel_id=1, source_target_pairs={{0,1},{1,2},{2,3},{3,4},{4,5},{5,6},{6,7},{7,8},{8,9},{9,10},{10,1... | collective-permute-start | bytes 393224 | tf_op jit(solution)/shard_map/ppermute | solution.py:21
  92.0 8.6 %collective-permute-start.3 = (bf16[1,256,256]{2,1,0:T(8,128)(2,1)S(1)}, bf16[1,256,256]{2,1,0:T(8,128)(2,1)S(1)}, u32[]{:S(2)}, u32[]{:S(2)}) collective-permute-start(bf16[1,256,256]{2,1,0:T(8,128)(2,1)S(1)} %get-tuple-element.23), channel_id=1, source_target_pairs={{1,0},{2,1},{3,2},{4,3},{5,4},{6,5},{7,6},{8,7},{9,8},{10,9},{11,1... | collective-permute-start | bytes 393224 | tf_op jit(solution)/shard_map/ppermute | solution.py:22
  96.6 4.0 %copy-start.2 = (bf16[1,256,256]{2,1,0:T(8,128)(2,1)}, bf16[1,256,256]{2,1,0:T(8,128)(2,1)S(1)}, u32[]{:S(2)}) copy-start(bf16[1,256,256]{2,1,0:T(8,128)(2,1)S(1)} %collective-permute-done.2.refs_3_) | copy-start | bytes 393220
  100.6 0.7 copy-start.3
